TPU v7x, 512 devices: a whole 4x8x8 slice. The times are simulated.
512 devices in a mesh: bits: 32 (over y_hi, z, core), cuts: 16 (over x, y_lo).
Axes of the slice: x: 4, y: 8 (y_hi: 2, y_lo: 4; y = y_hi * 4 + y_lo), z: 8, core: 2. Of those that a mesh axis runs over, the one named last changes fastest.
Arguments:
- boundary: float32 [16, 65536, 128], P('cuts', 'bits'), may hold values from -6 to 6
- gate_stack: float32 [34, 128, 128], replicated, may hold values from -0.5 to 0.5
- coupling: float32 [13, 128, 128], replicated, may hold values from 0.4 to 1.6
Outputs:
- probs: float32 [65536, 128], P('bits', 'cuts')
All inputs are finite; a program needn't handle non-finite values.
Results may differ from a plain program's by a relative error of at most 0.00018.
Values sent between devices are 32-bit elements; how exact they have to be, the bound alone decides.
No kernel may reach another device: no remote copies, remote signals or barrier semaphores. Data moves between devices by JAX's collectives and lax.ppermute only.
A program may use at most 64 MiB of HBM per device.

v0:
```python
import jax
import jax.numpy as jnp
from jax import lax
from jax.sharding import PartitionSpec as P

CYC_A = 4
CYC_B = 4
CYC_C = 5


HIGHEST_PREC = lax.Precision.HIGHEST


def partner(value, axis, distance):
    mask = 2**distance
    pairs = [(source, source ^ mask) for source in range(lax.axis_size(axis))]
    return lax.ppermute(value, axis, pairs)


def effective(weight_mat):
    order_size = weight_mat.shape[0]
    return 0.9 * jnp.eye(order_size, dtype=weight_mat.dtype) + 0.45 * weight_mat


def apply_lane(tensor, weight_mat):
    return jnp.dot(tensor, effective(weight_mat), precision=HIGHEST_PREC)


def apply_mid(tensor, weight_mat):
    order_size = weight_mat.shape[0]
    shaped = tensor.reshape(-1, order_size, tensor.shape[1])
    mixed = jnp.einsum("aic,ij->ajc", shaped, effective(weight_mat), precision=HIGHEST_PREC)
    return mixed.reshape(tensor.shape)


def apply_top(tensor, weight_mat):
    order_size = weight_mat.shape[0]
    shaped = tensor.reshape(order_size, -1)
    mixed = jnp.dot(effective(weight_mat).T, shaped, precision=HIGHEST_PREC)
    return mixed.reshape(tensor.shape)


def apply_couple(tensor, table):
    shaped = tensor.reshape(-1, table.shape[0], tensor.shape[1])
    return (shaped * table[None]).reshape(tensor.shape)


def layer_group(tensor, gate_stack, coupling, gate_base, cpl_base, cycles):
    for turn_index in range(cycles):
        first = gate_base + 3 * turn_index
        tensor = apply_top(tensor, gate_stack[first])
        tensor = apply_lane(tensor, gate_stack[first + 1])
        tensor = apply_couple(tensor, coupling[cpl_base + turn_index])
        tensor = apply_mid(tensor, gate_stack[first + 2])
    return tensor


def final_group_cols(cols, gate_stack, coupling, col_start):
    order_size = gate_stack.shape[1]
    width = cols.shape[0]
    gate_base = 3 * CYC_A + 3 * CYC_B
    cpl_base = CYC_A + CYC_B
    for turn_index in range(CYC_C):
        top_mat = effective(gate_stack[gate_base + 2 * turn_index])
        shaped = cols.reshape(width, order_size, -1)
        cols = jnp.einsum("cit,ij->cjt", shaped, top_mat, precision=HIGHEST_PREC).reshape(cols.shape)
        table = lax.dynamic_slice_in_dim(coupling[cpl_base + turn_index], col_start, width, axis=1)
        shaped = cols.reshape(width, -1, order_size)
        cols = (shaped * table.T[:, None, :]).reshape(cols.shape)
        mid_mat = effective(gate_stack[gate_base + 2 * turn_index + 1])
        cols = jnp.dot(cols.reshape(-1, order_size), mid_mat, precision=HIGHEST_PREC).reshape(cols.shape)
    return cols


def swap_bit(tensor, bit_pos):
    half_rows = tensor.shape[0] // 2
    lower = tensor[:half_rows]
    upper = tensor[half_rows:]
    parity = lax.axis_index("bits") >> bit_pos & 1
    outgoing = jnp.where(parity == 0, upper, lower)
    incoming = partner(outgoing, "bits", bit_pos)
    return jnp.where(
        parity == 0, jnp.concatenate([lower, incoming], 0), jnp.concatenate([incoming, upper], 0)
    )


def reduce_columns(tensor):
    n_cuts = lax.axis_size("cuts")
    blocks = tensor.T.reshape(n_cuts, tensor.shape[1] // n_cuts, tensor.shape[0])
    gathered = lax.all_to_all(blocks, "cuts", 0, 0, tiled=False)
    return gathered.sum(0)


def on_device(boundary, gate_stack, coupling):
    tensor = boundary[0]
    top_bit = lax.axis_size("bits").bit_length() - 2
    tensor = layer_group(tensor, gate_stack, coupling, 0, 0, CYC_A)
    tensor = swap_bit(tensor, top_bit)
    tensor = layer_group(tensor, gate_stack, coupling, 3 * CYC_A, CYC_A, CYC_B)
    cols = reduce_columns(tensor)
    cols = swap_bit(cols.T, 0).T
    col_start = lax.axis_index("cuts") * cols.shape[0]
    cols = final_group_cols(cols, gate_stack, coupling, col_start)
    return cols.T


def solution(mesh):
    in_specs = (P("cuts", "bits", None), P(), P())
    out_specs = P("bits", "cuts")
    return jax.shard_map(
        on_device, mesh=mesh, in_specs=in_specs, out_specs=out_specs, check_vma=False
    )
```

profile of v0, /device:TPU:1, one launch (start us, length us, event | category | flops | bytes accessed | tf_op | source)
XLA Modules:
  0.0 138.2 jit_solution(18145136743174061003)
XLA Ops:
  0.0 2.0 %fusion.369 = (f32[1,128,128]{2,1,0:T(8,128)}, f32[1,128,128]{2,1,0:T(8,128)}, f32[1,128,128]{2,1,0:T(8,128)}, f32[1,128,128]{2,1,0:T(8,128)}, f32[1,128,128]{2,...) fusion(f32[13,128,128]{2,1,0:T(8,128)} %param.5), kind=kLoop, calls=%fused_computation.403 | loop fusion | bytes 1703936 | tf_op jit(solution)/shard_map/slice | solution.py:67
  2.2 1.9 %fusion.54 = f32[128,2048]{1,0:T(8,128)S(1)} fusion(f32[128,2048]{1,0:T(8,128)S(1)} %reshape_squeeze.3, f32[34,128,128]{2,1,0:T(8,128)} %param.4), kind=kOutput, calls=%fused_computation.85 | convolution fusion | flops 402718720 | bytes 2162688 | tf_op jit(solution)/shard_map/dot_general | solution.py:39
  4.3 1.8 %convolution_multiply_fusion.7 = f32[16,128,128]{2,1,0:T(8,128)S(1)} fusion(f32[16,128,128]{2,1,0:T(8,128)S(1)} %dot_general.119, f32[128,128]{1,0:T(8,128)} %get-tuple-element.18, f32[34,128,128]{2,1,0:T(8,128)} %param.4), kind=kOutput, calls=%fused_computation.14 | convolution fusion | flops 402980864 | bytes 2228224 | tf_op jit(solution)/shard_map/dot_general | solution.py:26
  6.1 1.9 %convolution_bitcast_fusion.6 = f32[16,128,128]{2,1,0:T(8,128)S(1)} fusion(f32[16,128,128]{2,1,0:T(8,128)S(1)} %convolution_multiply_fusion.7, f32[34,128,128]{2,1,0:T(8,128)} %param.4), kind=kOutput, calls=%fused_computation.13 | convolution fusion | flops 402718720 | bytes 2162688 | tf_op jit(solution)/shard_map/aic,ij->ajc/dot_general | solution.py:32
  8.2 1.9 %fusion.51 = f32[128,2048]{1,0:T(8,128)S(1)} fusion(f32[128,2048]{1,0:T(8,128)S(1)} %reshape_reshape.40, f32[34,128,128]{2,1,0:T(8,128)} %param.4), kind=kOutput, calls=%fused_computation.83 | convolution fusion | flops 402718720 | bytes 2162688 | tf_op jit(solution)/shard_map/dot_general | solution.py:39
  10.3 1.8 %convolution_multiply_fusion.6 = f32[16,128,128]{2,1,0:T(8,128)S(1)} fusion(f32[16,128,128]{2,1,0:T(8,128)S(1)} %dot_general.123, f32[128,128]{1,0:T(8,128)} %get-tuple-element.17, f32[34,128,128]{2,1,0:T(8,128)} %param.4), kind=kOutput, calls=%fused_computation.12 | convolution fusion | flops 402980864 | bytes 2228224 | tf_op jit(solution)/shard_map/dot_general | solution.py:26
  12.1 1.9 %convolution_bitcast_fusion.5 = f32[16,128,128]{2,1,0:T(8,128)S(1)} fusion(f32[16,128,128]{2,1,0:T(8,128)S(1)} %convolution_multiply_fusion.6, f32[34,128,128]{2,1,0:T(8,128)} %param.4), kind=kOutput, calls=%fused_computation.11 | convolution fusion | flops 402718720 | bytes 2162688 | tf_op jit(solution)/shard_map/aic,ij->ajc/dot_general | solution.py:32
  14.2 1.9 %fusion.48 = f32[128,2048]{1,0:T(8,128)S(1)} fusion(f32[128,2048]{1,0:T(8,128)S(1)} %reshape_reshape.41, f32[34,128,128]{2,1,0:T(8,128)} %param.4), kind=kOutput, calls=%fused_computation.81 | convolution fusion | flops 402718720 | bytes 2162688 | tf_op jit(solution)/shard_map/dot_general | solution.py:39
  16.3 1.8 %convolution_multiply_fusion.5 = f32[16,128,128]{2,1,0:T(8,128)S(1)} fusion(f32[16,128,128]{2,1,0:T(8,128)S(1)} %dot_general.127, f32[128,128]{1,0:T(8,128)S(1)} %get-tuple-element.16, f32[34,128,128]{2,1,0:T(8,128)} %param.4), kind=kOutput, calls=%fused_computation.10 | convolution fusion | flops 402980864 | bytes 2228224 | tf_op jit(solution)/shard_map/dot_general | solution.py:26
  18.1 1.9 %convolution_bitcast_fusion.4 = f32[16,128,128]{2,1,0:T(8,128)S(1)} fusion(f32[16,128,128]{2,1,0:T(8,128)S(1)} %convolution_multiply_fusion.5, f32[34,128,128]{2,1,0:T(8,128)} %param.4), kind=kOutput, calls=%fused_computation.9 | convolution fusion | flops 402718720 | bytes 2162688 | tf_op jit(solution)/shard_map/aic,ij->ajc/dot_general | solution.py:32
  20.2 1.9 %fusion.45 = f32[128,2048]{1,0:T(8,128)S(1)} fusion(f32[128,2048]{1,0:T(8,128)S(1)} %reshape_reshape.42, f32[34,128,128]{2,1,0:T(8,128)} %param.4), kind=kOutput, calls=%fused_computation.79 | convolution fusion | flops 402718720 | bytes 2162688 | tf_op jit(solution)/shard_map/dot_general | solution.py:39
  22.3 2.0 %convolution_multiply_fusion.4 = f32[16,128,128]{2,1,0:T(8,128)S(1)} fusion(f32[16,128,128]{2,1,0:T(8,128)S(1)} %dot_general.131, f32[128,128]{1,0:T(8,128)S(1)} %get-tuple-element.15, f32[34,128,128]{2,1,0:T(8,128)} %param.4), kind=kOutput, calls=%fused_computation.8 | convolution fusion | flops 402980864 | bytes 2228224 | tf_op jit(solution)/shard_map/dot_general | solution.py:26
  24.3 1.9 %convolution_bitcast_fusion.3 = f32[16,128,128]{2,1,0:T(8,128)S(1)} fusion(f32[16,128,128]{2,1,0:T(8,128)S(1)} %convolution_multiply_fusion.4, f32[34,128,128]{2,1,0:T(8,128)} %param.4), kind=kOutput, calls=%fused_computation.7 | convolution fusion | flops 402718720 | bytes 2162688 | tf_op jit(solution)/shard_map/aic,ij->ajc/dot_general | solution.py:32
  26.4 8.3 %collective-permute-start = (f32[1024,128]{1,0:T(8,128)S(1)}, f32[1024,128]{1,0:T(8,128)S(1)}, u32[]{:S(2)}, u32[]{:S(2)}) collective-permute-start(f32[1024,128]{1,0:T(8,128)S(1)} %broadcast_select_fusion), channel_id=1, source_target_pairs={{0,256},{16,272},{32,288},{48,304},{64,320},{80,336},{96,352},{112... | collective-permute-start | bytes 1572872 | tf_op jit(solution)/shard_map/ppermute | solution.py:17
  34.7 14.3 %collective-permute-done = f32[1024,128]{1,0:T(8,128)S(1)} collective-permute-done((f32[1024,128]{1,0:T(8,128)S(1)}, f32[1024,128]{1,0:T(8,128)S(1)}, u32[]{:S(2)}, u32[]{:S(2)}) %collective-permute-start) | collective-permute-done | bytes 524320 | tf_op jit(solution)/shard_map/ppermute | solution.py:17
  49.3 1.9 %fusion.42 = f32[128,2048]{1,0:T(8,128)S(1)} fusion(f32[128,2048]{1,0:T(8,128)S(1)} %select_n.54, f32[34,128,128]{2,1,0:T(8,128)} %param.4), kind=kOutput, calls=%fused_computation.77 | convolution fusion | flops 402718720 | bytes 2162688 | tf_op jit(solution)/shard_map/dot_general | solution.py:39
  51.4 1.8 %convolution_multiply_fusion.3 = f32[16,128,128]{2,1,0:T(8,128)S(1)} fusion(f32[16,128,128]{2,1,0:T(8,128)S(1)} %dot_general.135, f32[128,128]{1,0:T(8,128)S(1)} %get-tuple-element.14, f32[34,128,128]{2,1,0:T(8,128)} %param.4), kind=kOutput, calls=%fused_computation.6 | convolution fusion | flops 402980864 | bytes 2228224 | tf_op jit(solution)/shard_map/dot_general | solution.py:26
  53.2 1.9 %convolution_bitcast_fusion.2 = f32[16,128,128]{2,1,0:T(8,128)S(1)} fusion(f32[16,128,128]{2,1,0:T(8,128)S(1)} %convolution_multiply_fusion.3, f32[34,128,128]{2,1,0:T(8,128)} %param.4), kind=kOutput, calls=%fused_computation.5 | convolution fusion | flops 402718720 | bytes 2162688 | tf_op jit(solution)/shard_map/aic,ij->ajc/dot_general | solution.py:32
  55.3 1.9 %fusion.39 = f32[128,2048]{1,0:T(8,128)S(1)} fusion(f32[128,2048]{1,0:T(8,128)S(1)} %reshape_reshape.43, f32[34,128,128]{2,1,0:T(8,128)} %param.4), kind=kOutput, calls=%fused_computation.75 | convolution fusion | flops 402718720 | bytes 2162688 | tf_op jit(solution)/shard_map/dot_general | solution.py:39
  57.4 1.8 %convolution_multiply_fusion.2 = f32[16,128,128]{2,1,0:T(8,128)S(1)} fusion(f32[16,128,128]{2,1,0:T(8,128)S(1)} %dot_general.139, f32[128,128]{1,0:T(8,128)S(1)} %get-tuple-element.13, f32[34,128,128]{2,1,0:T(8,128)} %param.4), kind=kOutput, calls=%fused_computation.4 | convolution fusion | flops 402980864 | bytes 2228224 | tf_op jit(solution)/shard_map/dot_general | solution.py:26
  59.2 1.9 %convolution_bitcast_fusion.1 = f32[16,128,128]{2,1,0:T(8,128)S(1)} fusion(f32[16,128,128]{2,1,0:T(8,128)S(1)} %convolution_multiply_fusion.2, f32[34,128,128]{2,1,0:T(8,128)} %param.4), kind=kOutput, calls=%fused_computation.3 | convolution fusion | flops 402718720 | bytes 2162688 | tf_op jit(solution)/shard_map/aic,ij->ajc/dot_general | solution.py:32
  61.3 1.9 %fusion.36 = f32[128,2048]{1,0:T(8,128)S(1)} fusion(f32[128,2048]{1,0:T(8,128)S(1)} %reshape_reshape.44, f32[34,128,128]{2,1,0:T(8,128)} %param.4), kind=kOutput, calls=%fused_computation.73 | convolution fusion | flops 402718720 | bytes 2162688 | tf_op jit(solution)/shard_map/dot_general | solution.py:39
  63.3 1.8 %convolution_multiply_fusion.1 = f32[16,128,128]{2,1,0:T(8,128)S(1)} fusion(f32[16,128,128]{2,1,0:T(8,128)S(1)} %dot_general.143, f32[128,128]{1,0:T(8,128)S(1)} %get-tuple-element.12, f32[34,128,128]{2,1,0:T(8,128)} %param.4), kind=kOutput, calls=%fused_computation.2 | convolution fusion | flops 402980864 | bytes 2228224 | tf_op jit(solution)/shard_map/dot_general | solution.py:26
  65.2 1.9 %convolution_bitcast_fusion = f32[16,128,128]{2,1,0:T(8,128)S(1)} fusion(f32[16,128,128]{2,1,0:T(8,128)S(1)} %convolution_multiply_fusion.1, f32[34,128,128]{2,1,0:T(8,128)} %param.4), kind=kOutput, calls=%fused_computation.1 | convolution fusion | flops 402718720 | bytes 2162688 | tf_op jit(solution)/shard_map/aic,ij->ajc/dot_general | solution.py:32
  67.3 1.9 %fusion.33 = f32[128,2048]{1,0:T(8,128)S(1)} fusion(f32[128,2048]{1,0:T(8,128)S(1)} %reshape_reshape.45, f32[34,128,128]{2,1,0:T(8,128)} %param.4), kind=kOutput, calls=%fused_computation.71 | convolution fusion | flops 402718720 | bytes 2162688 | tf_op jit(solution)/shard_map/dot_general | solution.py:39
  69.3 2.1 %convolution_multiply_fusion = f32[16,128,128]{2,1,0:T(8,128)S(1)} fusion(f32[16,128,128]{2,1,0:T(8,128)S(1)} %dot_general.147, f32[128,128]{1,0:T(8,128)S(1)} %get-tuple-element.19, f32[34,128,128]{2,1,0:T(8,128)} %param.4), kind=kOutput, calls=%fused_computation | convolution fusion | flops 402980864 | bytes 2228224 | tf_op jit(solution)/shard_map/dot_general | solution.py:26
  71.4 1.9 %fusion.1 = f32[128,16,128]{2,0,1:T(8,128)S(1)} fusion(f32[16,128,128]{2,1,0:T(8,128)S(1)} %convolution_multiply_fusion, f32[34,128,128]{2,1,0:T(8,128)} %param.4), kind=kOutput, calls=%fused_computation.52 | convolution fusion | flops 402718720 | bytes 2162688 | tf_op jit(solution)/shard_map/aic,ij->ajc/dot_general | solution.py:32
  73.4 1.3 copy.24
  74.7 15.3 %all-to-all-start = ((f32[16,8,2048]{2,1,0:T(8,128)}), f32[16,8,2048]{2,1,0:T(8,128)S(1)}, u32[]{:S(2)}, u32[]{:S(2)}) async-start(f32[16,8,2048]{2,1,0:T(8,128)} %bitcast.65), calls=%async_computation | async-start | bytes 2097152 | tf_op jit(solution)/shard_map/all_to_all | solution.py:90
  90.3 26.7 %all-to-all-done = f32[16,8,2048]{2,1,0:T(8,128)S(1)} async-done(((f32[16,8,2048]{2,1,0:T(8,128)}), f32[16,8,2048]{2,1,0:T(8,128)S(1)}, u32[]{:S(2)}, u32[]{:S(2)}) %all-to-all-start) | async-done | bytes 1048608 | tf_op jit(solution)/shard_map/all_to_all | solution.py:90
  117.1 3.6 %collective-permute-start.1 = (f32[1024,8]{0,1:T(8,128)S(1)}, f32[1024,8]{0,1:T(8,128)S(1)}, u32[]{:S(2)}, u32[]{:S(2)}) collective-permute-start(f32[1024,8]{0,1:T(8,128)S(1)} %get-tuple-element.21), channel_id=1, source_target_pairs={{0,16},{16,0},{32,48},{48,32},{64,80},{80,64},{96,112},{112,96},{1... | collective-permute-start | bytes 98312 | tf_op jit(solution)/shard_map/ppermute | solution.py:17
  121.2 0.2 mul.482
  121.6 0.2 mul.472
  121.9 0.2 mul.477
  122.3 0.2 mul.492
  122.7 0.2 mul.487
  122.9 0.2 copy.39
  123.1 0.2 reshape.198
  123.4 1.1 fusion.30
  124.5 0.2 copy.28
  124.7 0.2 mul.474
  124.9 1.0 fusion.73
  126.0 0.2 reshape_reshape.46
  126.3 1.1 fusion.27
  127.4 0.2 copy.32
  127.6 0.2 mul.479
  127.8 1.0 fusion.76
  128.9 0.2 reshape_reshape.47
  129.2 1.1 fusion.24
  130.3 0.2 copy.36
  130.5 0.2 mul.484
  130.7 1.0 fusion.79
  131.8 0.2 reshape_reshape.48
  132.0 0.2 copy.37
  132.1 1.1 fusion.21
  133.2 0.2 copy.40
  133.4 0.2 mul.489
  133.6 1.0 fusion.82
  134.7 0.2 reshape_reshape.49
  135.0 1.1 fusion.18
  136.1 0.2 copy.44
  136.3 0.2 mul.494
  136.5 1.0 fusion.85
  137.6 0.6 reshape.199
  (61 shorter events, 4.9 us)
Async XLA Ops:
  0.0 2.0 %copy-start = (f32[1,2048,128]{2,1,0:T(8,128)S(1)}, f32[1,2048,128]{2,1,0:T(8,128)}, u32[]{:S(2)}) copy-start(f32[1,2048,128]{2,1,0:T(8,128)} %param.3) | copy-start | bytes 3145732
  26.4 22.6 %collective-permute-start = (f32[1024,128]{1,0:T(8,128)S(1)}, f32[1024,128]{1,0:T(8,128)S(1)}, u32[]{:S(2)}, u32[]{:S(2)}) collective-permute-start(f32[1024,128]{1,0:T(8,128)S(1)} %broadcast_select_fusion), channel_id=1, source_target_pairs={{0,256},{16,272},{32,288},{48,304},{64,320},{80,336},{96,352},{112... | collective-permute-start | bytes 1572872 | tf_op jit(solution)/shard_map/ppermute | solution.py:17
  73.3 16.7 %copy-start.4 = (f32[1,128,128]{2,1,0:T(8,128)S(1)}, f32[1,128,128]{2,1,0:T(8,128)}, u32[]{:S(2)}) copy-start(f32[1,128,128]{2,1,0:T(8,128)} %get-tuple-element.7) | copy-start | bytes 196612
  73.3 16.7 %copy-start.5 = (f32[1,128,128]{2,1,0:T(8,128)S(1)}, f32[1,128,128]{2,1,0:T(8,128)}, u32[]{:S(2)}) copy-start(f32[1,128,128]{2,1,0:T(8,128)} %get-tuple-element.8) | copy-start | bytes 196612
  73.3 16.8 %copy-start.2 = (f32[1,128,128]{2,1,0:T(8,128)S(1)}, f32[1,128,128]{2,1,0:T(8,128)}, u32[]{:S(2)}) copy-start(f32[1,128,128]{2,1,0:T(8,128)} %get-tuple-element.9) | copy-start | bytes 196612
  73.3 16.8 %copy-start.3 = (f32[1,128,128]{2,1,0:T(8,128)S(1)}, f32[1,128,128]{2,1,0:T(8,128)}, u32[]{:S(2)}) copy-start(f32[1,128,128]{2,1,0:T(8,128)} %get-tuple-element.10) | copy-start | bytes 196612
  74.7 46.1 %copy-start.1 = (f32[1,128,128]{2,1,0:T(8,128)S(1)}, f32[1,128,128]{2,1,0:T(8,128)}, u32[]{:S(2)}) copy-start(f32[1,128,128]{2,1,0:T(8,128)} %get-tuple-element.11) | copy-start | bytes 196612
  74.7 42.3 %all-to-all-start = ((f32[16,8,2048]{2,1,0:T(8,128)}), f32[16,8,2048]{2,1,0:T(8,128)S(1)}, u32[]{:S(2)}, u32[]{:S(2)}) async-start(f32[16,8,2048]{2,1,0:T(8,128)} %bitcast.65), calls=%async_computation | async-start | bytes 2097152 | tf_op jit(solution)/shard_map/all_to_all | solution.py:90
  117.1 5.9 %collective-permute-start.1 = (f32[1024,8]{0,1:T(8,128)S(1)}, f32[1024,8]{0,1:T(8,128)S(1)}, u32[]{:S(2)}, u32[]{:S(2)}) collective-permute-start(f32[1024,8]{0,1:T(8,128)S(1)} %get-tuple-element.21), channel_id=1, source_target_pairs={{0,16},{16,0},{32,48},{48,32},{64,80},{80,64},{96,112},{112,96},{1... | collective-permute-start | bytes 98312 | tf_op jit(solution)/shard_map/ppermute | solution.py:17
where the time goes:
time: 140 us; the launch traced here: 138 us
  matrix products  56.1 us (40%)
  waiting for transfers between devices  41.1 us (29%)
  starting transfers between devices  27.3 us (20%)
  local copies, waits for them, and re-layouts  12.7 us (9%)
    all_to_all x1, waiting for transfers between devices, reduce_columns(): gathered = lax.all_to_all(blocks, 'cuts', 0, 0, tiled=False)  26.7 us
    all_to_all x1, starting transfers between devices, reduce_columns(): gathered = lax.all_to_all(blocks, 'cuts', 0, 0, tiled=False)  15.3 us
    dot_general x8, matrix products, apply_mid(): jnp.einsum('aic,ij->ajc', shaped, effective(weight_mat), precision=HIGHES...  15.3 us
    dot_general x8, matrix products, apply_top(): mixed = jnp.dot(effective(weight_mat).T, shaped, precision=HIGHEST_PREC)  15.3 us
    dot_general x8, matrix products, apply_lane(): return jnp.dot(tensor, effective(weight_mat), precision=HIGHEST_PREC)  15 us
    ppermute x2, waiting for transfers between devices, partner(): return lax.ppermute(value, axis, pairs)  14.3 us
    ppermute x2, starting transfers between devices, partner(): return lax.ppermute(value, axis, pairs)  11.9 us
    unnamed x5, matrix products  5.3 us
  transfers between devices with their start and end apart: 3, of which 2 were waited for; matrix products, arithmetic and copies ran while one was open for 2% of the time, Pallas kernels for 0%

commit v1 on v0

--- a/solution.py
+++ b/solution.py
@@ -1,11 +1,13 @@
 import jax
 import jax.numpy as jnp
 from jax import lax
-from jax.sharding import PartitionSpec as P
+from jax.sharding import Mesh, PartitionSpec as P
 
 CYC_A = 4
 CYC_B = 4
 CYC_C = 5
+BITS = ("yh", "z", "core")
+CUTS = ("x", "yl")
 
 
 HIGHEST_PREC = lax.Precision.HIGHEST
@@ -76,37 +78,41 @@
     half_rows = tensor.shape[0] // 2
     lower = tensor[:half_rows]
     upper = tensor[half_rows:]
-    parity = lax.axis_index("bits") >> bit_pos & 1
+    parity = lax.axis_index(BITS) >> bit_pos & 1
     outgoing = jnp.where(parity == 0, upper, lower)
-    incoming = partner(outgoing, "bits", bit_pos)
+    incoming = partner(outgoing, BITS, bit_pos)
     return jnp.where(
         parity == 0, jnp.concatenate([lower, incoming], 0), jnp.concatenate([incoming, upper], 0)
     )
 
 
 def reduce_columns(tensor):
-    n_cuts = lax.axis_size("cuts")
-    blocks = tensor.T.reshape(n_cuts, tensor.shape[1] // n_cuts, tensor.shape[0])
-    gathered = lax.all_to_all(blocks, "cuts", 0, 0, tiled=False)
-    return gathered.sum(0)
+    cols = tensor.T
+    for axis in ("x", "yl"):
+        n = lax.axis_size(axis)
+        blocks = cols.reshape(n, cols.shape[0] // n, cols.shape[1])
+        cols = lax.all_to_all(blocks, axis, 0, 0, tiled=False).sum(0)
+    return cols
 
 
 def on_device(boundary, gate_stack, coupling):
     tensor = boundary[0]
-    top_bit = lax.axis_size("bits").bit_length() - 2
+    top_bit = lax.axis_size(BITS).bit_length() - 2
     tensor = layer_group(tensor, gate_stack, coupling, 0, 0, CYC_A)
     tensor = swap_bit(tensor, top_bit)
     tensor = layer_group(tensor, gate_stack, coupling, 3 * CYC_A, CYC_A, CYC_B)
     cols = reduce_columns(tensor)
     cols = swap_bit(cols.T, 0).T
-    col_start = lax.axis_index("cuts") * cols.shape[0]
+    col_start = lax.axis_index(CUTS) * cols.shape[0]
     cols = final_group_cols(cols, gate_stack, coupling, col_start)
     return cols.T
 
 
 def solution(mesh):
-    in_specs = (P("cuts", "bits", None), P(), P())
-    out_specs = P("bits", "cuts")
+    n_bits, n_cuts = mesh.shape["bits"], mesh.shape["cuts"]
+    fine = Mesh(mesh.devices.reshape(2, n_bits // 4, 2, n_cuts // 4, 4), BITS + CUTS)
+    in_specs = (P(CUTS, BITS, None), P(), P())
+    out_specs = P(BITS, CUTS)
     return jax.shard_map(
-        on_device, mesh=mesh, in_specs=in_specs, out_specs=out_specs, check_vma=False
+        on_device, mesh=fine, in_specs=in_specs, out_specs=out_specs, check_vma=False
     )

time: 140 us -> 137 us (0.979)
  waiting for transfers between devices: 41.1 us -> 19.8 us
  blocking collectives: 0 us -> 14.5 us
  starting transfers between devices: 27.3 us -> 30.9 us
    all_to_all x1, waiting for transfers between devices: 26.7 us -> 5.44 us  [reduce_columns(): cols = lax.all_to_all(blocks, axis, 0, 0, tiled=False).sum(0)]
    all_to_all x0 -> x1, blocking collectives: none -> 14.5 us  [reduce_columns(): cols = lax.all_to_all(blocks, axis, 0, 0, tiled=False).sum(0)]
    ppermute x2, starting transfers between devices: 11.9 us -> 14.5 us  [partner(): return lax.ppermute(value, axis, pairs)]
where the time goes in v1:
time: 137 us; the launch traced here: 135 us
  matrix products  56 us (41%)
  starting transfers between devices  30.9 us (23%)
  waiting for transfers between devices  19.8 us (14%)
  blocking collectives  14.5 us (11%)
  local copies, waits for them, and re-layouts  12.3 us (9%)
    all_to_all x1, starting transfers between devices, reduce_columns(): cols = lax.all_to_all(blocks, axis, 0, 0, tiled=False).sum(0)  16.3 us
    dot_general x8, matrix products, apply_top(): mixed = jnp.dot(effective(weight_mat).T, shaped, precision=HIGHEST_PREC)  15.3 us
    dot_general x8, matrix products, apply_mid(): jnp.einsum('aic,ij->ajc', shaped, effective(weight_mat), precision=HIGHES...  15.2 us
    dot_general x8, matrix products, apply_lane(): return jnp.dot(tensor, effective(weight_mat), precision=HIGHEST_PREC)  15 us
    ppermute x2, starting transfers between devices, partner(): return lax.ppermute(value, axis, pairs)  14.5 us
    all_to_all x1, blocking collectives, reduce_columns(): cols = lax.all_to_all(blocks, axis, 0, 0, tiled=False).sum(0)  14.5 us
    ppermute x2, waiting for transfers between devices, partner(): return lax.ppermute(value, axis, pairs)  14.3 us
    all_to_all x1, waiting for transfers between devices, reduce_columns(): cols = lax.all_to_all(blocks, axis, 0, 0, tiled=False).sum(0)  5.44 us
  transfers between devices with their start and end apart: 3, of which 2 were waited for; matrix products, arithmetic and copies ran while one was open for 2% of the time, Pallas kernels for 0%

profile of v1, /device:TPU:1, one launch (start us, length us, event | category | flops | bytes accessed | tf_op | source)
XLA Modules:
  0.0 135.1 jit_solution(423352808665732572)
XLA Ops:
  0.0 2.0 %fusion.369 = (f32[1,128,128]{2,1,0:T(8,128)}, f32[1,128,128]{2,1,0:T(8,128)}, f32[1,128,128]{2,1,0:T(8,128)}, f32[1,128,128]{2,1,0:T(8,128)}, f32[1,128,128]{2,...) fusion(f32[13,128,128]{2,1,0:T(8,128)} %param.5), kind=kLoop, calls=%fused_computation.404 | loop fusion | bytes 1703936 | tf_op jit(solution)/shard_map/slice | solution.py:69
  2.2 1.9 %fusion.54 = f32[128,2048]{1,0:T(8,128)S(1)} fusion(f32[128,2048]{1,0:T(8,128)S(1)} %reshape_squeeze.3, f32[34,128,128]{2,1,0:T(8,128)} %param.4), kind=kOutput, calls=%fused_computation.86 | convolution fusion | flops 402718720 | bytes 2162688 | tf_op jit(solution)/shard_map/dot_general | solution.py:41
  4.3 1.8 %convolution_multiply_fusion.7 = f32[16,128,128]{2,1,0:T(8,128)S(1)} fusion(f32[16,128,128]{2,1,0:T(8,128)S(1)} %dot_general.119, f32[128,128]{1,0:T(8,128)} %get-tuple-element.18, f32[34,128,128]{2,1,0:T(8,128)} %param.4), kind=kOutput, calls=%fused_computation.14 | convolution fusion | flops 402980864 | bytes 2228224 | tf_op jit(solution)/shard_map/dot_general | solution.py:28
  6.1 1.9 %convolution_bitcast_fusion.6 = f32[16,128,128]{2,1,0:T(8,128)S(1)} fusion(f32[16,128,128]{2,1,0:T(8,128)S(1)} %convolution_multiply_fusion.7, f32[34,128,128]{2,1,0:T(8,128)} %param.4), kind=kOutput, calls=%fused_computation.13 | convolution fusion | flops 402718720 | bytes 2162688 | tf_op jit(solution)/shard_map/aic,ij->ajc/dot_general | solution.py:34
  8.2 1.9 %fusion.51 = f32[128,2048]{1,0:T(8,128)S(1)} fusion(f32[128,2048]{1,0:T(8,128)S(1)} %reshape_reshape.40, f32[34,128,128]{2,1,0:T(8,128)} %param.4), kind=kOutput, calls=%fused_computation.84 | convolution fusion | flops 402718720 | bytes 2162688 | tf_op jit(solution)/shard_map/dot_general | solution.py:41
  10.3 1.8 %convolution_multiply_fusion.6 = f32[16,128,128]{2,1,0:T(8,128)S(1)} fusion(f32[16,128,128]{2,1,0:T(8,128)S(1)} %dot_general.123, f32[128,128]{1,0:T(8,128)} %get-tuple-element.17, f32[34,128,128]{2,1,0:T(8,128)} %param.4), kind=kOutput, calls=%fused_computation.12 | convolution fusion | flops 402980864 | bytes 2228224 | tf_op jit(solution)/shard_map/dot_general | solution.py:28
  12.1 1.9 %convolution_bitcast_fusion.5 = f32[16,128,128]{2,1,0:T(8,128)S(1)} fusion(f32[16,128,128]{2,1,0:T(8,128)S(1)} %convolution_multiply_fusion.6, f32[34,128,128]{2,1,0:T(8,128)} %param.4), kind=kOutput, calls=%fused_computation.11 | convolution fusion | flops 402718720 | bytes 2162688 | tf_op jit(solution)/shard_map/aic,ij->ajc/dot_general | solution.py:34
  14.2 1.9 %fusion.48 = f32[128,2048]{1,0:T(8,128)S(1)} fusion(f32[128,2048]{1,0:T(8,128)S(1)} %reshape_reshape.41, f32[34,128,128]{2,1,0:T(8,128)} %param.4), kind=kOutput, calls=%fused_computation.82 | convolution fusion | flops 402718720 | bytes 2162688 | tf_op jit(solution)/shard_map/dot_general | solution.py:41
  16.3 1.8 %convolution_multiply_fusion.5 = f32[16,128,128]{2,1,0:T(8,128)S(1)} fusion(f32[16,128,128]{2,1,0:T(8,128)S(1)} %dot_general.127, f32[128,128]{1,0:T(8,128)S(1)} %get-tuple-element.16, f32[34,128,128]{2,1,0:T(8,128)} %param.4), kind=kOutput, calls=%fused_computation.10 | convolution fusion | flops 402980864 | bytes 2228224 | tf_op jit(solution)/shard_map/dot_general | solution.py:28
  18.1 1.9 %convolution_bitcast_fusion.4 = f32[16,128,128]{2,1,0:T(8,128)S(1)} fusion(f32[16,128,128]{2,1,0:T(8,128)S(1)} %convolution_multiply_fusion.5, f32[34,128,128]{2,1,0:T(8,128)} %param.4), kind=kOutput, calls=%fused_computation.9 | convolution fusion | flops 402718720 | bytes 2162688 | tf_op jit(solution)/shard_map/aic,ij->ajc/dot_general | solution.py:34
  20.2 1.9 %fusion.45 = f32[128,2048]{1,0:T(8,128)S(1)} fusion(f32[128,2048]{1,0:T(8,128)S(1)} %reshape_reshape.42, f32[34,128,128]{2,1,0:T(8,128)} %param.4), kind=kOutput, calls=%fused_computation.80 | convolution fusion | flops 402718720 | bytes 2162688 | tf_op jit(solution)/shard_map/dot_general | solution.py:41
  22.3 2.0 %convolution_multiply_fusion.4 = f32[16,128,128]{2,1,0:T(8,128)S(1)} fusion(f32[16,128,128]{2,1,0:T(8,128)S(1)} %dot_general.131, f32[128,128]{1,0:T(8,128)S(1)} %get-tuple-element.15, f32[34,128,128]{2,1,0:T(8,128)} %param.4), kind=kOutput, calls=%fused_computation.8 | convolution fusion | flops 402980864 | bytes 2228224 | tf_op jit(solution)/shard_map/dot_general | solution.py:28
  24.3 1.9 %convolution_bitcast_fusion.3 = f32[16,128,128]{2,1,0:T(8,128)S(1)} fusion(f32[16,128,128]{2,1,0:T(8,128)S(1)} %convolution_multiply_fusion.4, f32[34,128,128]{2,1,0:T(8,128)} %param.4), kind=kOutput, calls=%fused_computation.7 | convolution fusion | flops 402718720 | bytes 2162688 | tf_op jit(solution)/shard_map/aic,ij->ajc/dot_general | solution.py:34
  26.4 8.3 %collective-permute-start = (f32[1024,128]{1,0:T(8,128)S(1)}, f32[1024,128]{1,0:T(8,128)S(1)}, u32[]{:S(2)}, u32[]{:S(2)}) collective-permute-start(f32[1024,128]{1,0:T(8,128)S(1)} %broadcast_select_fusion), channel_id=1, source_target_pairs={{0,256},{16,272},{32,288},{48,304},{64,320},{80,336},{96,352},{112... | collective-permute-start | bytes 1572872 | tf_op jit(solution)/shard_map/ppermute | solution.py:19
  34.7 14.3 %collective-permute-done = f32[1024,128]{1,0:T(8,128)S(1)} collective-permute-done((f32[1024,128]{1,0:T(8,128)S(1)}, f32[1024,128]{1,0:T(8,128)S(1)}, u32[]{:S(2)}, u32[]{:S(2)}) %collective-permute-start) | collective-permute-done | bytes 524320 | tf_op jit(solution)/shard_map/ppermute | solution.py:19
  49.3 1.9 %fusion.42 = f32[128,2048]{1,0:T(8,128)S(1)} fusion(f32[128,2048]{1,0:T(8,128)S(1)} %select_n.54, f32[34,128,128]{2,1,0:T(8,128)} %param.4), kind=kOutput, calls=%fused_computation.78 | convolution fusion | flops 402718720 | bytes 2162688 | tf_op jit(solution)/shard_map/dot_general | solution.py:41
  51.4 1.8 %convolution_multiply_fusion.3 = f32[16,128,128]{2,1,0:T(8,128)S(1)} fusion(f32[16,128,128]{2,1,0:T(8,128)S(1)} %dot_general.135, f32[128,128]{1,0:T(8,128)S(1)} %get-tuple-element.14, f32[34,128,128]{2,1,0:T(8,128)} %param.4), kind=kOutput, calls=%fused_computation.6 | convolution fusion | flops 402980864 | bytes 2228224 | tf_op jit(solution)/shard_map/dot_general | solution.py:28
  53.2 1.9 %convolution_bitcast_fusion.2 = f32[16,128,128]{2,1,0:T(8,128)S(1)} fusion(f32[16,128,128]{2,1,0:T(8,128)S(1)} %convolution_multiply_fusion.3, f32[34,128,128]{2,1,0:T(8,128)} %param.4), kind=kOutput, calls=%fused_computation.5 | convolution fusion | flops 402718720 | bytes 2162688 | tf_op jit(solution)/shard_map/aic,ij->ajc/dot_general | solution.py:34
  55.3 1.9 %fusion.39 = f32[128,2048]{1,0:T(8,128)S(1)} fusion(f32[128,2048]{1,0:T(8,128)S(1)} %reshape_reshape.43, f32[34,128,128]{2,1,0:T(8,128)} %param.4), kind=kOutput, calls=%fused_computation.76 | convolution fusion | flops 402718720 | bytes 2162688 | tf_op jit(solution)/shard_map/dot_general | solution.py:41
  57.4 1.8 %convolution_multiply_fusion.2 = f32[16,128,128]{2,1,0:T(8,128)S(1)} fusion(f32[16,128,128]{2,1,0:T(8,128)S(1)} %dot_general.139, f32[128,128]{1,0:T(8,128)S(1)} %get-tuple-element.13, f32[34,128,128]{2,1,0:T(8,128)} %param.4), kind=kOutput, calls=%fused_computation.4 | convolution fusion | flops 402980864 | bytes 2228224 | tf_op jit(solution)/shard_map/dot_general | solution.py:28
  59.2 1.9 %convolution_bitcast_fusion.1 = f32[16,128,128]{2,1,0:T(8,128)S(1)} fusion(f32[16,128,128]{2,1,0:T(8,128)S(1)} %convolution_multiply_fusion.2, f32[34,128,128]{2,1,0:T(8,128)} %param.4), kind=kOutput, calls=%fused_computation.3 | convolution fusion | flops 402718720 | bytes 2162688 | tf_op jit(solution)/shard_map/aic,ij->ajc/dot_general | solution.py:34
  61.3 1.9 %fusion.36 = f32[128,2048]{1,0:T(8,128)S(1)} fusion(f32[128,2048]{1,0:T(8,128)S(1)} %reshape_reshape.44, f32[34,128,128]{2,1,0:T(8,128)} %param.4), kind=kOutput, calls=%fused_computation.74 | convolution fusion | flops 402718720 | bytes 2162688 | tf_op jit(solution)/shard_map/dot_general | solution.py:41
  63.3 1.8 %convolution_multiply_fusion.1 = f32[16,128,128]{2,1,0:T(8,128)S(1)} fusion(f32[16,128,128]{2,1,0:T(8,128)S(1)} %dot_general.143, f32[128,128]{1,0:T(8,128)S(1)} %get-tuple-element.12, f32[34,128,128]{2,1,0:T(8,128)} %param.4), kind=kOutput, calls=%fused_computation.2 | convolution fusion | flops 402980864 | bytes 2228224 | tf_op jit(solution)/shard_map/dot_general | solution.py:28
  65.2 1.9 %convolution_bitcast_fusion = f32[16,128,128]{2,1,0:T(8,128)S(1)} fusion(f32[16,128,128]{2,1,0:T(8,128)S(1)} %convolution_multiply_fusion.1, f32[34,128,128]{2,1,0:T(8,128)} %param.4), kind=kOutput, calls=%fused_computation.1 | convolution fusion | flops 402718720 | bytes 2162688 | tf_op jit(solution)/shard_map/aic,ij->ajc/dot_general | solution.py:34
  67.2 1.9 %fusion.33 = f32[128,2048]{1,0:T(8,128)S(1)} fusion(f32[128,2048]{1,0:T(8,128)S(1)} %reshape_reshape.45, f32[34,128,128]{2,1,0:T(8,128)} %param.4), kind=kOutput, calls=%fused_computation.72 | convolution fusion | flops 402718720 | bytes 2162688 | tf_op jit(solution)/shard_map/dot_general | solution.py:41
  69.3 2.1 %convolution_multiply_fusion = f32[16,128,128]{2,1,0:T(8,128)S(1)} fusion(f32[16,128,128]{2,1,0:T(8,128)S(1)} %dot_general.147, f32[128,128]{1,0:T(8,128)S(1)} %get-tuple-element.19, f32[34,128,128]{2,1,0:T(8,128)} %param.4), kind=kOutput, calls=%fused_computation | convolution fusion | flops 402980864 | bytes 2228224 | tf_op jit(solution)/shard_map/dot_general | solution.py:28
  71.4 0.5 copy.52
  71.9 1.8 %fusion.1 = f32[128,16,128]{0,1,2:T(8,128)S(1)} fusion(f32[16,128,128]{1,0,2:T(8,128)S(1)} %copy.52, f32[34,128,128]{2,1,0:T(8,128)} %param.4), kind=kOutput, calls=%fused_computation.53 | convolution fusion | flops 402718720 | bytes 2162688 | tf_op jit(solution)/shard_map/aic,ij->ajc/dot_general | solution.py:34
  73.7 0.3 copy.99
  74.1 14.5 %all_to_all.10 = f32[4,32,2048]{2,1,0:T(8,128)S(1)} all-to-all(f32[4,32,2048]{2,1,0:T(8,128)S(1)} %bitcast.281), channel_id=1, replica_groups=mesh['yh'=2,'z'=8,'core'=2,'x'=4,'yl'=4] {'x'}, dimensions={0} | all-to-all | bytes 2097152 | tf_op jit(solution)/shard_map/all_to_all | solution.py:94
  88.6 0.8 reduce_sum.18
  89.4 16.3 %all-to-all-start.1 = ((f32[4,8,2048]{2,1,0:T(8,128)}), f32[4,8,2048]{2,1,0:T(8,128)S(1)}, u32[]{:S(2)}, u32[]{:S(2)}) async-start(f32[4,8,2048]{2,1,0:T(8,128)} %bitcast.65), calls=%async_computation.1 | async-start | bytes 524288 | tf_op jit(solution)/shard_map/all_to_all | solution.py:94
  105.9 5.4 %all-to-all-done.1 = f32[4,8,2048]{2,1,0:T(8,128)S(1)} async-done(((f32[4,8,2048]{2,1,0:T(8,128)}), f32[4,8,2048]{2,1,0:T(8,128)S(1)}, u32[]{:S(2)}, u32[]{:S(2)}) %all-to-all-start.1) | async-done | bytes 262176 | tf_op jit(solution)/shard_map/all_to_all | solution.py:94
  111.4 6.3 %collective-permute-start.1 = (f32[1024,8]{0,1:T(8,128)S(1)}, f32[1024,8]{0,1:T(8,128)S(1)}, u32[]{:S(2)}, u32[]{:S(2)}) collective-permute-start(f32[1024,8]{0,1:T(8,128)S(1)} %get-tuple-element.21), channel_id=1, source_target_pairs={{0,16},{16,0},{32,48},{48,32},{64,80},{80,64},{96,112},{112,96},{1... | collective-permute-start | bytes 98312 | tf_op jit(solution)/shard_map/ppermute | solution.py:19
  118.1 0.2 mul.496
  118.5 0.2 mul.486
  118.9 0.2 mul.491
  119.2 0.2 mul.506
  119.6 0.2 mul.501
  120.0 0.2 reshape.202
  120.4 1.1 fusion.30
  121.4 0.2 copy.56
  121.6 0.2 mul.488
  121.8 1.0 fusion.73
  122.9 0.2 reshape_reshape.46
  123.3 1.1 fusion.27
  124.3 0.2 copy.60
  124.5 0.2 mul.493
  124.7 1.0 fusion.76
  125.8 0.2 reshape_reshape.47
  126.1 1.1 fusion.24
  127.2 0.2 copy.64
  127.4 0.2 mul.498
  127.6 1.0 fusion.79
  128.7 0.2 reshape_reshape.48
  129.0 1.1 fusion.21
  130.1 0.2 copy.68
  130.3 0.2 mul.503
  130.5 1.0 fusion.82
  131.9 1.1 fusion.18
  133.0 0.2 copy.72
  133.2 0.2 mul.508
  133.4 1.0 fusion.85
  134.5 0.6 reshape.203
  (64 shorter events, 5.4 us)
Async XLA Ops:
  0.0 2.0 %copy-start = (f32[1,2048,128]{2,1,0:T(8,128)S(1)}, f32[1,2048,128]{2,1,0:T(8,128)}, u32[]{:S(2)}) copy-start(f32[1,2048,128]{2,1,0:T(8,128)} %param.3) | copy-start | bytes 3145732
  26.4 22.6 %collective-permute-start = (f32[1024,128]{1,0:T(8,128)S(1)}, f32[1024,128]{1,0:T(8,128)S(1)}, u32[]{:S(2)}, u32[]{:S(2)}) collective-permute-start(f32[1024,128]{1,0:T(8,128)S(1)} %broadcast_select_fusion), channel_id=1, source_target_pairs={{0,256},{16,272},{32,288},{48,304},{64,320},{80,336},{96,352},{112... | collective-permute-start | bytes 1572872 | tf_op jit(solution)/shard_map/ppermute | solution.py:19
  74.1 31.6 %copy-start.4 = (f32[1,128,128]{2,1,0:T(8,128)S(1)}, f32[1,128,128]{2,1,0:T(8,128)}, u32[]{:S(2)}) copy-start(f32[1,128,128]{2,1,0:T(8,128)} %get-tuple-element.7) | copy-start | bytes 196612
  74.1 31.6 %copy-start.5 = (f32[1,128,128]{2,1,0:T(8,128)S(1)}, f32[1,128,128]{2,1,0:T(8,128)}, u32[]{:S(2)}) copy-start(f32[1,128,128]{2,1,0:T(8,128)} %get-tuple-element.8) | copy-start | bytes 196612
  74.1 31.7 %copy-start.2 = (f32[1,128,128]{2,1,0:T(8,128)S(1)}, f32[1,128,128]{2,1,0:T(8,128)}, u32[]{:S(2)}) copy-start(f32[1,128,128]{2,1,0:T(8,128)} %get-tuple-element.9) | copy-start | bytes 196612
  74.1 31.7 %copy-start.3 = (f32[1,128,128]{2,1,0:T(8,128)S(1)}, f32[1,128,128]{2,1,0:T(8,128)}, u32[]{:S(2)}) copy-start(f32[1,128,128]{2,1,0:T(8,128)} %get-tuple-element.10) | copy-start | bytes 196612
  74.1 43.5 %copy-start.1 = (f32[1,128,128]{2,1,0:T(8,128)S(1)}, f32[1,128,128]{2,1,0:T(8,128)}, u32[]{:S(2)}) copy-start(f32[1,128,128]{2,1,0:T(8,128)} %get-tuple-element.11) | copy-start | bytes 196612
  89.4 22.0 %all-to-all-start.1 = ((f32[4,8,2048]{2,1,0:T(8,128)}), f32[4,8,2048]{2,1,0:T(8,128)S(1)}, u32[]{:S(2)}, u32[]{:S(2)}) async-start(f32[4,8,2048]{2,1,0:T(8,128)} %bitcast.65), calls=%async_computation.1 | async-start | bytes 524288 | tf_op jit(solution)/shard_map/all_to_all | solution.py:94
  111.4 8.6 %collective-permute-start.1 = (f32[1024,8]{0,1:T(8,128)S(1)}, f32[1024,8]{0,1:T(8,128)S(1)}, u32[]{:S(2)}, u32[]{:S(2)}) collective-permute-start(f32[1024,8]{0,1:T(8,128)S(1)} %get-tuple-element.21), channel_id=1, source_target_pairs={{0,16},{16,0},{32,48},{48,32},{64,80},{80,64},{96,112},{112,96},{1... | collective-permute-start | bytes 98312 | tf_op jit(solution)/shard_map/ppermute | solution.py:19

commit v2 on v1

--- a/solution.py
+++ b/solution.py
@@ -1,6 +1,9 @@
+import functools
+
 import jax
 import jax.numpy as jnp
 from jax import lax
+from jax.experimental import pallas as pl
 from jax.sharding import Mesh, PartitionSpec as P
 
 CYC_A = 4
@@ -8,6 +11,57 @@
 CYC_C = 5
 BITS = ("yh", "z", "core")
 CUTS = ("x", "yl")
+
+BLOCK = 128
+
+
+def _split(a):
+    hi = a.astype(jnp.bfloat16)
+    lo = (a - hi.astype(jnp.float32)).astype(jnp.bfloat16)
+    return hi, lo
+
+
+def _mm3(a, b):
+    dot = functools.partial(jnp.dot, preferred_element_type=jnp.float32)
+    return dot(a[0], b[0]) + (dot(a[1], b[0]) + dot(a[0], b[1]))
+
+
+def _layers_kernel(x_ref, g_ref, c_ref, o_ref, *, gate_base, cpl_base, cycles):
+    rows = x_ref.shape[0]
+    n_blocks = rows // BLOCK
+    stride = rows // BLOCK
+    o_ref[...] = x_ref[...]
+    for turn in range(cycles):
+        first = gate_base + 3 * turn
+        top_t = _split((0.45 * g_ref[first]).T)
+        lane_g = _split(0.45 * g_ref[first + 1])
+        mid_t = _split((0.45 * g_ref[first + 2]).T)
+        table = c_ref[cpl_base + turn]
+
+        def top(t, carry):
+            rows_t = pl.ds(t, BLOCK, stride=stride)
+            xt = o_ref[rows_t, :]
+            o_ref[rows_t, :] = 0.9 * xt + _mm3(top_t, _split(xt))
+            return carry
+
+        lax.fori_loop(0, stride, top, 0)
+
+        def lane_mid(a, carry):
+            rows_a = pl.ds(pl.multiple_of(a * BLOCK, BLOCK), BLOCK)
+            xa = o_ref[rows_a, :]
+            xa = (0.9 * xa + _mm3(_split(xa), lane_g)) * table
+            o_ref[rows_a, :] = 0.9 * xa + _mm3(mid_t, _split(xa))
+            return carry
+
+        lax.fori_loop(0, n_blocks, lane_mid, 0)
+
+
+def layers(x, gate_stack, coupling, gate_base, cpl_base, cycles):
+    kernel = functools.partial(_layers_kernel, gate_base=gate_base, cpl_base=cpl_base, cycles=cycles)
+    return pl.pallas_call(
+        kernel,
+        out_shape=jax.ShapeDtypeStruct(x.shape, x.dtype),
+    )(x, gate_stack, coupling)
 
 
 HIGHEST_PREC = lax.Precision.HIGHEST
@@ -98,9 +152,9 @@
 def on_device(boundary, gate_stack, coupling):
     tensor = boundary[0]
     top_bit = lax.axis_size(BITS).bit_length() - 2
-    tensor = layer_group(tensor, gate_stack, coupling, 0, 0, CYC_A)
+    tensor = layers(tensor, gate_stack, coupling, 0, 0, CYC_A)
     tensor = swap_bit(tensor, top_bit)
-    tensor = layer_group(tensor, gate_stack, coupling, 3 * CYC_A, CYC_A, CYC_B)
+    tensor = layers(tensor, gate_stack, coupling, 3 * CYC_A, CYC_A, CYC_B)
     cols = reduce_columns(tensor)
     cols = swap_bit(cols.T, 0).T
     col_start = lax.axis_index(CUTS) * cols.shape[0]

time: 137 us -> 171 us (1.25)
  Pallas kernels: 0 us -> 81 us
  matrix products: 56 us -> 10.6 us
  blocking collectives: 14.5 us -> 0 us
  waiting for transfers between devices: 19.8 us -> 28.5 us
  starting transfers between devices: 30.9 us -> 35.7 us
  other arithmetic: 1.04 us -> 3.31 us
  local copies, waits for them, and re-layouts: 12.3 us -> 10.3 us
    pallas_call x0 -> x2, Pallas kernels: none -> 81 us  [layers(): pl.pallas_call(kernel, out_shape=jax.ShapeDtypeStruct(x.shape, x.dtype))]
    dot_general x24 -> x0, matrix products: 45.5 us -> none  [the longest x8 15.3 us: apply_top(): mixed = jnp.dot(effective(weight_mat).T, shaped, precision=HIGHEST_PREC)]
    all_to_all x1 -> x0, blocking collectives: 14.5 us -> none  [reduce_columns(): cols = lax.all_to_all(blocks, axis, 0, 0, tiled=False).sum(0)]
    all_to_all x1 -> x2, waiting for transfers between devices: 5.44 us -> 14.2 us  [reduce_columns(): cols = lax.all_to_all(blocks, axis, 0, 0, tiled=False).sum(0)]
    all_to_all x1 -> x2, starting transfers between devices: 16.3 us -> 21.1 us  [reduce_columns(): cols = lax.all_to_all(blocks, axis, 0, 0, tiled=False).sum(0)]
    transpose x0 -> x1, local copies, waits for them, and re-layouts: none -> 2.58 us  [reduce_columns(): cols = tensor.T]
  transfers between devices with their start and end apart: 3 -> 4, of which waited for: 2 -> 3; matrix products, arithmetic and copies ran while one was open for 2% -> 2% of each run, Pallas kernels for 0% -> 0%
where the time goes in v2:
time: 171 us; the launch traced here: 170 us
  Pallas kernels  81 us (47%)
  starting transfers between devices  35.7 us (21%)
  waiting for transfers between devices  28.5 us (17%)
  matrix products  10.6 us (6%)
  local copies, waits for them, and re-layouts  10.3 us (6%)
  other arithmetic  3.31 us (2%)
    pallas_call x2, Pallas kernels, layers(): pl.pallas_call(kernel, out_shape=jax.ShapeDtypeStruct(x.shape, x.dtype))  81 us
    all_to_all x2, starting transfers between devices, reduce_columns(): cols = lax.all_to_all(blocks, axis, 0, 0, tiled=False).sum(0)  21.1 us
    ppermute x2, starting transfers between devices, partner(): return lax.ppermute(value, axis, pairs)  14.5 us
    ppermute x2, waiting for transfers between devices, partner(): return lax.ppermute(value, axis, pairs)  14.3 us
    all_to_all x2, waiting for transfers between devices, reduce_columns(): cols = lax.all_to_all(blocks, axis, 0, 0, tiled=False).sum(0)  14.2 us
    unnamed x5, matrix products  5.3 us
    dot_general x5, matrix products, final_group_cols(): jnp.dot(cols.reshape(-1, order_size), mid_mat, precision=HIGHEST_PREC)  5.25 us
    mul x25, local copies, waits for them, and re-layouts, final_group_cols(): cols = (shaped * table.T[:, None, :]).reshape(cols.shape)  3.82 us
  transfers between devices with their start and end apart: 4, of which 3 were waited for; matrix products, arithmetic and copies ran while one was open for 2% of the time, Pallas kernels for 0%

profile of v2, /device:TPU:1, one launch (start us, length us, event | category | flops | bytes accessed | tf_op | source)
XLA Modules:
  0.0 169.7 jit_solution(4618256578432205177)
XLA Ops:
  0.0 40.5 %shard_map.37 = f32[2048,128]{1,0:T(8,128)} custom-call(f32[2048,128]{1,0:T(8,128)} %bitcast.94, f32[34,128,128]{2,1,0:T(8,128)} %g_ref.3, f32[13,128,128]{2,1,0:T(8,128)} %c_ref.3), custom_call_target="tpu_custom_call" | custom-call | tf_op jit(solution)/shard_map/pallas_call | solution.py:61
  40.5 1.3 fusion.111
  41.8 8.3 %collective-permute-start = (f32[1024,128]{1,0:T(8,128)S(1)}, f32[1024,128]{1,0:T(8,128)S(1)}, u32[]{:S(2)}, u32[]{:S(2)}) collective-permute-start(f32[1024,128]{1,0:T(8,128)S(1)} %get-tuple-element.6), channel_id=1, source_target_pairs={{0,256},{16,272},{32,288},{48,304},{64,320},{80,336},{96,352},{112... | collective-permute-start | bytes 1572872 | tf_op jit(solution)/shard_map/ppermute | solution.py:73
  50.1 14.3 %collective-permute-done = f32[1024,128]{1,0:T(8,128)S(1)} collective-permute-done((f32[1024,128]{1,0:T(8,128)S(1)}, f32[1024,128]{1,0:T(8,128)S(1)}, u32[]{:S(2)}, u32[]{:S(2)}) %collective-permute-start) | collective-permute-done | bytes 524320 | tf_op jit(solution)/shard_map/ppermute | solution.py:73
  64.4 1.1 maximum_select_fusion.x_ref
  65.5 40.5 %shard_map.38 = f32[2048,128]{1,0:T(8,128)} custom-call(f32[2048,128]{1,0:T(8,128)} %maximum_select_fusion.x_ref, f32[34,128,128]{2,1,0:T(8,128)} %g_ref.3, f32[13,128,128]{2,1,0:T(8,128)} %c_ref.3), custom_call_target="tpu_custom_call" | custom-call | tf_op jit(solution)/shard_map/pallas_call | solution.py:61
  106.0 2.6 %copy.29 = f32[128,2048]{1,0:T(8,128)} copy(f32[128,2048]{0,1:T(8,128)} %bitcast.93) | data formatting | bytes 2097152 | tf_op jit(solution)/shard_map/transpose | solution.py:144
  108.6 4.8 %all-to-all-start = ((f32[4,32,2048]{2,1,0:T(8,128)}), f32[4,32,2048]{2,1,0:T(8,128)S(1)}, u32[]{:S(2)}, u32[]{:S(2)}) async-start(f32[4,32,2048]{2,1,0:T(8,128)} %bitcast.7), calls=%async_computation | async-start | bytes 2097152 | tf_op jit(solution)/shard_map/all_to_all | solution.py:148
  113.4 9.7 %all-to-all-done = f32[4,32,2048]{2,1,0:T(8,128)S(1)} async-done(((f32[4,32,2048]{2,1,0:T(8,128)}), f32[4,32,2048]{2,1,0:T(8,128)S(1)}, u32[]{:S(2)}, u32[]{:S(2)}) %all-to-all-start) | async-done | bytes 1048608 | tf_op jit(solution)/shard_map/all_to_all | solution.py:148
  123.2 0.8 reduce_sum.18
  123.9 16.3 %all-to-all-start.1 = ((f32[4,8,2048]{2,1,0:T(8,128)}), f32[4,8,2048]{2,1,0:T(8,128)S(1)}, u32[]{:S(2)}, u32[]{:S(2)}) async-start(f32[4,8,2048]{2,1,0:T(8,128)} %bitcast.8), calls=%async_computation.1 | async-start | bytes 524288 | tf_op jit(solution)/shard_map/all_to_all | solution.py:148
  140.3 1.0 fusion.112
  141.3 0.1 constant_dynamic-slice_fusion.2
  141.4 0.1 constant_dynamic-slice_fusion
  141.5 4.5 %all-to-all-done.1 = f32[4,8,2048]{2,1,0:T(8,128)S(1)} async-done(((f32[4,8,2048]{2,1,0:T(8,128)}), f32[4,8,2048]{2,1,0:T(8,128)S(1)}, u32[]{:S(2)}, u32[]{:S(2)}) %all-to-all-start.1) | async-done | bytes 262176 | tf_op jit(solution)/shard_map/all_to_all | solution.py:148
  146.0 6.3 %collective-permute-start.1 = (f32[1024,8]{0,1:T(8,128)S(1)}, f32[1024,8]{0,1:T(8,128)S(1)}, u32[]{:S(2)}, u32[]{:S(2)}) collective-permute-start(f32[1024,8]{0,1:T(8,128)S(1)} %get-tuple-element.14), channel_id=1, source_target_pairs={{0,16},{16,0},{32,48},{48,32},{64,80},{80,64},{96,112},{112,96},{1... | collective-permute-start | bytes 98312 | tf_op jit(solution)/shard_map/ppermute | solution.py:73
  152.2 0.1 constant_dynamic-slice_fusion.4
  152.3 0.1 copy.51
  152.4 0.2 mul.165
  152.6 0.2 copy.32
  152.8 0.1 copy.53
  152.8 0.2 mul.170
  153.0 0.2 copy.36
  153.2 0.1 copy.55
  153.3 0.2 mul.175
  153.5 0.2 copy.40
  153.7 0.1 copy.57
  153.7 0.2 mul.180
  153.9 0.2 copy.44
  154.1 0.1 copy.59
  154.2 0.2 mul.185
  154.4 0.2 copy.48
  154.5 0.0 collective-permute-done.1
  154.6 0.2 reshape.86
  154.8 0.2 copy.30
  154.9 1.1 fusion.13
  156.0 0.2 copy.33
  156.2 0.2 mul.167
  156.4 1.0 fusion.16
  157.5 0.2 reshape_reshape.8
  157.7 0.2 copy.34
  157.8 1.1 fusion.10
  158.9 0.2 copy.37
  159.1 0.2 mul.172
  159.3 1.0 fusion.19
  160.4 0.2 reshape_reshape.9
  160.6 0.2 copy.38
  160.7 1.1 fusion.7
  161.8 0.2 copy.41
  162.0 0.2 mul.177
  162.2 1.0 fusion.22
  163.3 0.2 reshape_reshape.10
  163.5 0.2 copy.42
  163.6 1.1 fusion.4
  164.7 0.2 copy.45
  164.9 0.2 mul.182
  165.1 1.0 fusion.25
  166.2 0.2 reshape_reshape.11
  166.4 0.2 copy.46
  166.5 1.1 fusion.1
  167.6 0.2 copy.49
  167.8 0.2 mul.187
  168.0 1.0 fusion.28
  169.1 0.6 reshape.87
  (13 shorter events, 0.1 us)
Async XLA Ops:
  41.8 22.6 %collective-permute-start = (f32[1024,128]{1,0:T(8,128)S(1)}, f32[1024,128]{1,0:T(8,128)S(1)}, u32[]{:S(2)}, u32[]{:S(2)}) collective-permute-start(f32[1024,128]{1,0:T(8,128)S(1)} %get-tuple-element.6), channel_id=1, source_target_pairs={{0,256},{16,272},{32,288},{48,304},{64,320},{80,336},{96,352},{112... | collective-permute-start | bytes 1572872 | tf_op jit(solution)/shard_map/ppermute | solution.py:73
  108.6 14.5 %all-to-all-start = ((f32[4,32,2048]{2,1,0:T(8,128)}), f32[4,32,2048]{2,1,0:T(8,128)S(1)}, u32[]{:S(2)}, u32[]{:S(2)}) async-start(f32[4,32,2048]{2,1,0:T(8,128)} %bitcast.7), calls=%async_computation | async-start | bytes 2097152 | tf_op jit(solution)/shard_map/all_to_all | solution.py:148
  123.9 22.0 %all-to-all-start.1 = ((f32[4,8,2048]{2,1,0:T(8,128)}), f32[4,8,2048]{2,1,0:T(8,128)S(1)}, u32[]{:S(2)}, u32[]{:S(2)}) async-start(f32[4,8,2048]{2,1,0:T(8,128)} %bitcast.8), calls=%async_computation.1 | async-start | bytes 524288 | tf_op jit(solution)/shard_map/all_to_all | solution.py:148
  146.0 8.6 %collective-permute-start.1 = (f32[1024,8]{0,1:T(8,128)S(1)}, f32[1024,8]{0,1:T(8,128)S(1)}, u32[]{:S(2)}, u32[]{:S(2)}) collective-permute-start(f32[1024,8]{0,1:T(8,128)S(1)} %get-tuple-element.14), channel_id=1, source_target_pairs={{0,16},{16,0},{32,48},{48,32},{64,80},{80,64},{96,112},{112,96},{1... | collective-permute-start | bytes 98312 | tf_op jit(solution)/shard_map/ppermute | solution.py:73

commit v3 on v2

--- a/solution.py
+++ b/solution.py
@@ -4,6 +4,7 @@
 import jax.numpy as jnp
 from jax import lax
 from jax.experimental import pallas as pl
+from jax.experimental.pallas import tpu as pltpu
 from jax.sharding import Mesh, PartitionSpec as P
 
 CYC_A = 4
@@ -21,39 +22,36 @@
     return hi, lo
 
 
-def _mm3(a, b):
-    dot = functools.partial(jnp.dot, preferred_element_type=jnp.float32)
-    return dot(a[0], b[0]) + (dot(a[1], b[0]) + dot(a[0], b[1]))
+def _weights(g):
+    hi, lo = _split(0.45 * g)
+    return jnp.concatenate([hi, hi, lo], axis=0)
 
 
-def _layers_kernel(x_ref, g_ref, c_ref, o_ref, *, gate_base, cpl_base, cycles):
+def _apply(x, w):
+    hi, lo = _split(x)
+    lhs = jnp.concatenate([hi, lo, hi], axis=1)
+    return 0.9 * x + jnp.dot(lhs, w, preferred_element_type=jnp.float32)
+
+
+def _layers_kernel(x_ref, g_ref, c_ref, o_ref, t_ref, *, gate_base, cpl_base, cycles):
     rows = x_ref.shape[0]
     n_blocks = rows // BLOCK
-    stride = rows // BLOCK
     o_ref[...] = x_ref[...]
     for turn in range(cycles):
         first = gate_base + 3 * turn
-        top_t = _split((0.45 * g_ref[first]).T)
-        lane_g = _split(0.45 * g_ref[first + 1])
-        mid_t = _split((0.45 * g_ref[first + 2]).T)
         table = c_ref[cpl_base + turn]
-
-        def top(t, carry):
-            rows_t = pl.ds(t, BLOCK, stride=stride)
-            xt = o_ref[rows_t, :]
-            o_ref[rows_t, :] = 0.9 * xt + _mm3(top_t, _split(xt))
-            return carry
-
-        lax.fori_loop(0, stride, top, 0)
-
-        def lane_mid(a, carry):
-            rows_a = pl.ds(pl.multiple_of(a * BLOCK, BLOCK), BLOCK)
-            xa = o_ref[rows_a, :]
-            xa = (0.9 * xa + _mm3(_split(xa), lane_g)) * table
-            o_ref[rows_a, :] = 0.9 * xa + _mm3(mid_t, _split(xa))
-            return carry
-
-        lax.fori_loop(0, n_blocks, lane_mid, 0)
+        for t in range(n_blocks):
+            t_ref[pl.ds(t * BLOCK, BLOCK), :] = o_ref[pl.ds(t, BLOCK, stride=n_blocks), :].T
+        t_ref[...] = _apply(t_ref[...], _weights(g_ref[first]))
+        for t in range(n_blocks):
+            o_ref[pl.ds(t, BLOCK, stride=n_blocks), :] = t_ref[pl.ds(t * BLOCK, BLOCK), :].T
+        y = _apply(o_ref[...], _weights(g_ref[first + 1]))
+        o_ref[...] = (y.reshape(n_blocks, BLOCK, -1) * table[None]).reshape(y.shape)
+        for a in range(n_blocks):
+            t_ref[pl.ds(a * BLOCK, BLOCK), :] = o_ref[pl.ds(a * BLOCK, BLOCK), :].T
+        t_ref[...] = _apply(t_ref[...], _weights(g_ref[first + 2]))
+        for a in range(n_blocks):
+            o_ref[pl.ds(a * BLOCK, BLOCK), :] = t_ref[pl.ds(a * BLOCK, BLOCK), :].T
 
 
 def layers(x, gate_stack, coupling, gate_base, cpl_base, cycles):
@@ -61,6 +59,7 @@
     return pl.pallas_call(
         kernel,
         out_shape=jax.ShapeDtypeStruct(x.shape, x.dtype),
+        scratch_shapes=[pltpu.VMEM(x.shape, jnp.float32)],
     )(x, gate_stack, coupling)
 
 

time: 171 us -> 112 us (0.65)
  Pallas kernels: 81 us -> 22.6 us
    pallas_call x2, Pallas kernels: 81 us -> 22.6 us  [layers(): pl.pallas_call(kernel, out_shape=jax.ShapeDtypeStruct(x.shape, x.dtype),...]
  transfers between devices with their start and end apart: 4 -> 4, of which waited for: 3 -> 3; matrix products, arithmetic and copies ran while one was open for 2% -> 3% of each run, Pallas kernels for 0% -> 0%
where the time goes in v3:
time: 112 us
  starting transfers between devices  36.1 us (32%)
  waiting for transfers between devices  28.4 us (25%)
  Pallas kernels  22.6 us (20%)
  matrix products  10.5 us (9%)
  local copies, waits for them, and re-layouts  10.3 us (9%)
  other arithmetic  3.31 us (3%)
    pallas_call x2, Pallas kernels, layers(): pl.pallas_call(kernel, out_shape=jax.ShapeDtypeStruct(x.shape, x.dtype),...  22.6 us
    all_to_all x2, starting transfers between devices, reduce_columns(): cols = lax.all_to_all(blocks, axis, 0, 0, tiled=False).sum(0)  21.1 us
    ppermute x2, starting transfers between devices, partner(): return lax.ppermute(value, axis, pairs)  14.9 us
    all_to_all x2, waiting for transfers between devices, reduce_columns(): cols = lax.all_to_all(blocks, axis, 0, 0, tiled=False).sum(0)  14.2 us
    ppermute x2, waiting for transfers between devices, partner(): return lax.ppermute(value, axis, pairs)  14.1 us
    unnamed x5, matrix products  5.3 us
    dot_general x5, matrix products, final_group_cols(): jnp.dot(cols.reshape(-1, order_size), mid_mat, precision=HIGHEST_PREC)  5.25 us
    mul x25, local copies, waits for them, and re-layouts, final_group_cols(): cols = (shaped * table.T[:, None, :]).reshape(cols.shape)  3.82 us
  transfers between devices with their start and end apart: 4, of which 3 were waited for; matrix products, arithmetic and copies ran while one was open for 3% of the time, Pallas kernels for 0%

profile of v3, /device:TPU:1, one launch (start us, length us, event | category | flops | bytes accessed | tf_op | source)
XLA Modules:
  0.0 111.5 jit_solution(17126853991962165721)
XLA Ops:
  0.0 11.3 %shard_map.37 = f32[2048,128]{1,0:T(8,128)} custom-call(f32[2048,128]{1,0:T(8,128)} %bitcast.94, f32[34,128,128]{2,1,0:T(8,128)} %g_ref.3, f32[13,128,128]{2,1,0:T(8,128)} %c_ref.3), custom_call_target="tpu_custom_call" | custom-call | tf_op jit(solution)/shard_map/pallas_call | solution.py:59
  11.3 1.3 %fusion.111 = (f32[1024,128]{1,0:T(8,128)S(1)}, f32[1024,128]{1,0:T(8,128)S(1)}, f32[1024,128]{1,0:T(8,128)S(1)}) fusion(f32[2048,128]{1,0:T(8,128)} %shard_map.37, pred[]{:T(512)S(6)} %eq.56), kind=kLoop, calls=%fused_computation.121 | loop fusion | flops 131072 | bytes 2621441 | tf_op jit(solution)/shard_map/slice | solution.py:133
  12.6 8.5 %collective-permute-start = (f32[1024,128]{1,0:T(8,128)S(1)}, f32[1024,128]{1,0:T(8,128)S(1)}, u32[]{:S(2)}, u32[]{:S(2)}) collective-permute-start(f32[1024,128]{1,0:T(8,128)S(1)} %get-tuple-element.6), channel_id=1, source_target_pairs={{0,256},{16,272},{32,288},{48,304},{64,320},{80,336},{96,352},{112... | collective-permute-start | bytes 1572872 | tf_op jit(solution)/shard_map/ppermute | solution.py:72
  21.1 14.1 %collective-permute-done = f32[1024,128]{1,0:T(8,128)S(1)} collective-permute-done((f32[1024,128]{1,0:T(8,128)S(1)}, f32[1024,128]{1,0:T(8,128)S(1)}, u32[]{:S(2)}, u32[]{:S(2)}) %collective-permute-start) | collective-permute-done | bytes 524320 | tf_op jit(solution)/shard_map/ppermute | solution.py:72
  35.2 1.1 %maximum_select_fusion.x_ref = f32[2048,128]{1,0:T(8,128)} fusion(f32[1024,128]{1,0:T(8,128)S(1)} %collective-permute-done, f32[1024,128]{1,0:T(8,128)S(1)} %get-tuple-element.7, f32[1024,128]{1,0:T(8,128)S(1)} %get-tuple-element.5, pred[]{:T(512)S(6)} %eq.56), kind=kLoop, calls=%fused_computation | loop fusion | flops 786432 | bytes 2621441 | tf_op jit(solution)/shard_map/jit(_where)/select_n | solution.py:137
  36.3 11.3 %shard_map.38 = f32[2048,128]{1,0:T(8,128)} custom-call(f32[2048,128]{1,0:T(8,128)} %maximum_select_fusion.x_ref, f32[34,128,128]{2,1,0:T(8,128)} %g_ref.3, f32[13,128,128]{2,1,0:T(8,128)} %c_ref.3), custom_call_target="tpu_custom_call" | custom-call | tf_op jit(solution)/shard_map/pallas_call | solution.py:59
  47.6 2.6 %copy.29 = f32[128,2048]{1,0:T(8,128)} copy(f32[128,2048]{0,1:T(8,128)} %bitcast.93) | data formatting | bytes 2097152 | tf_op jit(solution)/shard_map/transpose | solution.py:143
  50.2 4.7 %all-to-all-start = ((f32[4,32,2048]{2,1,0:T(8,128)}), f32[4,32,2048]{2,1,0:T(8,128)S(1)}, u32[]{:S(2)}, u32[]{:S(2)}) async-start(f32[4,32,2048]{2,1,0:T(8,128)} %bitcast.7), calls=%async_computation | async-start | bytes 2097152 | tf_op jit(solution)/shard_map/all_to_all | solution.py:147
  55.0 9.7 %all-to-all-done = f32[4,32,2048]{2,1,0:T(8,128)S(1)} async-done(((f32[4,32,2048]{2,1,0:T(8,128)}), f32[4,32,2048]{2,1,0:T(8,128)S(1)}, u32[]{:S(2)}, u32[]{:S(2)}) %all-to-all-start) | async-done | bytes 1048608 | tf_op jit(solution)/shard_map/all_to_all | solution.py:147
  64.7 0.8 reduce_sum.18
  65.5 16.4 %all-to-all-start.1 = ((f32[4,8,2048]{2,1,0:T(8,128)}), f32[4,8,2048]{2,1,0:T(8,128)S(1)}, u32[]{:S(2)}, u32[]{:S(2)}) async-start(f32[4,8,2048]{2,1,0:T(8,128)} %bitcast.8), calls=%async_computation.1 | async-start | bytes 524288 | tf_op jit(solution)/shard_map/all_to_all | solution.py:147
  81.9 1.0 fusion.112
  82.9 0.1 constant_dynamic-slice_fusion.2
  83.0 0.1 constant_dynamic-slice_fusion
  83.1 4.5 %all-to-all-done.1 = f32[4,8,2048]{2,1,0:T(8,128)S(1)} async-done(((f32[4,8,2048]{2,1,0:T(8,128)}), f32[4,8,2048]{2,1,0:T(8,128)S(1)}, u32[]{:S(2)}, u32[]{:S(2)}) %all-to-all-start.1) | async-done | bytes 262176 | tf_op jit(solution)/shard_map/all_to_all | solution.py:147
  87.6 6.5 %collective-permute-start.1 = (f32[1024,8]{0,1:T(8,128)S(1)}, f32[1024,8]{0,1:T(8,128)S(1)}, u32[]{:S(2)}, u32[]{:S(2)}) collective-permute-start(f32[1024,8]{0,1:T(8,128)S(1)} %get-tuple-element.14), channel_id=1, source_target_pairs={{0,16},{16,0},{32,48},{48,32},{64,80},{80,64},{96,112},{112,96},{1... | collective-permute-start | bytes 98312 | tf_op jit(solution)/shard_map/ppermute | solution.py:72
  94.1 0.1 constant_dynamic-slice_fusion.4
  94.1 0.1 copy.51
  94.2 0.2 mul.165
  94.4 0.2 copy.32
  94.6 0.1 copy.53
  94.7 0.2 mul.170
  94.9 0.2 copy.36
  95.0 0.1 copy.55
  95.1 0.2 mul.175
  95.3 0.2 copy.40
  95.5 0.1 copy.57
  95.5 0.2 mul.180
  95.8 0.2 copy.44
  95.9 0.1 copy.59
  96.0 0.2 mul.185
  96.2 0.2 copy.48
  96.4 0.0 collective-permute-done.1
  96.4 0.2 reshape.86
  96.6 0.2 copy.30
  96.8 1.1 fusion.13
  97.9 0.2 copy.33
  98.1 0.2 mul.167
  98.3 1.0 fusion.16
  99.3 0.2 reshape_reshape.8
  99.5 0.2 copy.34
  99.7 1.1 fusion.10
  100.7 0.2 copy.37
  100.9 0.2 mul.172
  101.1 1.0 fusion.19
  102.2 0.2 reshape_reshape.9
  102.4 0.2 copy.38
  102.6 1.1 fusion.7
  103.6 0.2 copy.41
  103.8 0.2 mul.177
  104.0 1.0 fusion.22
  105.1 0.2 reshape_reshape.10
  105.3 0.2 copy.42
  105.5 1.1 fusion.4
  106.5 0.2 copy.45
  106.7 0.2 mul.182
  106.9 1.0 fusion.25
  108.0 0.2 reshape_reshape.11
  108.2 0.2 copy.46
  108.3 1.1 fusion.1
  109.4 0.2 copy.49
  109.6 0.2 mul.187
  109.8 1.0 fusion.28
  110.9 0.6 reshape.87
  (13 shorter events, 0.1 us)
Async XLA Ops:
  12.6 22.6 %collective-permute-start = (f32[1024,128]{1,0:T(8,128)S(1)}, f32[1024,128]{1,0:T(8,128)S(1)}, u32[]{:S(2)}, u32[]{:S(2)}) collective-permute-start(f32[1024,128]{1,0:T(8,128)S(1)} %get-tuple-element.6), channel_id=1, source_target_pairs={{0,256},{16,272},{32,288},{48,304},{64,320},{80,336},{96,352},{112... | collective-permute-start | bytes 1572872 | tf_op jit(solution)/shard_map/ppermute | solution.py:72
  50.2 14.5 %all-to-all-start = ((f32[4,32,2048]{2,1,0:T(8,128)}), f32[4,32,2048]{2,1,0:T(8,128)S(1)}, u32[]{:S(2)}, u32[]{:S(2)}) async-start(f32[4,32,2048]{2,1,0:T(8,128)} %bitcast.7), calls=%async_computation | async-start | bytes 2097152 | tf_op jit(solution)/shard_map/all_to_all | solution.py:147
  65.5 22.1 %all-to-all-start.1 = ((f32[4,8,2048]{2,1,0:T(8,128)}), f32[4,8,2048]{2,1,0:T(8,128)S(1)}, u32[]{:S(2)}, u32[]{:S(2)}) async-start(f32[4,8,2048]{2,1,0:T(8,128)} %bitcast.8), calls=%async_computation.1 | async-start | bytes 524288 | tf_op jit(solution)/shard_map/all_to_all | solution.py:147
  87.6 8.8 %collective-permute-start.1 = (f32[1024,8]{0,1:T(8,128)S(1)}, f32[1024,8]{0,1:T(8,128)S(1)}, u32[]{:S(2)}, u32[]{:S(2)}) collective-permute-start(f32[1024,8]{0,1:T(8,128)S(1)} %get-tuple-element.14), channel_id=1, source_target_pairs={{0,16},{16,0},{32,48},{48,32},{64,80},{80,64},{96,112},{112,96},{1... | collective-permute-start | bytes 98312 | tf_op jit(solution)/shard_map/ppermute | solution.py:72

commit v4 on v3

--- a/solution.py
+++ b/solution.py
@@ -61,6 +61,35 @@
         out_shape=jax.ShapeDtypeStruct(x.shape, x.dtype),
         scratch_shapes=[pltpu.VMEM(x.shape, jnp.float32)],
     )(x, gate_stack, coupling)
+
+
+def _final_kernel(d_ref, g_ref, tab_ref, o_ref, m_ref, *, gate_base, cycles):
+    width = d_ref.shape[0]
+    n_blocks = d_ref.shape[1] // BLOCK
+    for a in range(n_blocks):
+        o_ref[pl.ds(a * BLOCK, BLOCK), :] = d_ref[:, pl.ds(a * BLOCK, BLOCK)].T
+    for turn in range(cycles):
+        for t in range(n_blocks):
+            m_ref[pl.ds(t * width, width), :] = o_ref[pl.ds(t, BLOCK, stride=n_blocks), :].T
+        m_ref[...] = _apply(m_ref[...], _weights(g_ref[gate_base + 2 * turn]))
+        for t in range(n_blocks):
+            o_ref[pl.ds(t, BLOCK, stride=n_blocks), :] = m_ref[pl.ds(t * width, width), :].T
+        table = tab_ref[turn]
+        for a in range(n_blocks):
+            m_ref[pl.ds(a * width, width), :] = o_ref[pl.ds(a * BLOCK, BLOCK), :].T * table
+        m_ref[...] = _apply(m_ref[...], _weights(g_ref[gate_base + 2 * turn + 1]))
+        for a in range(n_blocks):
+            o_ref[pl.ds(a * BLOCK, BLOCK), :] = m_ref[pl.ds(a * width, width), :].T
+
+
+def final_layers(d, gate_stack, tables, gate_base, cycles):
+    width, rows = d.shape
+    kernel = functools.partial(_final_kernel, gate_base=gate_base, cycles=cycles)
+    return pl.pallas_call(
+        kernel,
+        out_shape=jax.ShapeDtypeStruct((rows, width), d.dtype),
+        scratch_shapes=[pltpu.VMEM((BLOCK, BLOCK), jnp.float32)],
+    )(d, gate_stack, tables)
 
 
 HIGHEST_PREC = lax.Precision.HIGHEST
@@ -156,9 +185,11 @@
     tensor = layers(tensor, gate_stack, coupling, 3 * CYC_A, CYC_A, CYC_B)
     cols = reduce_columns(tensor)
     cols = swap_bit(cols.T, 0).T
-    col_start = lax.axis_index(CUTS) * cols.shape[0]
-    cols = final_group_cols(cols, gate_stack, coupling, col_start)
-    return cols.T
+    width = cols.shape[0]
+    col_start = lax.axis_index(CUTS) * width
+    cpl_base = CYC_A + CYC_B
+    tables = lax.dynamic_slice_in_dim(coupling[cpl_base:cpl_base + CYC_C], col_start, width, axis=2)
+    return final_layers(cols, gate_stack, jnp.swapaxes(tables, 1, 2), 3 * CYC_A + 3 * CYC_B, CYC_C)
 
 
 def solution(mesh):

time: 112 us -> 106 us (0.946)
  blocking collectives: 0 us -> 14.4 us
  matrix products: 10.5 us -> 0 us
  Pallas kernels: 22.6 us -> 32 us
  waiting for transfers between devices: 28.4 us -> 19.8 us
  local copies, waits for them, and re-layouts: 10.3 us -> 4.61 us
  starting transfers between devices: 36.1 us -> 31.3 us
    all_to_all x0 -> x1, blocking collectives: none -> 14.4 us  [reduce_columns(): cols = lax.all_to_all(blocks, axis, 0, 0, tiled=False).sum(0)]
    pallas_call x0 -> x1, Pallas kernels: none -> 9.35 us  [final_layers(): pl.pallas_call(kernel, out_shape=jax.ShapeDtypeStruct((rows, width), d.dt...]
    all_to_all x2 -> x1, waiting for transfers between devices: 14.2 us -> 5.67 us  [reduce_columns(): cols = lax.all_to_all(blocks, axis, 0, 0, tiled=False).sum(0)]
    unnamed x5 -> x0, matrix products: 5.3 us -> none
    dot_general x5 -> x0, matrix products: 5.25 us -> none  [final_group_cols(): jnp.dot(cols.reshape(-1, order_size), mid_mat, precision=HIGHEST_PREC)]
    all_to_all x2 -> x1, starting transfers between devices: 21.1 us -> 16.4 us  [reduce_columns(): cols = lax.all_to_all(blocks, axis, 0, 0, tiled=False).sum(0)]
    mul x25 -> x0, local copies, waits for them, and re-layouts: 3.82 us -> none  [final_group_cols(): cols = (shaped * table.T[:, None, :]).reshape(cols.shape)]
    pallas_call x0 -> x1, local copies, waits for them, and re-layouts: none -> 2.16 us  [final_layers(): pl.pallas_call(kernel, out_shape=jax.ShapeDtypeStruct((rows, width), d.dt...]
  transfers between devices with their start and end apart: 4 -> 3, of which waited for: 3 -> 2; matrix products, arithmetic and copies ran while one was open for 3% -> 1% of each run, Pallas kernels for 0% -> 0%
where the time goes in v4:
time: 106 us
  Pallas kernels  32 us (30%)
  starting transfers between devices  31.3 us (30%)
  waiting for transfers between devices  19.8 us (19%)
  blocking collectives  14.4 us (14%)
  local copies, waits for them, and re-layouts  4.61 us (4%)
  other arithmetic  3.81 us (4%)
    pallas_call x2, Pallas kernels, layers(): pl.pallas_call(kernel, out_shape=jax.ShapeDtypeStruct(x.shape, x.dtype),...  22.6 us
    all_to_all x1, starting transfers between devices, reduce_columns(): cols = lax.all_to_all(blocks, axis, 0, 0, tiled=False).sum(0)  16.4 us
    ppermute x2, starting transfers between devices, partner(): return lax.ppermute(value, axis, pairs)  14.9 us
    all_to_all x1, blocking collectives, reduce_columns(): cols = lax.all_to_all(blocks, axis, 0, 0, tiled=False).sum(0)  14.4 us
    ppermute x2, waiting for transfers between devices, partner(): return lax.ppermute(value, axis, pairs)  14.1 us
    pallas_call x1, Pallas kernels, final_layers(): pl.pallas_call(kernel, out_shape=jax.ShapeDtypeStruct((rows, width), d.dt...  9.35 us
    all_to_all x1, waiting for transfers between devices, reduce_columns(): cols = lax.all_to_all(blocks, axis, 0, 0, tiled=False).sum(0)  5.67 us
    pallas_call x1, local copies, waits for them, and re-layouts, final_layers(): pl.pallas_call(kernel, out_shape=jax.ShapeDtypeStruct((rows, width), d.dt...  2.16 us
  transfers between devices with their start and end apart: 3, of which 2 were waited for; matrix products, arithmetic and copies ran while one was open for 1% of the time, Pallas kernels for 0%

profile of v4, /device:TPU:1, one launch (start us, length us, event | category | flops | bytes accessed | tf_op | source)
XLA Modules:
  0.0 106.0 jit_solution(15793153240789611665)
XLA Ops:
  0.0 11.3 %shard_map.37 = f32[2048,128]{1,0:T(8,128)} custom-call(f32[2048,128]{1,0:T(8,128)} %bitcast.10, f32[34,128,128]{2,1,0:T(8,128)} %g_ref.5, f32[13,128,128]{2,1,0:T(8,128)} %c_ref.3), custom_call_target="tpu_custom_call" | custom-call | tf_op jit(solution)/shard_map/pallas_call | solution.py:59
  11.3 1.3 %fusion.1 = (f32[1024,128]{1,0:T(8,128)S(1)}, f32[1024,128]{1,0:T(8,128)S(1)}, f32[1024,128]{1,0:T(8,128)S(1)}) fusion(f32[2048,128]{1,0:T(8,128)} %shard_map.37, pred[]{:T(512)S(6)} %eq.9), kind=kLoop, calls=%fused_computation.6 | loop fusion | flops 131072 | bytes 2621441 | tf_op jit(solution)/shard_map/slice | solution.py:162
  12.6 8.5 %collective-permute-start = (f32[1024,128]{1,0:T(8,128)S(1)}, f32[1024,128]{1,0:T(8,128)S(1)}, u32[]{:S(2)}, u32[]{:S(2)}) collective-permute-start(f32[1024,128]{1,0:T(8,128)S(1)} %get-tuple-element.6), channel_id=1, source_target_pairs={{0,256},{16,272},{32,288},{48,304},{64,320},{80,336},{96,352},{112... | collective-permute-start | bytes 1572872 | tf_op jit(solution)/shard_map/ppermute | solution.py:101
  21.1 14.1 %collective-permute-done = f32[1024,128]{1,0:T(8,128)S(1)} collective-permute-done((f32[1024,128]{1,0:T(8,128)S(1)}, f32[1024,128]{1,0:T(8,128)S(1)}, u32[]{:S(2)}, u32[]{:S(2)}) %collective-permute-start) | collective-permute-done | bytes 524320 | tf_op jit(solution)/shard_map/ppermute | solution.py:101
  35.2 1.1 %maximum_select_fusion.x_ref = f32[2048,128]{1,0:T(8,128)} fusion(f32[1024,128]{1,0:T(8,128)S(1)} %collective-permute-done, f32[1024,128]{1,0:T(8,128)S(1)} %get-tuple-element.7, f32[1024,128]{1,0:T(8,128)S(1)} %get-tuple-element.5, pred[]{:T(512)S(6)} %eq.9), kind=kLoop, calls=%fused_computation | loop fusion | flops 786432 | bytes 2621441 | tf_op jit(solution)/shard_map/jit(_where)/select_n | solution.py:166
  36.3 11.3 %shard_map.38 = f32[2048,128]{1,0:T(8,128)} custom-call(f32[2048,128]{1,0:T(8,128)} %maximum_select_fusion.x_ref, f32[34,128,128]{2,1,0:T(8,128)} %g_ref.5, f32[13,128,128]{2,1,0:T(8,128)} %c_ref.3), custom_call_target="tpu_custom_call" | custom-call | tf_op jit(solution)/shard_map/pallas_call | solution.py:59
  47.6 1.6 %copy.9 = f32[128,2048]{1,0:T(8,128)S(1)} copy(f32[128,2048]{0,1:T(8,128)} %bitcast.8) | data formatting | bytes 2097152 | tf_op jit(solution)/shard_map/transpose | solution.py:172
  49.2 0.0 slice-start
  49.2 14.4 %all_to_all.10 = f32[4,32,2048]{2,1,0:T(8,128)S(1)} all-to-all(f32[4,32,2048]{2,1,0:T(8,128)S(1)} %bitcast.9), channel_id=1, replica_groups=mesh['yh'=2,'z'=8,'core'=2,'x'=4,'yl'=4] {'x'}, dimensions={0} | all-to-all | bytes 2097152 | tf_op jit(solution)/shard_map/all_to_all | solution.py:176
  63.6 0.8 reduce_sum.18
  64.4 16.4 %all-to-all-start.1 = ((f32[4,8,2048]{2,1,0:T(8,128)}), f32[4,8,2048]{2,1,0:T(8,128)S(1)}, u32[]{:S(2)}, u32[]{:S(2)}) async-start(f32[4,8,2048]{2,1,0:T(8,128)} %bitcast.3), calls=%async_computation.1 | async-start | bytes 524288 | tf_op jit(solution)/shard_map/all_to_all | solution.py:176
  80.8 5.7 %all-to-all-done.1 = f32[4,8,2048]{2,1,0:T(8,128)S(1)} async-done(((f32[4,8,2048]{2,1,0:T(8,128)}), f32[4,8,2048]{2,1,0:T(8,128)S(1)}, u32[]{:S(2)}, u32[]{:S(2)}) %all-to-all-start.1) | async-done | bytes 262176 | tf_op jit(solution)/shard_map/all_to_all | solution.py:176
  86.5 6.5 %collective-permute-start.1 = (f32[1024,8]{0,1:T(8,128)S(1)}, f32[1024,8]{0,1:T(8,128)S(1)}, u32[]{:S(2)}, u32[]{:S(2)}) collective-permute-start(f32[1024,8]{0,1:T(8,128)S(1)} %get-tuple-element.9), channel_id=1, source_target_pairs={{0,16},{16,0},{32,48},{48,32},{64,80},{80,64},{96,112},{112,96},{1... | collective-permute-start | bytes 98312 | tf_op jit(solution)/shard_map/ppermute | solution.py:101
  93.0 0.0 slice-done
  93.0 0.1 constant_dynamic-slice_fusion
  93.1 0.7 copy.13
  93.9 0.0 collective-permute-done.1
  93.9 0.6 fusion.d_ref
  94.5 9.4 %shard_map.39 = f32[2048,8]{1,0:T(8,128)} custom-call(f32[8,2048]{1,0:T(8,128)} %fusion.d_ref, f32[34,128,128]{2,1,0:T(8,128)} %g_ref.5, f32[5,8,128]{2,1,0:T(8,128)} %bitcast.12), custom_call_target="tpu_custom_call" | custom-call | tf_op jit(solution)/shard_map/pallas_call | solution.py:88
  103.9 2.2 %copy.11 = f32[2048,8]{0,1:T(8,128)} copy(f32[2048,8]{1,0:T(8,128)} %shard_map.39) | data formatting | bytes 131072 | tf_op jit(solution)/shard_map/pallas_call | solution.py:88
  (2 shorter events, 0.0 us)
Async XLA Ops:
  12.6 22.6 %collective-permute-start = (f32[1024,128]{1,0:T(8,128)S(1)}, f32[1024,128]{1,0:T(8,128)S(1)}, u32[]{:S(2)}, u32[]{:S(2)}) collective-permute-start(f32[1024,128]{1,0:T(8,128)S(1)} %get-tuple-element.6), channel_id=1, source_target_pairs={{0,256},{16,272},{32,288},{48,304},{64,320},{80,336},{96,352},{112... | collective-permute-start | bytes 1572872 | tf_op jit(solution)/shard_map/ppermute | solution.py:101
  49.2 43.8 %slice-start = ((f32[13,128,128]{2,1,0:T(8,128)}), f32[5,128,128]{2,1,0:T(8,128)S(1)}, s32[]{:S(2)}) async-start(f32[13,128,128]{2,1,0:T(8,128)} %c_ref.3), calls=%async_computation.2 | async-start | bytes 655360 | tf_op jit(solution)/shard_map/slice | solution.py:191
  64.4 22.0 %all-to-all-start.1 = ((f32[4,8,2048]{2,1,0:T(8,128)}), f32[4,8,2048]{2,1,0:T(8,128)S(1)}, u32[]{:S(2)}, u32[]{:S(2)}) async-start(f32[4,8,2048]{2,1,0:T(8,128)} %bitcast.3), calls=%async_computation.1 | async-start | bytes 524288 | tf_op jit(solution)/shard_map/all_to_all | solution.py:176
  86.5 7.4 %collective-permute-start.1 = (f32[1024,8]{0,1:T(8,128)S(1)}, f32[1024,8]{0,1:T(8,128)S(1)}, u32[]{:S(2)}, u32[]{:S(2)}) collective-permute-start(f32[1024,8]{0,1:T(8,128)S(1)} %get-tuple-element.9), channel_id=1, source_target_pairs={{0,16},{16,0},{32,48},{48,32},{64,80},{80,64},{96,112},{112,96},{1... | collective-permute-start | bytes 98312 | tf_op jit(solution)/shard_map/ppermute | solution.py:101

commit v5 on v4

--- a/solution.py
+++ b/solution.py
@@ -33,10 +33,9 @@
     return 0.9 * x + jnp.dot(lhs, w, preferred_element_type=jnp.float32)
 
 
-def _layers_kernel(x_ref, g_ref, c_ref, o_ref, t_ref, *, gate_base, cpl_base, cycles):
-    rows = x_ref.shape[0]
+def _layer_turns(o_ref, t_ref, g_ref, c_ref, gate_base, cpl_base, cycles, last_to=None):
+    rows = o_ref.shape[0]
     n_blocks = rows // BLOCK
-    o_ref[...] = x_ref[...]
     for turn in range(cycles):
         first = gate_base + 3 * turn
         table = c_ref[cpl_base + turn]
@@ -50,17 +49,60 @@
         for a in range(n_blocks):
             t_ref[pl.ds(a * BLOCK, BLOCK), :] = o_ref[pl.ds(a * BLOCK, BLOCK), :].T
         t_ref[...] = _apply(t_ref[...], _weights(g_ref[first + 2]))
-        for a in range(n_blocks):
-            o_ref[pl.ds(a * BLOCK, BLOCK), :] = t_ref[pl.ds(a * BLOCK, BLOCK), :].T
-
-
-def layers(x, gate_stack, coupling, gate_base, cpl_base, cycles):
-    kernel = functools.partial(_layers_kernel, gate_base=gate_base, cpl_base=cpl_base, cycles=cycles)
+        if last_to is not None and turn == cycles - 1:
+            for a in range(n_blocks):
+                last_to[:, pl.ds(a * BLOCK, BLOCK)] = t_ref[pl.ds(a * BLOCK, BLOCK), :]
+        else:
+            for a in range(n_blocks):
+                o_ref[pl.ds(a * BLOCK, BLOCK), :] = t_ref[pl.ds(a * BLOCK, BLOCK), :].T
+
+
+def _group_a_kernel(p_ref, x_ref, g_ref, c_ref, keep_ref, send_ref, o_ref, t_ref, *, cycles):
+    half = keep_ref.shape[0]
+    o_ref[...] = x_ref[...]
+    _layer_turns(o_ref, t_ref, g_ref, c_ref, 0, 0, cycles)
+    p = p_ref[0]
+    keep_ref[...] = o_ref[pl.ds(pl.multiple_of(p * half, half), half), :]
+    send_ref[...] = o_ref[pl.ds(pl.multiple_of((1 - p) * half, half), half), :]
+
+
+def _group_b_kernel(p_ref, keep_ref, recv_ref, g_ref, c_ref, out_ref, o_ref, t_ref, *, gate_base, cpl_base, cycles):
+    half = keep_ref.shape[0]
+    p = p_ref[0]
+    o_ref[pl.ds(pl.multiple_of(p * half, half), half), :] = keep_ref[...]
+    o_ref[pl.ds(pl.multiple_of((1 - p) * half, half), half), :] = recv_ref[...]
+    _layer_turns(o_ref, t_ref, g_ref, c_ref, gate_base, cpl_base, cycles, last_to=out_ref)
+
+
+def _smem():
+    return pl.BlockSpec(memory_space=pltpu.SMEM)
+
+
+def _vmem():
+    return pl.BlockSpec(memory_space=pltpu.VMEM)
+
+
+def group_a(parity, x, gate_stack, coupling, cycles):
+    half = jax.ShapeDtypeStruct((x.shape[0] // 2, x.shape[1]), x.dtype)
+    return pl.pallas_call(
+        functools.partial(_group_a_kernel, cycles=cycles),
+        out_shape=(half, half),
+        in_specs=[_smem(), _vmem(), _vmem(), _vmem()],
+        out_specs=(_vmem(), _vmem()),
+        scratch_shapes=[pltpu.VMEM(x.shape, jnp.float32), pltpu.VMEM(x.shape, jnp.float32)],
+    )(parity, x, gate_stack, coupling)
+
+
+def group_b(parity, keep, recv, gate_stack, coupling, gate_base, cpl_base, cycles):
+    rows, cols = keep.shape[0] * 2, keep.shape[1]
+    kernel = functools.partial(_group_b_kernel, gate_base=gate_base, cpl_base=cpl_base, cycles=cycles)
     return pl.pallas_call(
         kernel,
-        out_shape=jax.ShapeDtypeStruct(x.shape, x.dtype),
-        scratch_shapes=[pltpu.VMEM(x.shape, jnp.float32)],
-    )(x, gate_stack, coupling)
+        out_shape=jax.ShapeDtypeStruct((cols, rows), keep.dtype),
+        in_specs=[_smem(), _vmem(), _vmem(), _vmem(), _vmem()],
+        out_specs=_vmem(),
+        scratch_shapes=[pltpu.VMEM((rows, cols), jnp.float32), pltpu.VMEM((rows, cols), jnp.float32)],
+    )(parity, keep, recv, gate_stack, coupling)
 
 
 def _final_kernel(d_ref, g_ref, tab_ref, o_ref, m_ref, *, gate_base, cycles):
@@ -168,8 +210,7 @@
     )
 
 
-def reduce_columns(tensor):
-    cols = tensor.T
+def reduce_columns(cols):
     for axis in ("x", "yl"):
         n = lax.axis_size(axis)
         blocks = cols.reshape(n, cols.shape[0] // n, cols.shape[1])
@@ -177,14 +218,25 @@
     return cols
 
 
+def swap_lanes(cols, bit_pos):
+    half = cols.shape[1] // 2
+    lower = cols[:, :half]
+    upper = cols[:, half:]
+    parity = lax.axis_index(BITS) >> bit_pos & 1
+    outgoing = jnp.where(parity == 0, upper, lower)
+    incoming = partner(outgoing, BITS, bit_pos)
+    return jnp.where(
+        parity == 0, jnp.concatenate([lower, incoming], 1), jnp.concatenate([incoming, upper], 1)
+    )
+
+
 def on_device(boundary, gate_stack, coupling):
-    tensor = boundary[0]
     top_bit = lax.axis_size(BITS).bit_length() - 2
-    tensor = layers(tensor, gate_stack, coupling, 0, 0, CYC_A)
-    tensor = swap_bit(tensor, top_bit)
-    tensor = layers(tensor, gate_stack, coupling, 3 * CYC_A, CYC_A, CYC_B)
-    cols = reduce_columns(tensor)
-    cols = swap_bit(cols.T, 0).T
+    parity = (lax.axis_index(BITS) >> top_bit & 1).astype(jnp.int32).reshape(1)
+    keep, send = group_a(parity, boundary[0], gate_stack, coupling, CYC_A)
+    recv = partner(send, BITS, top_bit)
+    cols = group_b(parity, keep, recv, gate_stack, coupling, 3 * CYC_A, CYC_A, CYC_B)
+    cols = swap_lanes(reduce_columns(cols), 0)
     width = cols.shape[0]
     col_start = lax.axis_index(CUTS) * width
     cpl_base = CYC_A + CYC_B

time: 106 us -> 104 us (0.981)
  other arithmetic: 3.81 us -> 1.42 us
    transpose x1 -> x0, local copies, waits for them, and re-layouts: 1.55 us -> none  [reduce_columns(): cols = tensor.T]
    slice x2 -> x1, other arithmetic: 1.31 us -> 0.01 us  [swap_lanes(): upper = cols[:, half:]]
where the time goes in v5:
time: 104 us; the launch traced here: 103 us
  Pallas kernels  31.9 us (31%)
  starting transfers between devices  31.3 us (30%)
  waiting for transfers between devices  20.1 us (19%)
  blocking collectives  14.5 us (14%)
  local copies, waits for them, and re-layouts  3.84 us (4%)
  other arithmetic  1.42 us (1%)
    all_to_all x1, starting transfers between devices, reduce_columns(): cols = lax.all_to_all(blocks, axis, 0, 0, tiled=False).sum(0)  16.4 us
    ppermute x2, starting transfers between devices, partner(): return lax.ppermute(value, axis, pairs)  14.9 us
    all_to_all x1, blocking collectives, reduce_columns(): cols = lax.all_to_all(blocks, axis, 0, 0, tiled=False).sum(0)  14.5 us
    ppermute x2, waiting for transfers between devices, partner(): return lax.ppermute(value, axis, pairs)  14.4 us
    pallas_call x1, Pallas kernels, group_a(): pl.pallas_call(functools.partial(_group_a_kernel, cycles=cycles), out_sha...  11.3 us
    pallas_call x1, Pallas kernels, group_b(): pl.pallas_call(kernel, out_shape=jax.ShapeDtypeStruct((cols, rows), keep....  11.2 us
    pallas_call x1, Pallas kernels, final_layers(): pl.pallas_call(kernel, out_shape=jax.ShapeDtypeStruct((rows, width), d.dt...  9.35 us
    all_to_all x1, waiting for transfers between devices, reduce_columns(): cols = lax.all_to_all(blocks, axis, 0, 0, tiled=False).sum(0)  5.67 us
  transfers between devices with their start and end apart: 3, of which 2 were waited for; matrix products, arithmetic and copies ran while one was open for 1% of the time, Pallas kernels for 0%

profile of v5, /device:TPU:1, one launch (start us, length us, event | category | flops | bytes accessed | tf_op | source)
XLA Modules:
  0.0 103.1 jit_solution(15060831651572218983)
XLA Ops:
  0.0 11.3 %shard_map.37 = (f32[1024,128]{1,0:T(8,128)}, f32[1024,128]{1,0:T(8,128)}) custom-call(s32[1]{0:T(128)} %bitcast.p_ref, f32[2048,128]{1,0:T(8,128)} %bitcast.6, f32[34,128,128]{2,1,0:T(8,128)} %g_ref.5, f32[13,128,128]{2,1,0:T(8,128)} %c_ref.3), custom_call_target="tpu_custom_call" | custom-call | tf_op jit(solution)/shard_map/pallas_call | solution.py:87
  11.3 8.4 %collective-permute-start = (f32[1024,128]{1,0:T(8,128)}, f32[1024,128]{1,0:T(8,128)S(1)}, u32[]{:S(2)}, u32[]{:S(2)}) collective-permute-start(f32[1024,128]{1,0:T(8,128)} %get-tuple-element.8), channel_id=1, source_target_pairs={{0,256},{16,272},{32,288},{48,304},{64,320},{80,336},{96,352},{112... | collective-permute-start | bytes 1572872 | tf_op jit(solution)/shard_map/ppermute | solution.py:143
  19.8 14.4 %collective-permute-done.recv_ref = f32[1024,128]{1,0:T(8,128)S(1)} collective-permute-done((f32[1024,128]{1,0:T(8,128)}, f32[1024,128]{1,0:T(8,128)S(1)}, u32[]{:S(2)}, u32[]{:S(2)}) %collective-permute-start) | collective-permute-done | bytes 524320 | tf_op jit(solution)/shard_map/ppermute | solution.py:143
  34.2 0.0 copy-start
  34.2 0.8 copy-done
  35.0 11.2 %shard_map.38 = f32[128,2048]{1,0:T(8,128)} custom-call(s32[1]{0:T(128)} %bitcast.p_ref, f32[1024,128]{1,0:T(8,128)} %get-tuple-element.7.keep_ref, f32[1024,128]{1,0:T(8,128)} %copy-done, f32[34,128,128]{2,1,0:T(8,128)} %g_ref.5, f32[13,128,128]{2,1,0:T(8,128)} %c_ref.3), custom_call_target="tpu_custom_call" | custom-call | tf_op jit(solution)/shard_map/pallas_call | solution.py:99
  46.2 0.0 slice-start
  46.2 14.5 %all_to_all.10 = f32[4,32,2048]{2,1,0:T(8,128)S(1)} all-to-all(f32[4,32,2048]{2,1,0:T(8,128)} %bitcast.5), channel_id=1, replica_groups=mesh['yh'=2,'z'=8,'core'=2,'x'=4,'yl'=4] {'x'}, dimensions={0} | all-to-all | bytes 2097152 | tf_op jit(solution)/shard_map/all_to_all | solution.py:217
  60.8 0.8 reduce_sum.18
  61.5 16.4 %all-to-all-start.1 = ((f32[4,8,2048]{2,1,0:T(8,128)}), f32[4,8,2048]{2,1,0:T(8,128)S(1)}, u32[]{:S(2)}, u32[]{:S(2)}) async-start(f32[4,8,2048]{2,1,0:T(8,128)} %bitcast.3), calls=%async_computation.1 | async-start | bytes 524288 | tf_op jit(solution)/shard_map/all_to_all | solution.py:217
  77.9 5.7 %all-to-all-done.1 = f32[4,8,2048]{2,1,0:T(8,128)S(1)} async-done(((f32[4,8,2048]{2,1,0:T(8,128)}), f32[4,8,2048]{2,1,0:T(8,128)S(1)}, u32[]{:S(2)}, u32[]{:S(2)}) %all-to-all-start.1) | async-done | bytes 262176 | tf_op jit(solution)/shard_map/all_to_all | solution.py:217
  83.6 6.5 %collective-permute-start.1 = (f32[8,1024]{1,0:T(8,128)S(1)}, f32[8,1024]{1,0:T(8,128)S(1)}, u32[]{:S(2)}, u32[]{:S(2)}) collective-permute-start(f32[8,1024]{1,0:T(8,128)S(1)} %get-tuple-element.10), channel_id=1, source_target_pairs={{0,16},{16,0},{32,48},{48,32},{64,80},{80,64},{96,112},{112,96},{1... | collective-permute-start | bytes 98312 | tf_op jit(solution)/shard_map/ppermute | solution.py:143
  90.1 0.0 slice-done
  90.1 0.1 constant_dynamic-slice_fusion
  90.2 0.7 copy.9
  91.0 0.0 collective-permute-done.1
  91.0 0.6 maximum_select_fusion.d_ref
  91.6 9.3 %shard_map.39 = f32[2048,8]{1,0:T(8,128)} custom-call(f32[8,2048]{1,0:T(8,128)} %maximum_select_fusion.d_ref, f32[34,128,128]{2,1,0:T(8,128)} %g_ref.5, f32[5,8,128]{2,1,0:T(8,128)} %bitcast.7), custom_call_target="tpu_custom_call" | custom-call | tf_op jit(solution)/shard_map/pallas_call | solution.py:130
  101.0 2.2 %copy.7 = f32[2048,8]{0,1:T(8,128)} copy(f32[2048,8]{1,0:T(8,128)} %shard_map.39) | data formatting | bytes 131072 | tf_op jit(solution)/shard_map/pallas_call | solution.py:130
  (2 shorter events, 0.0 us)
Async XLA Ops:
  11.3 22.9 %collective-permute-start = (f32[1024,128]{1,0:T(8,128)}, f32[1024,128]{1,0:T(8,128)S(1)}, u32[]{:S(2)}, u32[]{:S(2)}) collective-permute-start(f32[1024,128]{1,0:T(8,128)} %get-tuple-element.8), channel_id=1, source_target_pairs={{0,256},{16,272},{32,288},{48,304},{64,320},{80,336},{96,352},{112... | collective-permute-start | bytes 1572872 | tf_op jit(solution)/shard_map/ppermute | solution.py:143
  34.2 0.8 copy-start
  46.2 43.9 %slice-start = ((f32[13,128,128]{2,1,0:T(8,128)}), f32[5,128,128]{2,1,0:T(8,128)S(1)}, s32[]{:S(2)}) async-start(f32[13,128,128]{2,1,0:T(8,128)} %c_ref.3), calls=%async_computation.2 | async-start | bytes 655360 | tf_op jit(solution)/shard_map/slice | solution.py:243
  61.5 22.0 %all-to-all-start.1 = ((f32[4,8,2048]{2,1,0:T(8,128)}), f32[4,8,2048]{2,1,0:T(8,128)S(1)}, u32[]{:S(2)}, u32[]{:S(2)}) async-start(f32[4,8,2048]{2,1,0:T(8,128)} %bitcast.3), calls=%async_computation.1 | async-start | bytes 524288 | tf_op jit(solution)/shard_map/all_to_all | solution.py:217
  83.6 7.4 %collective-permute-start.1 = (f32[8,1024]{1,0:T(8,128)S(1)}, f32[8,1024]{1,0:T(8,128)S(1)}, u32[]{:S(2)}, u32[]{:S(2)}) collective-permute-start(f32[8,1024]{1,0:T(8,128)S(1)} %get-tuple-element.10), channel_id=1, source_target_pairs={{0,16},{16,0},{32,48},{48,32},{64,80},{80,64},{96,112},{112,96},{1... | collective-permute-start | bytes 98312 | tf_op jit(solution)/shard_map/ppermute | solution.py:143

commit v6 on v5

--- a/solution.py
+++ b/solution.py
@@ -105,7 +105,7 @@
     )(parity, keep, recv, gate_stack, coupling)
 
 
-def _final_kernel(d_ref, g_ref, tab_ref, o_ref, m_ref, *, gate_base, cycles):
+def _final_kernel(d_ref, g_ref, tab_ref, out_ref, o_ref, m_ref, *, gate_base, cycles):
     width = d_ref.shape[0]
     n_blocks = d_ref.shape[1] // BLOCK
     for a in range(n_blocks):
@@ -121,17 +121,21 @@
             m_ref[pl.ds(a * width, width), :] = o_ref[pl.ds(a * BLOCK, BLOCK), :].T * table
         m_ref[...] = _apply(m_ref[...], _weights(g_ref[gate_base + 2 * turn + 1]))
         for a in range(n_blocks):
-            o_ref[pl.ds(a * BLOCK, BLOCK), :] = m_ref[pl.ds(a * width, width), :].T
+            if turn == cycles - 1:
+                out_ref[:, pl.ds(a * BLOCK, BLOCK)] = m_ref[pl.ds(a * width, width), :]
+            else:
+                o_ref[pl.ds(a * BLOCK, BLOCK), :] = m_ref[pl.ds(a * width, width), :].T
 
 
 def final_layers(d, gate_stack, tables, gate_base, cycles):
     width, rows = d.shape
     kernel = functools.partial(_final_kernel, gate_base=gate_base, cycles=cycles)
-    return pl.pallas_call(
+    out = pl.pallas_call(
         kernel,
-        out_shape=jax.ShapeDtypeStruct((rows, width), d.dtype),
-        scratch_shapes=[pltpu.VMEM((BLOCK, BLOCK), jnp.float32)],
+        out_shape=jax.ShapeDtypeStruct((width, rows), d.dtype),
+        scratch_shapes=[pltpu.VMEM((rows, width), jnp.float32), pltpu.VMEM((BLOCK, BLOCK), jnp.float32)],
     )(d, gate_stack, tables)
+    return out.T
 
 
 HIGHEST_PREC = lax.Precision.HIGHEST

time: 104 us -> 101 us (0.971)
  local copies, waits for them, and re-layouts: 3.84 us -> 1.67 us
    pallas_call x1 -> x0, local copies, waits for them, and re-layouts: 2.16 us -> none  [final_layers(): pl.pallas_call(kernel, out_shape=jax.ShapeDtypeStruct((rows, width), d.dt...]
where the time goes in v6:
time: 101 us; the launch traced here: 100 us
  Pallas kernels  31.4 us (31%)
  starting transfers between devices  31.3 us (31%)
  waiting for transfers between devices  20.1 us (20%)
  blocking collectives  14.5 us (14%)
  local copies, waits for them, and re-layouts  1.67 us (2%)
  other arithmetic  1.41 us (1%)
    all_to_all x1, starting transfers between devices, reduce_columns(): cols = lax.all_to_all(blocks, axis, 0, 0, tiled=False).sum(0)  16.4 us
    ppermute x2, starting transfers between devices, partner(): return lax.ppermute(value, axis, pairs)  14.9 us
    all_to_all x1, blocking collectives, reduce_columns(): cols = lax.all_to_all(blocks, axis, 0, 0, tiled=False).sum(0)  14.5 us
    ppermute x2, waiting for transfers between devices, partner(): return lax.ppermute(value, axis, pairs)  14.4 us
    pallas_call x1, Pallas kernels, group_a(): pl.pallas_call(functools.partial(_group_a_kernel, cycles=cycles), out_sha...  11.3 us
    pallas_call x1, Pallas kernels, group_b(): pl.pallas_call(kernel, out_shape=jax.ShapeDtypeStruct((cols, rows), keep....  11.2 us
    pallas_call x1, Pallas kernels, final_layers(): pl.pallas_call(kernel, out_shape=jax.ShapeDtypeStruct((width, rows), d.dt...  8.82 us
    all_to_all x1, waiting for transfers between devices, reduce_columns(): cols = lax.all_to_all(blocks, axis, 0, 0, tiled=False).sum(0)  5.67 us
  transfers between devices with their start and end apart: 3, of which 2 were waited for; matrix products, arithmetic and copies ran while one was open for 1% of the time, Pallas kernels for 0%

profile of v6, /device:TPU:1, one launch (start us, length us, event | category | flops | bytes accessed | tf_op | source)
XLA Modules:
  0.0 100.4 jit_solution(14854803274966128872)
XLA Ops:
  0.0 11.3 %shard_map.37 = (f32[1024,128]{1,0:T(8,128)}, f32[1024,128]{1,0:T(8,128)}) custom-call(s32[1]{0:T(128)} %bitcast.p_ref, f32[2048,128]{1,0:T(8,128)} %bitcast.7, f32[34,128,128]{2,1,0:T(8,128)} %g_ref.5, f32[13,128,128]{2,1,0:T(8,128)} %c_ref.3), custom_call_target="tpu_custom_call" | custom-call | tf_op jit(solution)/shard_map/pallas_call | solution.py:87
  11.3 8.4 %collective-permute-start = (f32[1024,128]{1,0:T(8,128)}, f32[1024,128]{1,0:T(8,128)S(1)}, u32[]{:S(2)}, u32[]{:S(2)}) collective-permute-start(f32[1024,128]{1,0:T(8,128)} %get-tuple-element.8), channel_id=1, source_target_pairs={{0,256},{16,272},{32,288},{48,304},{64,320},{80,336},{96,352},{112... | collective-permute-start | bytes 1572872 | tf_op jit(solution)/shard_map/ppermute | solution.py:147
  19.8 14.4 %collective-permute-done.recv_ref = f32[1024,128]{1,0:T(8,128)S(1)} collective-permute-done((f32[1024,128]{1,0:T(8,128)}, f32[1024,128]{1,0:T(8,128)S(1)}, u32[]{:S(2)}, u32[]{:S(2)}) %collective-permute-start) | collective-permute-done | bytes 524320 | tf_op jit(solution)/shard_map/ppermute | solution.py:147
  34.2 0.0 copy-start
  34.2 0.8 copy-done
  35.0 11.2 %shard_map.38 = f32[128,2048]{1,0:T(8,128)} custom-call(s32[1]{0:T(128)} %bitcast.p_ref, f32[1024,128]{1,0:T(8,128)} %get-tuple-element.7.keep_ref, f32[1024,128]{1,0:T(8,128)} %copy-done, f32[34,128,128]{2,1,0:T(8,128)} %g_ref.5, f32[13,128,128]{2,1,0:T(8,128)} %c_ref.3), custom_call_target="tpu_custom_call" | custom-call | tf_op jit(solution)/shard_map/pallas_call | solution.py:99
  46.2 0.0 slice-start
  46.2 14.5 %all_to_all.10 = f32[4,32,2048]{2,1,0:T(8,128)S(1)} all-to-all(f32[4,32,2048]{2,1,0:T(8,128)} %bitcast.6), channel_id=1, replica_groups=mesh['yh'=2,'z'=8,'core'=2,'x'=4,'yl'=4] {'x'}, dimensions={0} | all-to-all | bytes 2097152 | tf_op jit(solution)/shard_map/all_to_all | solution.py:221
  60.8 0.8 reduce_sum.18
  61.5 16.4 %all-to-all-start.1 = ((f32[4,8,2048]{2,1,0:T(8,128)}), f32[4,8,2048]{2,1,0:T(8,128)S(1)}, u32[]{:S(2)}, u32[]{:S(2)}) async-start(f32[4,8,2048]{2,1,0:T(8,128)} %bitcast.3), calls=%async_computation.1 | async-start | bytes 524288 | tf_op jit(solution)/shard_map/all_to_all | solution.py:221
  77.9 5.7 %all-to-all-done.1 = f32[4,8,2048]{2,1,0:T(8,128)S(1)} async-done(((f32[4,8,2048]{2,1,0:T(8,128)}), f32[4,8,2048]{2,1,0:T(8,128)S(1)}, u32[]{:S(2)}, u32[]{:S(2)}) %all-to-all-start.1) | async-done | bytes 262176 | tf_op jit(solution)/shard_map/all_to_all | solution.py:221
  83.6 6.5 %collective-permute-start.1 = (f32[8,1024]{1,0:T(8,128)S(1)}, f32[8,1024]{1,0:T(8,128)S(1)}, u32[]{:S(2)}, u32[]{:S(2)}) collective-permute-start(f32[8,1024]{1,0:T(8,128)S(1)} %get-tuple-element.10), channel_id=1, source_target_pairs={{0,16},{16,0},{32,48},{48,32},{64,80},{80,64},{96,112},{112,96},{1... | collective-permute-start | bytes 98312 | tf_op jit(solution)/shard_map/ppermute | solution.py:147
  90.1 0.0 slice-done
  90.1 0.1 constant_dynamic-slice_fusion
  90.2 0.7 copy.7
  91.0 0.0 collective-permute-done.1
  91.0 0.6 maximum_select_fusion.d_ref
  91.6 8.8 %shard_map.39 = f32[8,2048]{1,0:T(8,128)} custom-call(f32[8,2048]{1,0:T(8,128)} %maximum_select_fusion.d_ref, f32[34,128,128]{2,1,0:T(8,128)} %g_ref.5, f32[5,8,128]{2,1,0:T(8,128)} %bitcast.8), custom_call_target="tpu_custom_call" | custom-call | tf_op jit(solution)/shard_map/pallas_call | solution.py:133
  (2 shorter events, 0.0 us)
Async XLA Ops:
  11.3 22.9 %collective-permute-start = (f32[1024,128]{1,0:T(8,128)}, f32[1024,128]{1,0:T(8,128)S(1)}, u32[]{:S(2)}, u32[]{:S(2)}) collective-permute-start(f32[1024,128]{1,0:T(8,128)} %get-tuple-element.8), channel_id=1, source_target_pairs={{0,256},{16,272},{32,288},{48,304},{64,320},{80,336},{96,352},{112... | collective-permute-start | bytes 1572872 | tf_op jit(solution)/shard_map/ppermute | solution.py:147
  34.2 0.8 copy-start
  46.2 43.9 %slice-start = ((f32[13,128,128]{2,1,0:T(8,128)}), f32[5,128,128]{2,1,0:T(8,128)S(1)}, s32[]{:S(2)}) async-start(f32[13,128,128]{2,1,0:T(8,128)} %c_ref.3), calls=%async_computation.2 | async-start | bytes 655360 | tf_op jit(solution)/shard_map/slice | solution.py:247
  61.5 22.0 %all-to-all-start.1 = ((f32[4,8,2048]{2,1,0:T(8,128)}), f32[4,8,2048]{2,1,0:T(8,128)S(1)}, u32[]{:S(2)}, u32[]{:S(2)}) async-start(f32[4,8,2048]{2,1,0:T(8,128)} %bitcast.3), calls=%async_computation.1 | async-start | bytes 524288 | tf_op jit(solution)/shard_map/all_to_all | solution.py:221
  83.6 7.4 %collective-permute-start.1 = (f32[8,1024]{1,0:T(8,128)S(1)}, f32[8,1024]{1,0:T(8,128)S(1)}, u32[]{:S(2)}, u32[]{:S(2)}) collective-permute-start(f32[8,1024]{1,0:T(8,128)S(1)} %get-tuple-element.10), channel_id=1, source_target_pairs={{0,16},{16,0},{32,48},{48,32},{64,80},{80,64},{96,112},{112,96},{1... | collective-permute-start | bytes 98312 | tf_op jit(solution)/shard_map/ppermute | solution.py:147

commit v7 on v6

--- a/solution.py
+++ b/solution.py
@@ -33,45 +33,57 @@
     return 0.9 * x + jnp.dot(lhs, w, preferred_element_type=jnp.float32)
 
 
-def _layer_turns(o_ref, t_ref, g_ref, c_ref, gate_base, cpl_base, cycles, last_to=None):
+def _weights_left(g):
+    hi, lo = _split((0.45 * g).T)
+    return jnp.concatenate([hi, lo, hi], axis=1)
+
+
+def _apply_left(w, x):
+    hi, lo = _split(x)
+    rhs = jnp.concatenate([hi, hi, lo], axis=0)
+    return 0.9 * x + jnp.dot(w, rhs, preferred_element_type=jnp.float32)
+
+
+def _layer_turns(o_ref, t_ref, g_ref, c_ref, cycles, last_to=None):
     rows = o_ref.shape[0]
     n_blocks = rows // BLOCK
     for turn in range(cycles):
-        first = gate_base + 3 * turn
-        table = c_ref[cpl_base + turn]
+        first = 3 * turn
+        table = c_ref[turn]
+        xs = jnp.concatenate([o_ref[pl.ds(t, BLOCK, stride=n_blocks), :] for t in range(n_blocks)], axis=1)
+        ys = _apply_left(_weights_left(g_ref[first]), xs)
         for t in range(n_blocks):
-            t_ref[pl.ds(t * BLOCK, BLOCK), :] = o_ref[pl.ds(t, BLOCK, stride=n_blocks), :].T
-        t_ref[...] = _apply(t_ref[...], _weights(g_ref[first]))
-        for t in range(n_blocks):
-            o_ref[pl.ds(t, BLOCK, stride=n_blocks), :] = t_ref[pl.ds(t * BLOCK, BLOCK), :].T
+            o_ref[pl.ds(t, BLOCK, stride=n_blocks), :] = ys[:, t * BLOCK:(t + 1) * BLOCK]
         y = _apply(o_ref[...], _weights(g_ref[first + 1]))
         o_ref[...] = (y.reshape(n_blocks, BLOCK, -1) * table[None]).reshape(y.shape)
-        for a in range(n_blocks):
-            t_ref[pl.ds(a * BLOCK, BLOCK), :] = o_ref[pl.ds(a * BLOCK, BLOCK), :].T
-        t_ref[...] = _apply(t_ref[...], _weights(g_ref[first + 2]))
         if last_to is not None and turn == cycles - 1:
+            for a in range(n_blocks):
+                t_ref[pl.ds(a * BLOCK, BLOCK), :] = o_ref[pl.ds(a * BLOCK, BLOCK), :].T
+            t_ref[...] = _apply(t_ref[...], _weights(g_ref[first + 2]))
             for a in range(n_blocks):
                 last_to[:, pl.ds(a * BLOCK, BLOCK)] = t_ref[pl.ds(a * BLOCK, BLOCK), :]
         else:
+            xs = jnp.concatenate([o_ref[pl.ds(a * BLOCK, BLOCK), :] for a in range(n_blocks)], axis=1)
+            ys = _apply_left(_weights_left(g_ref[first + 2]), xs)
             for a in range(n_blocks):
-                o_ref[pl.ds(a * BLOCK, BLOCK), :] = t_ref[pl.ds(a * BLOCK, BLOCK), :].T
-
-
-def _group_a_kernel(p_ref, x_ref, g_ref, c_ref, keep_ref, send_ref, o_ref, t_ref, *, cycles):
+                o_ref[pl.ds(a * BLOCK, BLOCK), :] = ys[:, a * BLOCK:(a + 1) * BLOCK]
+
+
+def _group_a_kernel(p_ref, x_ref, g_ref, c_ref, keep_ref, send_ref, o_ref, *, cycles):
     half = keep_ref.shape[0]
     o_ref[...] = x_ref[...]
-    _layer_turns(o_ref, t_ref, g_ref, c_ref, 0, 0, cycles)
+    _layer_turns(o_ref, None, g_ref, c_ref, cycles)
     p = p_ref[0]
     keep_ref[...] = o_ref[pl.ds(pl.multiple_of(p * half, half), half), :]
     send_ref[...] = o_ref[pl.ds(pl.multiple_of((1 - p) * half, half), half), :]
 
 
-def _group_b_kernel(p_ref, keep_ref, recv_ref, g_ref, c_ref, out_ref, o_ref, t_ref, *, gate_base, cpl_base, cycles):
+def _group_b_kernel(p_ref, keep_ref, recv_ref, g_ref, c_ref, out_ref, o_ref, t_ref, *, cycles):
     half = keep_ref.shape[0]
     p = p_ref[0]
     o_ref[pl.ds(pl.multiple_of(p * half, half), half), :] = keep_ref[...]
     o_ref[pl.ds(pl.multiple_of((1 - p) * half, half), half), :] = recv_ref[...]
-    _layer_turns(o_ref, t_ref, g_ref, c_ref, gate_base, cpl_base, cycles, last_to=out_ref)
+    _layer_turns(o_ref, t_ref, g_ref, c_ref, cycles, last_to=out_ref)
 
 
 def _smem():
@@ -80,6 +92,10 @@
 
 def _vmem():
     return pl.BlockSpec(memory_space=pltpu.VMEM)
+
+
+def _stack_block(count, index):
+    return pl.BlockSpec((count, BLOCK, BLOCK), lambda step: (index, 0, 0), memory_space=pltpu.VMEM)
 
 
 def group_a(parity, x, gate_stack, coupling, cycles):
@@ -87,19 +103,20 @@
     return pl.pallas_call(
         functools.partial(_group_a_kernel, cycles=cycles),
         out_shape=(half, half),
-        in_specs=[_smem(), _vmem(), _vmem(), _vmem()],
+        grid=(1,),
+        in_specs=[_smem(), _vmem(), _stack_block(3 * cycles, 0), _stack_block(cycles, 0)],
         out_specs=(_vmem(), _vmem()),
-        scratch_shapes=[pltpu.VMEM(x.shape, jnp.float32), pltpu.VMEM(x.shape, jnp.float32)],
+        scratch_shapes=[pltpu.VMEM(x.shape, jnp.float32)],
     )(parity, x, gate_stack, coupling)
 
 
-def group_b(parity, keep, recv, gate_stack, coupling, gate_base, cpl_base, cycles):
+def group_b(parity, keep, recv, gate_stack, coupling, cycles):
     rows, cols = keep.shape[0] * 2, keep.shape[1]
-    kernel = functools.partial(_group_b_kernel, gate_base=gate_base, cpl_base=cpl_base, cycles=cycles)
     return pl.pallas_call(
-        kernel,
+        functools.partial(_group_b_kernel, cycles=cycles),
         out_shape=jax.ShapeDtypeStruct((cols, rows), keep.dtype),
-        in_specs=[_smem(), _vmem(), _vmem(), _vmem(), _vmem()],
+        grid=(1,),
+        in_specs=[_smem(), _vmem(), _vmem(), _stack_block(3 * cycles, 1), _stack_block(cycles, 1)],
         out_specs=_vmem(),
         scratch_shapes=[pltpu.VMEM((rows, cols), jnp.float32), pltpu.VMEM((rows, cols), jnp.float32)],
     )(parity, keep, recv, gate_stack, coupling)
@@ -239,7 +256,7 @@
     parity = (lax.axis_index(BITS) >> top_bit & 1).astype(jnp.int32).reshape(1)
     keep, send = group_a(parity, boundary[0], gate_stack, coupling, CYC_A)
     recv = partner(send, BITS, top_bit)
-    cols = group_b(parity, keep, recv, gate_stack, coupling, 3 * CYC_A, CYC_A, CYC_B)
+    cols = group_b(parity, keep, recv, gate_stack, coupling, CYC_B)
     cols = swap_lanes(reduce_columns(cols), 0)
     width = cols.shape[0]
     col_start = lax.axis_index(CUTS) * width

time: 101 us -> 97.1 us (0.961)
  Pallas kernels: 31.4 us -> 27.7 us
    pallas_call x1, Pallas kernels: 11.3 us -> 9.3 us  [group_a(): pl.pallas_call(functools.partial(_group_a_kernel, cycles=cycles), out_sha...]
    pallas_call x1, Pallas kernels: 11.2 us -> 9.53 us  [group_b(): pl.pallas_call(functools.partial(_group_b_kernel, cycles=cycles), out_sha...]
where the time goes in v7:
time: 97.1 us; the launch traced here: 96.7 us
  starting transfers between devices  31.3 us (32%)
  Pallas kernels  27.7 us (29%)
  waiting for transfers between devices  20.2 us (21%)
  blocking collectives  14.5 us (15%)
  local copies, waits for them, and re-layouts  1.67 us (2%)
  other arithmetic  1.41 us (1%)
    all_to_all x1, starting transfers between devices, reduce_columns(): cols = lax.all_to_all(blocks, axis, 0, 0, tiled=False).sum(0)  16.3 us
    ppermute x2, starting transfers between devices, partner(): return lax.ppermute(value, axis, pairs)  14.9 us
    all_to_all x1, blocking collectives, reduce_columns(): cols = lax.all_to_all(blocks, axis, 0, 0, tiled=False).sum(0)  14.5 us
    ppermute x2, waiting for transfers between devices, partner(): return lax.ppermute(value, axis, pairs)  14.5 us
    pallas_call x1, Pallas kernels, group_b(): pl.pallas_call(functools.partial(_group_b_kernel, cycles=cycles), out_sha...  9.53 us
    pallas_call x1, Pallas kernels, group_a(): pl.pallas_call(functools.partial(_group_a_kernel, cycles=cycles), out_sha...  9.3 us
    pallas_call x1, Pallas kernels, final_layers(): pl.pallas_call(kernel, out_shape=jax.ShapeDtypeStruct((width, rows), d.dt...  8.82 us
    all_to_all x1, waiting for transfers between devices, reduce_columns(): cols = lax.all_to_all(blocks, axis, 0, 0, tiled=False).sum(0)  5.67 us
  transfers between devices with their start and end apart: 3, of which 2 were waited for; matrix products, arithmetic and copies ran while one was open for 1% of the time, Pallas kernels for 0%

profile of v7, /device:TPU:1, one launch (start us, length us, event | category | flops | bytes accessed | tf_op | source)
XLA Modules:
  0.0 96.7 jit_solution(16017534660191718566)
XLA Ops:
  0.0 9.3 %shard_map.37 = (f32[1024,128]{1,0:T(8,128)}, f32[1024,128]{1,0:T(8,128)}) custom-call(s32[1]{0:T(128)} %bitcast.p_ref, f32[2048,128]{1,0:T(8,128)} %bitcast.7, f32[34,128,128]{2,1,0:T(8,128)} %g_ref.5, f32[13,128,128]{2,1,0:T(8,128)} %c_ref.3), custom_call_target="tpu_custom_call" | custom-call | tf_op jit(solution)/shard_map/pallas_call | solution.py:103
  9.3 8.5 %collective-permute-start = (f32[1024,128]{1,0:T(8,128)}, f32[1024,128]{1,0:T(8,128)S(1)}, u32[]{:S(2)}, u32[]{:S(2)}) collective-permute-start(f32[1024,128]{1,0:T(8,128)} %get-tuple-element.8), channel_id=1, source_target_pairs={{0,256},{16,272},{32,288},{48,304},{64,320},{80,336},{96,352},{112... | collective-permute-start | bytes 1572872 | tf_op jit(solution)/shard_map/ppermute | solution.py:164
  17.8 14.5 %collective-permute-done.recv_ref = f32[1024,128]{1,0:T(8,128)S(1)} collective-permute-done((f32[1024,128]{1,0:T(8,128)}, f32[1024,128]{1,0:T(8,128)S(1)}, u32[]{:S(2)}, u32[]{:S(2)}) %collective-permute-start) | collective-permute-done | bytes 524320 | tf_op jit(solution)/shard_map/ppermute | solution.py:164
  32.2 0.0 copy-start
  32.2 0.8 copy-done
  33.0 9.5 %shard_map.38 = f32[128,2048]{1,0:T(8,128)} custom-call(s32[1]{0:T(128)} %bitcast.p_ref, f32[1024,128]{1,0:T(8,128)} %get-tuple-element.7.keep_ref, f32[1024,128]{1,0:T(8,128)} %copy-done, f32[34,128,128]{2,1,0:T(8,128)} %g_ref.5, f32[13,128,128]{2,1,0:T(8,128)} %c_ref.3), custom_call_target="tpu_custom_call" | custom-call | tf_op jit(solution)/shard_map/pallas_call | solution.py:115
  42.6 0.0 slice-start
  42.6 14.5 %all_to_all.10 = f32[4,32,2048]{2,1,0:T(8,128)S(1)} all-to-all(f32[4,32,2048]{2,1,0:T(8,128)} %bitcast.6), channel_id=1, replica_groups=mesh['yh'=2,'z'=8,'core'=2,'x'=4,'yl'=4] {'x'}, dimensions={0} | all-to-all | bytes 2097152 | tf_op jit(solution)/shard_map/all_to_all | solution.py:238
  57.1 0.8 reduce_sum.18
  57.8 16.3 %all-to-all-start.1 = ((f32[4,8,2048]{2,1,0:T(8,128)}), f32[4,8,2048]{2,1,0:T(8,128)S(1)}, u32[]{:S(2)}, u32[]{:S(2)}) async-start(f32[4,8,2048]{2,1,0:T(8,128)} %bitcast.3), calls=%async_computation.1 | async-start | bytes 524288 | tf_op jit(solution)/shard_map/all_to_all | solution.py:238
  74.2 5.7 %all-to-all-done.1 = f32[4,8,2048]{2,1,0:T(8,128)S(1)} async-done(((f32[4,8,2048]{2,1,0:T(8,128)}), f32[4,8,2048]{2,1,0:T(8,128)S(1)}, u32[]{:S(2)}, u32[]{:S(2)}) %all-to-all-start.1) | async-done | bytes 262176 | tf_op jit(solution)/shard_map/all_to_all | solution.py:238
  79.9 6.5 %collective-permute-start.1 = (f32[8,1024]{1,0:T(8,128)S(1)}, f32[8,1024]{1,0:T(8,128)S(1)}, u32[]{:S(2)}, u32[]{:S(2)}) collective-permute-start(f32[8,1024]{1,0:T(8,128)S(1)} %get-tuple-element.10), channel_id=1, source_target_pairs={{0,16},{16,0},{32,48},{48,32},{64,80},{80,64},{96,112},{112,96},{1... | collective-permute-start | bytes 98312 | tf_op jit(solution)/shard_map/ppermute | solution.py:164
  86.4 0.0 slice-done
  86.4 0.1 constant_dynamic-slice_fusion
  86.5 0.7 copy.7
  87.3 0.0 collective-permute-done.1
  87.3 0.6 maximum_select_fusion.d_ref
  87.9 8.8 %shard_map.39 = f32[8,2048]{1,0:T(8,128)} custom-call(f32[8,2048]{1,0:T(8,128)} %maximum_select_fusion.d_ref, f32[34,128,128]{2,1,0:T(8,128)} %g_ref.5, f32[5,8,128]{2,1,0:T(8,128)} %bitcast.8), custom_call_target="tpu_custom_call" | custom-call | tf_op jit(solution)/shard_map/pallas_call | solution.py:150
  (2 shorter events, 0.0 us)
Async XLA Ops:
  9.3 22.9 %collective-permute-start = (f32[1024,128]{1,0:T(8,128)}, f32[1024,128]{1,0:T(8,128)S(1)}, u32[]{:S(2)}, u32[]{:S(2)}) collective-permute-start(f32[1024,128]{1,0:T(8,128)} %get-tuple-element.8), channel_id=1, source_target_pairs={{0,256},{16,272},{32,288},{48,304},{64,320},{80,336},{96,352},{112... | collective-permute-start | bytes 1572872 | tf_op jit(solution)/shard_map/ppermute | solution.py:164
  32.2 0.8 copy-start
  42.6 43.8 %slice-start = ((f32[13,128,128]{2,1,0:T(8,128)}), f32[5,128,128]{2,1,0:T(8,128)S(1)}, s32[]{:S(2)}) async-start(f32[13,128,128]{2,1,0:T(8,128)} %c_ref.3), calls=%async_computation.2 | async-start | bytes 655360 | tf_op jit(solution)/shard_map/slice | solution.py:264
  57.8 22.0 %all-to-all-start.1 = ((f32[4,8,2048]{2,1,0:T(8,128)}), f32[4,8,2048]{2,1,0:T(8,128)S(1)}, u32[]{:S(2)}, u32[]{:S(2)}) async-start(f32[4,8,2048]{2,1,0:T(8,128)} %bitcast.3), calls=%async_computation.1 | async-start | bytes 524288 | tf_op jit(solution)/shard_map/all_to_all | solution.py:238
  79.9 7.4 %collective-permute-start.1 = (f32[8,1024]{1,0:T(8,128)S(1)}, f32[8,1024]{1,0:T(8,128)S(1)}, u32[]{:S(2)}, u32[]{:S(2)}) collective-permute-start(f32[8,1024]{1,0:T(8,128)S(1)} %get-tuple-element.10), channel_id=1, source_target_pairs={{0,16},{16,0},{32,48},{48,32},{64,80},{80,64},{96,112},{112,96},{1... | collective-permute-start | bytes 98312 | tf_op jit(solution)/shard_map/ppermute | solution.py:164

commit v8 on v7

--- a/solution.py
+++ b/solution.py
@@ -122,21 +122,28 @@
     )(parity, keep, recv, gate_stack, coupling)
 
 
-def _final_kernel(d_ref, g_ref, tab_ref, out_ref, o_ref, m_ref, *, gate_base, cycles):
+def _final_kernel(p_ref, d_ref, recv_ref, g_ref, tab_ref, out_ref, o_ref, m_ref, *, cycles):
     width = d_ref.shape[0]
     n_blocks = d_ref.shape[1] // BLOCK
+    half = n_blocks // 2
+    p = p_ref[0]
     for a in range(n_blocks):
-        o_ref[pl.ds(a * BLOCK, BLOCK), :] = d_ref[:, pl.ds(a * BLOCK, BLOCK)].T
+        lane_block = pl.ds(a * BLOCK, BLOCK)
+        other = pl.ds((a % half) * BLOCK, BLOCK)
+        own = d_ref[:, lane_block]
+        got = recv_ref[:, other]
+        keep = (a // half) == p
+        o_ref[lane_block, :] = jnp.where(keep, own, got).T
     for turn in range(cycles):
         for t in range(n_blocks):
             m_ref[pl.ds(t * width, width), :] = o_ref[pl.ds(t, BLOCK, stride=n_blocks), :].T
-        m_ref[...] = _apply(m_ref[...], _weights(g_ref[gate_base + 2 * turn]))
+        m_ref[...] = _apply(m_ref[...], _weights(g_ref[2 * turn]))
         for t in range(n_blocks):
             o_ref[pl.ds(t, BLOCK, stride=n_blocks), :] = m_ref[pl.ds(t * width, width), :].T
         table = tab_ref[turn]
         for a in range(n_blocks):
             m_ref[pl.ds(a * width, width), :] = o_ref[pl.ds(a * BLOCK, BLOCK), :].T * table
-        m_ref[...] = _apply(m_ref[...], _weights(g_ref[gate_base + 2 * turn + 1]))
+        m_ref[...] = _apply(m_ref[...], _weights(g_ref[2 * turn + 1]))
         for a in range(n_blocks):
             if turn == cycles - 1:
                 out_ref[:, pl.ds(a * BLOCK, BLOCK)] = m_ref[pl.ds(a * width, width), :]
@@ -144,14 +151,15 @@
                 o_ref[pl.ds(a * BLOCK, BLOCK), :] = m_ref[pl.ds(a * width, width), :].T
 
 
-def final_layers(d, gate_stack, tables, gate_base, cycles):
-    width, rows = d.shape
-    kernel = functools.partial(_final_kernel, gate_base=gate_base, cycles=cycles)
+def final_layers(parity, cols, recv, gates, tables, cycles):
+    width, rows = cols.shape
     out = pl.pallas_call(
-        kernel,
-        out_shape=jax.ShapeDtypeStruct((width, rows), d.dtype),
+        functools.partial(_final_kernel, cycles=cycles),
+        out_shape=jax.ShapeDtypeStruct((width, rows), cols.dtype),
+        in_specs=[_smem(), _vmem(), _vmem(), _vmem(), _vmem()],
+        out_specs=_vmem(),
         scratch_shapes=[pltpu.VMEM((rows, width), jnp.float32), pltpu.VMEM((BLOCK, BLOCK), jnp.float32)],
-    )(d, gate_stack, tables)
+    )(parity, cols, recv, gates, tables)
     return out.T
 
 
@@ -256,13 +264,17 @@
     parity = (lax.axis_index(BITS) >> top_bit & 1).astype(jnp.int32).reshape(1)
     keep, send = group_a(parity, boundary[0], gate_stack, coupling, CYC_A)
     recv = partner(send, BITS, top_bit)
-    cols = group_b(parity, keep, recv, gate_stack, coupling, CYC_B)
-    cols = swap_lanes(reduce_columns(cols), 0)
+    cols = reduce_columns(group_b(parity, keep, recv, gate_stack, coupling, CYC_B))
+    half = cols.shape[1] // 2
+    low = (lax.axis_index(BITS) & 1).astype(jnp.int32).reshape(1)
+    outgoing = jnp.where(low[0] == 0, cols[:, half:], cols[:, :half])
+    incoming = partner(outgoing, BITS, 0)
     width = cols.shape[0]
     col_start = lax.axis_index(CUTS) * width
-    cpl_base = CYC_A + CYC_B
+    gate_base, cpl_base = 3 * CYC_A + 3 * CYC_B, CYC_A + CYC_B
     tables = lax.dynamic_slice_in_dim(coupling[cpl_base:cpl_base + CYC_C], col_start, width, axis=2)
-    return final_layers(cols, gate_stack, jnp.swapaxes(tables, 1, 2), 3 * CYC_A + 3 * CYC_B, CYC_C)
+    gates = gate_stack[gate_base:gate_base + 2 * CYC_C]
+    return final_layers(low, cols, incoming, gates, jnp.swapaxes(tables, 1, 2), CYC_C)
 
 
 def solution(mesh):

time: 97.1 us -> 98.7 us (1.016)
  local copies, waits for them, and re-layouts: 1.67 us -> 4.28 us
    slice x0 -> x1, local copies, waits for them, and re-layouts: none -> 1.99 us  [on_device(): gates = gate_stack[gate_base:gate_base + 2 * CYC_C]]
    unnamed x3 -> x7, local copies, waits for them, and re-layouts: 1.52 us -> 2.14 us
  transfers between devices with their start and end apart: 3 -> 3, of which waited for: 2 -> 2; matrix products, arithmetic and copies ran while one was open for 1% -> 3% of each run, Pallas kernels for 0% -> 0%
where the time goes in v8:
time: 98.7 us; the launch traced here: 98.3 us
  starting transfers between devices  31.3 us (32%)
  Pallas kernels  27.2 us (28%)
  waiting for transfers between devices  20.2 us (20%)
  blocking collectives  14.5 us (15%)
  local copies, waits for them, and re-layouts  4.28 us (4%)
    all_to_all x1, starting transfers between devices, reduce_columns(): cols = lax.all_to_all(blocks, axis, 0, 0, tiled=False).sum(0)  16.3 us
    ppermute x2, starting transfers between devices, partner(): return lax.ppermute(value, axis, pairs)  14.9 us
    all_to_all x1, blocking collectives, reduce_columns(): cols = lax.all_to_all(blocks, axis, 0, 0, tiled=False).sum(0)  14.5 us
    ppermute x2, waiting for transfers between devices, partner(): return lax.ppermute(value, axis, pairs)  14.5 us
    pallas_call x1, Pallas kernels, group_b(): pl.pallas_call(functools.partial(_group_b_kernel, cycles=cycles), out_sha...  9.53 us
    pallas_call x1, Pallas kernels, group_a(): pl.pallas_call(functools.partial(_group_a_kernel, cycles=cycles), out_sha...  9.32 us
    pallas_call x1, Pallas kernels, final_layers(): pl.pallas_call(functools.partial(_final_kernel, cycles=cycles), out_shape...  8.35 us
    all_to_all x1, waiting for transfers between devices, reduce_columns(): cols = lax.all_to_all(blocks, axis, 0, 0, tiled=False).sum(0)  5.67 us
  transfers between devices with their start and end apart: 3, of which 2 were waited for; matrix products, arithmetic and copies ran while one was open for 3% of the time, Pallas kernels for 0%

profile of v8, /device:TPU:1, one launch (start us, length us, event | category | flops | bytes accessed | tf_op | source)
XLA Modules:
  0.0 98.3 jit_solution(17129858287170345584)
XLA Ops:
  0.0 9.3 %shard_map.37 = (f32[1024,128]{1,0:T(8,128)}, f32[1024,128]{1,0:T(8,128)}) custom-call(s32[1]{0:T(128)} %bitcast.1.p_ref, f32[2048,128]{1,0:T(8,128)} %bitcast.8, f32[34,128,128]{2,1,0:T(8,128)} %g_ref.3, f32[13,128,128]{2,1,0:T(8,128)} %c_ref.3), custom_call_target="tpu_custom_call" | custom-call | tf_op jit(solution)/shard_map/pallas_call | solution.py:103
  9.3 8.5 %collective-permute-start = (f32[1024,128]{1,0:T(8,128)}, f32[1024,128]{1,0:T(8,128)S(1)}, u32[]{:S(2)}, u32[]{:S(2)}) collective-permute-start(f32[1024,128]{1,0:T(8,128)} %get-tuple-element.8), channel_id=1, source_target_pairs={{0,256},{16,272},{32,288},{48,304},{64,320},{80,336},{96,352},{112... | collective-permute-start | bytes 1572872 | tf_op jit(solution)/shard_map/ppermute | solution.py:172
  17.8 14.5 %collective-permute-done.recv_ref = f32[1024,128]{1,0:T(8,128)S(1)} collective-permute-done((f32[1024,128]{1,0:T(8,128)}, f32[1024,128]{1,0:T(8,128)S(1)}, u32[]{:S(2)}, u32[]{:S(2)}) %collective-permute-start) | collective-permute-done | bytes 524320 | tf_op jit(solution)/shard_map/ppermute | solution.py:172
  32.3 0.0 copy-start.1
  32.3 0.8 copy-done.1
  33.0 9.5 %shard_map.38 = f32[128,2048]{1,0:T(8,128)} custom-call(s32[1]{0:T(128)} %bitcast.1.p_ref, f32[1024,128]{1,0:T(8,128)} %get-tuple-element.7.keep_ref, f32[1024,128]{1,0:T(8,128)} %copy-done.1, f32[34,128,128]{2,1,0:T(8,128)} %g_ref.3, f32[13,128,128]{2,1,0:T(8,128)} %c_ref.3), custom_call_target="tpu_custom_call" | custom-call | tf_op jit(solution)/shard_map/pallas_call | solution.py:115
  42.6 0.0 slice-start
  42.6 14.5 %all_to_all.10 = f32[4,32,2048]{2,1,0:T(8,128)S(1)} all-to-all(f32[4,32,2048]{2,1,0:T(8,128)} %bitcast.7), channel_id=1, replica_groups=mesh['yh'=2,'z'=8,'core'=2,'x'=4,'yl'=4] {'x'}, dimensions={0} | all-to-all | bytes 2097152 | tf_op jit(solution)/shard_map/all_to_all | solution.py:246
  57.1 0.8 reduce_sum.18
  57.8 16.3 %all-to-all-start.1 = ((f32[4,8,2048]{2,1,0:T(8,128)}), f32[4,8,2048]{2,1,0:T(8,128)S(1)}, u32[]{:S(2)}, u32[]{:S(2)}) async-start(f32[4,8,2048]{2,1,0:T(8,128)} %bitcast.4), calls=%async_computation.1 | async-start | bytes 524288 | tf_op jit(solution)/shard_map/all_to_all | solution.py:246
  74.2 5.7 %all-to-all-done.1 = f32[4,8,2048]{2,1,0:T(8,128)S(1)} async-done(((f32[4,8,2048]{2,1,0:T(8,128)}), f32[4,8,2048]{2,1,0:T(8,128)S(1)}, u32[]{:S(2)}, u32[]{:S(2)}) %all-to-all-start.1) | async-done | bytes 262176 | tf_op jit(solution)/shard_map/all_to_all | solution.py:246
  79.9 0.0 copy-start
  79.9 6.5 %collective-permute-start.1 = (f32[8,1024]{1,0:T(8,128)S(1)}, f32[8,1024]{1,0:T(8,128)S(1)}, u32[]{:S(2)}, u32[]{:S(2)}) collective-permute-start(f32[8,1024]{1,0:T(8,128)S(1)} %slice_select_fusion), channel_id=1, source_target_pairs={{0,16},{16,0},{32,48},{48,32},{64,80},{80,64},{96,112},{112,96},{1... | collective-permute-start | bytes 98312 | tf_op jit(solution)/shard_map/ppermute | solution.py:172
  86.4 0.0 slice-done
  86.4 0.1 constant_dynamic-slice_fusion
  86.6 2.0 %slice.14.g_ref = f32[10,128,128]{2,1,0:T(8,128)} slice(f32[34,128,128]{2,1,0:T(8,128)} %g_ref.3), slice={[24:34], [0:128], [0:128]} | slice | bytes 1310720 | tf_op jit(solution)/shard_map/slice | solution.py:276
  88.5 0.7 copy.7
  89.3 0.0 collective-permute-done.1.recv_ref
  89.3 0.0 copy-start.2
  89.3 0.0 copy-done
  89.3 0.6 copy-done.2
  89.9 8.3 %shard_map.39 = f32[8,2048]{1,0:T(8,128)} custom-call(s32[1]{0:T(128)} %bitcast.p_ref, f32[8,2048]{1,0:T(8,128)} %copy-done, f32[8,1024]{1,0:T(8,128)} %copy-done.2, f32[10,128,128]{2,1,0:T(8,128)} %slice.14.g_ref, f32[5,8,128]{2,1,0:T(8,128)} %bitcast.9), custom_call_target="tpu_custom_call" | custom-call | tf_op jit(solution)/shard_map/pallas_call | solution.py:156
  (2 shorter events, 0.0 us)
Async XLA Ops:
  9.3 22.9 %collective-permute-start = (f32[1024,128]{1,0:T(8,128)}, f32[1024,128]{1,0:T(8,128)S(1)}, u32[]{:S(2)}, u32[]{:S(2)}) collective-permute-start(f32[1024,128]{1,0:T(8,128)} %get-tuple-element.8), channel_id=1, source_target_pairs={{0,256},{16,272},{32,288},{48,304},{64,320},{80,336},{96,352},{112... | collective-permute-start | bytes 1572872 | tf_op jit(solution)/shard_map/ppermute | solution.py:172
  32.3 0.8 copy-start.1
  42.6 43.8 %slice-start = ((f32[13,128,128]{2,1,0:T(8,128)}), f32[5,128,128]{2,1,0:T(8,128)S(1)}, s32[]{:S(2)}) async-start(f32[13,128,128]{2,1,0:T(8,128)} %c_ref.3), calls=%async_computation.2 | async-start | bytes 655360 | tf_op jit(solution)/shard_map/slice | solution.py:275
  57.8 22.0 %all-to-all-start.1 = ((f32[4,8,2048]{2,1,0:T(8,128)}), f32[4,8,2048]{2,1,0:T(8,128)S(1)}, u32[]{:S(2)}, u32[]{:S(2)}) async-start(f32[4,8,2048]{2,1,0:T(8,128)} %bitcast.4), calls=%async_computation.1 | async-start | bytes 524288 | tf_op jit(solution)/shard_map/all_to_all | solution.py:246
  79.9 9.4 %copy-start = (f32[8,2048]{1,0:T(8,128)}, f32[8,2048]{1,0:T(8,128)S(1)}, u32[]{:S(2)}) copy-start(f32[8,2048]{1,0:T(8,128)S(1)} %reduce_sum.19.d_ref) | copy-start | bytes 196612
  79.9 9.4 %collective-permute-start.1 = (f32[8,1024]{1,0:T(8,128)S(1)}, f32[8,1024]{1,0:T(8,128)S(1)}, u32[]{:S(2)}, u32[]{:S(2)}) collective-permute-start(f32[8,1024]{1,0:T(8,128)S(1)} %slice_select_fusion), channel_id=1, source_target_pairs={{0,16},{16,0},{32,48},{48,32},{64,80},{80,64},{96,112},{112,96},{1... | collective-permute-start | bytes 98312 | tf_op jit(solution)/shard_map/ppermute | solution.py:172
  89.3 0.6 copy-start.2

commit v9 on v8

--- a/solution.py
+++ b/solution.py
@@ -122,7 +122,7 @@
     )(parity, keep, recv, gate_stack, coupling)
 
 
-def _final_kernel(p_ref, d_ref, recv_ref, g_ref, tab_ref, out_ref, o_ref, m_ref, *, cycles):
+def _final_kernel(p_ref, d_ref, recv_ref, g_ref, tab_ref, out_ref, o_ref, m_ref, *, gate_base, cycles):
     width = d_ref.shape[0]
     n_blocks = d_ref.shape[1] // BLOCK
     half = n_blocks // 2
@@ -137,13 +137,13 @@
     for turn in range(cycles):
         for t in range(n_blocks):
             m_ref[pl.ds(t * width, width), :] = o_ref[pl.ds(t, BLOCK, stride=n_blocks), :].T
-        m_ref[...] = _apply(m_ref[...], _weights(g_ref[2 * turn]))
+        m_ref[...] = _apply(m_ref[...], _weights(g_ref[gate_base + 2 * turn]))
         for t in range(n_blocks):
             o_ref[pl.ds(t, BLOCK, stride=n_blocks), :] = m_ref[pl.ds(t * width, width), :].T
         table = tab_ref[turn]
         for a in range(n_blocks):
             m_ref[pl.ds(a * width, width), :] = o_ref[pl.ds(a * BLOCK, BLOCK), :].T * table
-        m_ref[...] = _apply(m_ref[...], _weights(g_ref[2 * turn + 1]))
+        m_ref[...] = _apply(m_ref[...], _weights(g_ref[gate_base + 2 * turn + 1]))
         for a in range(n_blocks):
             if turn == cycles - 1:
                 out_ref[:, pl.ds(a * BLOCK, BLOCK)] = m_ref[pl.ds(a * width, width), :]
@@ -151,15 +151,15 @@
                 o_ref[pl.ds(a * BLOCK, BLOCK), :] = m_ref[pl.ds(a * width, width), :].T
 
 
-def final_layers(parity, cols, recv, gates, tables, cycles):
+def final_layers(parity, cols, recv, gate_stack, tables, gate_base, cycles):
     width, rows = cols.shape
     out = pl.pallas_call(
-        functools.partial(_final_kernel, cycles=cycles),
+        functools.partial(_final_kernel, gate_base=gate_base, cycles=cycles),
         out_shape=jax.ShapeDtypeStruct((width, rows), cols.dtype),
         in_specs=[_smem(), _vmem(), _vmem(), _vmem(), _vmem()],
         out_specs=_vmem(),
         scratch_shapes=[pltpu.VMEM((rows, width), jnp.float32), pltpu.VMEM((BLOCK, BLOCK), jnp.float32)],
-    )(parity, cols, recv, gates, tables)
+    )(parity, cols, recv, gate_stack, tables)
     return out.T
 
 
@@ -273,8 +273,7 @@
     col_start = lax.axis_index(CUTS) * width
     gate_base, cpl_base = 3 * CYC_A + 3 * CYC_B, CYC_A + CYC_B
     tables = lax.dynamic_slice_in_dim(coupling[cpl_base:cpl_base + CYC_C], col_start, width, axis=2)
-    gates = gate_stack[gate_base:gate_base + 2 * CYC_C]
-    return final_layers(low, cols, incoming, gates, jnp.swapaxes(tables, 1, 2), CYC_C)
+    return final_layers(low, cols, incoming, gate_stack, jnp.swapaxes(tables, 1, 2), gate_base, CYC_C)
 
 
 def solution(mesh):

time: 98.7 us -> 97.2 us (0.985)
  local copies, waits for them, and re-layouts: 4.28 us -> 2.29 us
    slice x1 -> x0, local copies, waits for them, and re-layouts: 1.99 us -> none  [on_device(): gates = gate_stack[gate_base:gate_base + 2 * CYC_C]]
  transfers between devices with their start and end apart: 3 -> 3, of which waited for: 2 -> 2; matrix products, arithmetic and copies ran while one was open for 3% -> 1% of each run, Pallas kernels for 0% -> 0%
where the time goes in v9:
time: 97.2 us; the launch traced here: 96.8 us
  starting transfers between devices  31.3 us (32%)
  Pallas kernels  27.7 us (28%)
  waiting for transfers between devices  20.2 us (21%)
  blocking collectives  14.5 us (15%)
  local copies, waits for them, and re-layouts  2.29 us (2%)
    all_to_all x1, starting transfers between devices, reduce_columns(): cols = lax.all_to_all(blocks, axis, 0, 0, tiled=False).sum(0)  16.3 us
    ppermute x2, starting transfers between devices, partner(): return lax.ppermute(value, axis, pairs)  14.9 us
    all_to_all x1, blocking collectives, reduce_columns(): cols = lax.all_to_all(blocks, axis, 0, 0, tiled=False).sum(0)  14.5 us
    ppermute x2, waiting for transfers between devices, partner(): return lax.ppermute(value, axis, pairs)  14.5 us
    pallas_call x1, Pallas kernels, group_b(): pl.pallas_call(functools.partial(_group_b_kernel, cycles=cycles), out_sha...  9.53 us
    pallas_call x1, Pallas kernels, group_a(): pl.pallas_call(functools.partial(_group_a_kernel, cycles=cycles), out_sha...  9.32 us
    pallas_call x1, Pallas kernels, final_layers(): pl.pallas_call(functools.partial(_final_kernel, gate_base=gate_base, cycl...  8.89 us
    all_to_all x1, waiting for transfers between devices, reduce_columns(): cols = lax.all_to_all(blocks, axis, 0, 0, tiled=False).sum(0)  5.67 us
  transfers between devices with their start and end apart: 3, of which 2 were waited for; matrix products, arithmetic and copies ran while one was open for 1% of the time, Pallas kernels for 0%

profile of v9, /device:TPU:1, one launch (start us, length us, event | category | flops | bytes accessed | tf_op | source)
XLA Modules:
  0.0 96.8 jit_solution(10526486347152997752)
XLA Ops:
  0.0 9.3 %shard_map.37 = (f32[1024,128]{1,0:T(8,128)}, f32[1024,128]{1,0:T(8,128)}) custom-call(s32[1]{0:T(128)} %bitcast.1.p_ref, f32[2048,128]{1,0:T(8,128)} %bitcast.8, f32[34,128,128]{2,1,0:T(8,128)} %g_ref.5, f32[13,128,128]{2,1,0:T(8,128)} %c_ref.3), custom_call_target="tpu_custom_call" | custom-call | tf_op jit(solution)/shard_map/pallas_call | solution.py:103
  9.3 8.5 %collective-permute-start = (f32[1024,128]{1,0:T(8,128)}, f32[1024,128]{1,0:T(8,128)S(1)}, u32[]{:S(2)}, u32[]{:S(2)}) collective-permute-start(f32[1024,128]{1,0:T(8,128)} %get-tuple-element.8), channel_id=1, source_target_pairs={{0,256},{16,272},{32,288},{48,304},{64,320},{80,336},{96,352},{112... | collective-permute-start | bytes 1572872 | tf_op jit(solution)/shard_map/ppermute | solution.py:172
  17.8 14.5 %collective-permute-done.recv_ref = f32[1024,128]{1,0:T(8,128)S(1)} collective-permute-done((f32[1024,128]{1,0:T(8,128)}, f32[1024,128]{1,0:T(8,128)S(1)}, u32[]{:S(2)}, u32[]{:S(2)}) %collective-permute-start) | collective-permute-done | bytes 524320 | tf_op jit(solution)/shard_map/ppermute | solution.py:172
  32.3 0.0 copy-start.1
  32.3 0.8 copy-done.1
  33.0 9.5 %shard_map.38 = f32[128,2048]{1,0:T(8,128)} custom-call(s32[1]{0:T(128)} %bitcast.1.p_ref, f32[1024,128]{1,0:T(8,128)} %get-tuple-element.7.keep_ref, f32[1024,128]{1,0:T(8,128)} %copy-done.1, f32[34,128,128]{2,1,0:T(8,128)} %g_ref.5, f32[13,128,128]{2,1,0:T(8,128)} %c_ref.3), custom_call_target="tpu_custom_call" | custom-call | tf_op jit(solution)/shard_map/pallas_call | solution.py:115
  42.6 0.0 slice-start
  42.6 14.5 %all_to_all.10 = f32[4,32,2048]{2,1,0:T(8,128)S(1)} all-to-all(f32[4,32,2048]{2,1,0:T(8,128)} %bitcast.7), channel_id=1, replica_groups=mesh['yh'=2,'z'=8,'core'=2,'x'=4,'yl'=4] {'x'}, dimensions={0} | all-to-all | bytes 2097152 | tf_op jit(solution)/shard_map/all_to_all | solution.py:246
  57.1 0.8 reduce_sum.18
  57.8 16.3 %all-to-all-start.1 = ((f32[4,8,2048]{2,1,0:T(8,128)}), f32[4,8,2048]{2,1,0:T(8,128)S(1)}, u32[]{:S(2)}, u32[]{:S(2)}) async-start(f32[4,8,2048]{2,1,0:T(8,128)} %bitcast.4), calls=%async_computation.1 | async-start | bytes 524288 | tf_op jit(solution)/shard_map/all_to_all | solution.py:246
  74.2 5.7 %all-to-all-done.1 = f32[4,8,2048]{2,1,0:T(8,128)S(1)} async-done(((f32[4,8,2048]{2,1,0:T(8,128)}), f32[4,8,2048]{2,1,0:T(8,128)S(1)}, u32[]{:S(2)}, u32[]{:S(2)}) %all-to-all-start.1) | async-done | bytes 262176 | tf_op jit(solution)/shard_map/all_to_all | solution.py:246
  79.9 0.0 copy-start
  79.9 6.5 %collective-permute-start.1 = (f32[8,1024]{1,0:T(8,128)S(1)}, f32[8,1024]{1,0:T(8,128)S(1)}, u32[]{:S(2)}, u32[]{:S(2)}) collective-permute-start(f32[8,1024]{1,0:T(8,128)S(1)} %slice_select_fusion), channel_id=1, source_target_pairs={{0,16},{16,0},{32,48},{48,32},{64,80},{80,64},{96,112},{112,96},{1... | collective-permute-start | bytes 98312 | tf_op jit(solution)/shard_map/ppermute | solution.py:172
  86.4 0.0 slice-done
  86.4 0.1 constant_dynamic-slice_fusion
  86.6 0.7 copy.7
  87.3 0.0 collective-permute-done.1.recv_ref
  87.3 0.0 copy-start.2
  87.3 0.0 copy-done
  87.3 0.6 copy-done.2
  87.9 8.9 %shard_map.39 = f32[8,2048]{1,0:T(8,128)} custom-call(s32[1]{0:T(128)} %bitcast.p_ref, f32[8,2048]{1,0:T(8,128)} %copy-done, f32[8,1024]{1,0:T(8,128)} %copy-done.2, f32[34,128,128]{2,1,0:T(8,128)} %g_ref.5, f32[5,8,128]{2,1,0:T(8,128)} %bitcast.9), custom_call_target="tpu_custom_call" | custom-call | tf_op jit(solution)/shard_map/pallas_call | solution.py:156
  (2 shorter events, 0.0 us)
Async XLA Ops:
  9.3 22.9 %collective-permute-start = (f32[1024,128]{1,0:T(8,128)}, f32[1024,128]{1,0:T(8,128)S(1)}, u32[]{:S(2)}, u32[]{:S(2)}) collective-permute-start(f32[1024,128]{1,0:T(8,128)} %get-tuple-element.8), channel_id=1, source_target_pairs={{0,256},{16,272},{32,288},{48,304},{64,320},{80,336},{96,352},{112... | collective-permute-start | bytes 1572872 | tf_op jit(solution)/shard_map/ppermute | solution.py:172
  32.3 0.8 copy-start.1
  42.6 43.8 %slice-start = ((f32[13,128,128]{2,1,0:T(8,128)}), f32[5,128,128]{2,1,0:T(8,128)S(1)}, s32[]{:S(2)}) async-start(f32[13,128,128]{2,1,0:T(8,128)} %c_ref.3), calls=%async_computation.2 | async-start | bytes 655360 | tf_op jit(solution)/shard_map/slice | solution.py:275
  57.8 22.0 %all-to-all-start.1 = ((f32[4,8,2048]{2,1,0:T(8,128)}), f32[4,8,2048]{2,1,0:T(8,128)S(1)}, u32[]{:S(2)}, u32[]{:S(2)}) async-start(f32[4,8,2048]{2,1,0:T(8,128)} %bitcast.4), calls=%async_computation.1 | async-start | bytes 524288 | tf_op jit(solution)/shard_map/all_to_all | solution.py:246
  79.9 7.4 %copy-start = (f32[8,2048]{1,0:T(8,128)}, f32[8,2048]{1,0:T(8,128)S(1)}, u32[]{:S(2)}) copy-start(f32[8,2048]{1,0:T(8,128)S(1)} %reduce_sum.19.d_ref) | copy-start | bytes 196612
  79.9 7.4 %collective-permute-start.1 = (f32[8,1024]{1,0:T(8,128)S(1)}, f32[8,1024]{1,0:T(8,128)S(1)}, u32[]{:S(2)}, u32[]{:S(2)}) collective-permute-start(f32[8,1024]{1,0:T(8,128)S(1)} %slice_select_fusion), channel_id=1, source_target_pairs={{0,16},{16,0},{32,48},{48,32},{64,80},{80,64},{96,112},{112,96},{1... | collective-permute-start | bytes 98312 | tf_op jit(solution)/shard_map/ppermute | solution.py:172
  87.3 0.6 copy-start.2

commit v10 on v9

--- a/solution.py
+++ b/solution.py
@@ -122,11 +122,12 @@
     )(parity, keep, recv, gate_stack, coupling)
 
 
-def _final_kernel(p_ref, d_ref, recv_ref, g_ref, tab_ref, out_ref, o_ref, m_ref, *, gate_base, cycles):
+def _final_kernel(p_ref, d_ref, recv_ref, g_ref, c_ref, out_ref, o_ref, m_ref, tt_ref, *, gate_base, cpl_base, cycles):
     width = d_ref.shape[0]
     n_blocks = d_ref.shape[1] // BLOCK
     half = n_blocks // 2
     p = p_ref[0]
+    col_start = pl.multiple_of(p_ref[1] * width, width)
     for a in range(n_blocks):
         lane_block = pl.ds(a * BLOCK, BLOCK)
         other = pl.ds((a % half) * BLOCK, BLOCK)
@@ -140,7 +141,8 @@
         m_ref[...] = _apply(m_ref[...], _weights(g_ref[gate_base + 2 * turn]))
         for t in range(n_blocks):
             o_ref[pl.ds(t, BLOCK, stride=n_blocks), :] = m_ref[pl.ds(t * width, width), :].T
-        table = tab_ref[turn]
+        tt_ref[...] = c_ref[cpl_base + turn].T
+        table = tt_ref[pl.ds(col_start, width), :]
         for a in range(n_blocks):
             m_ref[pl.ds(a * width, width), :] = o_ref[pl.ds(a * BLOCK, BLOCK), :].T * table
         m_ref[...] = _apply(m_ref[...], _weights(g_ref[gate_base + 2 * turn + 1]))
@@ -151,15 +153,20 @@
                 o_ref[pl.ds(a * BLOCK, BLOCK), :] = m_ref[pl.ds(a * width, width), :].T
 
 
-def final_layers(parity, cols, recv, gate_stack, tables, gate_base, cycles):
+def final_layers(scalars, cols, recv, gate_stack, coupling, gate_base, cpl_base, cycles):
     width, rows = cols.shape
+    kernel = functools.partial(_final_kernel, gate_base=gate_base, cpl_base=cpl_base, cycles=cycles)
     out = pl.pallas_call(
-        functools.partial(_final_kernel, gate_base=gate_base, cycles=cycles),
+        kernel,
         out_shape=jax.ShapeDtypeStruct((width, rows), cols.dtype),
         in_specs=[_smem(), _vmem(), _vmem(), _vmem(), _vmem()],
         out_specs=_vmem(),
-        scratch_shapes=[pltpu.VMEM((rows, width), jnp.float32), pltpu.VMEM((BLOCK, BLOCK), jnp.float32)],
-    )(parity, cols, recv, gate_stack, tables)
+        scratch_shapes=[
+            pltpu.VMEM((rows, width), jnp.float32),
+            pltpu.VMEM((BLOCK, BLOCK), jnp.float32),
+            pltpu.VMEM((BLOCK, BLOCK), jnp.float32),
+        ],
+    )(scalars, cols, recv, gate_stack, coupling)
     return out.T
 
 
@@ -269,11 +276,9 @@
     low = (lax.axis_index(BITS) & 1).astype(jnp.int32).reshape(1)
     outgoing = jnp.where(low[0] == 0, cols[:, half:], cols[:, :half])
     incoming = partner(outgoing, BITS, 0)
-    width = cols.shape[0]
-    col_start = lax.axis_index(CUTS) * width
     gate_base, cpl_base = 3 * CYC_A + 3 * CYC_B, CYC_A + CYC_B
-    tables = lax.dynamic_slice_in_dim(coupling[cpl_base:cpl_base + CYC_C], col_start, width, axis=2)
-    return final_layers(low, cols, incoming, gate_stack, jnp.swapaxes(tables, 1, 2), gate_base, CYC_C)
+    scalars = jnp.concatenate([low, lax.axis_index(CUTS).astype(jnp.int32).reshape(1)])
+    return final_layers(scalars, cols, incoming, gate_stack, coupling, gate_base, cpl_base, CYC_C)
 
 
 def solution(mesh):

time: 97.2 us -> 97 us (level)
    unnamed x7 -> x6, local copies, waits for them, and re-layouts: 2.14 us -> 1.41 us
  transfers between devices with their start and end apart: 3 -> 3, of which waited for: 2 -> 3; matrix products, arithmetic and copies ran while one was open for 1% -> 1% of each run, Pallas kernels for 0% -> 0%
where the time goes in v10:
time: 97 us; the launch traced here: 96.7 us
  starting transfers between devices  31 us (32%)
  Pallas kernels  28 us (29%)
  waiting for transfers between devices  20.3 us (21%)
  blocking collectives  14.4 us (15%)
  other arithmetic  1.44 us (1%)
  local copies, waits for them, and re-layouts  1.41 us (1%)
    all_to_all x1, starting transfers between devices, reduce_columns(): cols = lax.all_to_all(blocks, axis, 0, 0, tiled=False).sum(0)  16.3 us
    ppermute x2, starting transfers between devices, partner(): return lax.ppermute(value, axis, pairs)  14.7 us
    ppermute x2, waiting for transfers between devices, partner(): return lax.ppermute(value, axis, pairs)  14.7 us
    all_to_all x1, blocking collectives, reduce_columns(): cols = lax.all_to_all(blocks, axis, 0, 0, tiled=False).sum(0)  14.4 us
    pallas_call x1, Pallas kernels, group_b(): pl.pallas_call(functools.partial(_group_b_kernel, cycles=cycles), out_sha...  9.53 us
    pallas_call x1, Pallas kernels, group_a(): pl.pallas_call(functools.partial(_group_a_kernel, cycles=cycles), out_sha...  9.31 us
    pallas_call x1, Pallas kernels, final_layers(): pl.pallas_call(kernel, out_shape=jax.ShapeDtypeStruct((width, rows), cols...  9.17 us
    all_to_all x1, waiting for transfers between devices, reduce_columns(): cols = lax.all_to_all(blocks, axis, 0, 0, tiled=False).sum(0)  5.67 us
  transfers between devices with their start and end apart: 3, of which 3 were waited for; matrix products, arithmetic and copies ran while one was open for 1% of the time, Pallas kernels for 0%

profile of v10, /device:TPU:1, one launch (start us, length us, event | category | flops | bytes accessed | tf_op | source)
XLA Modules:
  0.0 96.7 jit_solution(382408162646910045)
XLA Ops:
  0.0 9.3 %shard_map.37 = (f32[1024,128]{1,0:T(8,128)}, f32[1024,128]{1,0:T(8,128)}) custom-call(s32[1]{0:T(128)} %bitcast.2.p_ref, f32[2048,128]{1,0:T(8,128)} %bitcast.8, f32[34,128,128]{2,1,0:T(8,128)} %g_ref.5, f32[13,128,128]{2,1,0:T(8,128)} %c_ref.5), custom_call_target="tpu_custom_call" | custom-call | tf_op jit(solution)/shard_map/pallas_call | solution.py:103
  9.3 8.5 %collective-permute-start = (f32[1024,128]{1,0:T(8,128)}, f32[1024,128]{1,0:T(8,128)S(1)}, u32[]{:S(2)}, u32[]{:S(2)}) collective-permute-start(f32[1024,128]{1,0:T(8,128)} %get-tuple-element.8), channel_id=1, source_target_pairs={{0,256},{16,272},{32,288},{48,304},{64,320},{80,336},{96,352},{112... | collective-permute-start | bytes 1572872 | tf_op jit(solution)/shard_map/ppermute | solution.py:179
  17.8 14.5 %collective-permute-done.recv_ref = f32[1024,128]{1,0:T(8,128)S(1)} collective-permute-done((f32[1024,128]{1,0:T(8,128)}, f32[1024,128]{1,0:T(8,128)S(1)}, u32[]{:S(2)}, u32[]{:S(2)}) %collective-permute-start) | collective-permute-done | bytes 524320 | tf_op jit(solution)/shard_map/ppermute | solution.py:179
  32.2 0.0 copy-start.1
  32.2 0.8 copy-done.1
  33.0 9.5 %shard_map.38 = f32[128,2048]{1,0:T(8,128)} custom-call(s32[1]{0:T(128)} %bitcast.2.p_ref, f32[1024,128]{1,0:T(8,128)} %get-tuple-element.7.keep_ref, f32[1024,128]{1,0:T(8,128)} %copy-done.1, f32[34,128,128]{2,1,0:T(8,128)} %g_ref.5, f32[13,128,128]{2,1,0:T(8,128)} %c_ref.5), custom_call_target="tpu_custom_call" | custom-call | tf_op jit(solution)/shard_map/pallas_call | solution.py:115
  42.6 14.4 %all_to_all.10 = f32[4,32,2048]{2,1,0:T(8,128)S(1)} all-to-all(f32[4,32,2048]{2,1,0:T(8,128)} %bitcast.7), channel_id=1, replica_groups=mesh['yh'=2,'z'=8,'core'=2,'x'=4,'yl'=4] {'x'}, dimensions={0} | all-to-all | bytes 2097152 | tf_op jit(solution)/shard_map/all_to_all | solution.py:253
  57.0 0.8 reduce_sum.18
  57.7 16.3 %all-to-all-start.1 = ((f32[4,8,2048]{2,1,0:T(8,128)}), f32[4,8,2048]{2,1,0:T(8,128)S(1)}, u32[]{:S(2)}, u32[]{:S(2)}) async-start(f32[4,8,2048]{2,1,0:T(8,128)} %bitcast.5), calls=%async_computation.1 | async-start | bytes 524288 | tf_op jit(solution)/shard_map/all_to_all | solution.py:253
  74.1 5.7 %all-to-all-done.1 = f32[4,8,2048]{2,1,0:T(8,128)S(1)} async-done(((f32[4,8,2048]{2,1,0:T(8,128)}), f32[4,8,2048]{2,1,0:T(8,128)S(1)}, u32[]{:S(2)}, u32[]{:S(2)}) %all-to-all-start.1) | async-done | bytes 262176 | tf_op jit(solution)/shard_map/all_to_all | solution.py:253
  79.7 0.0 copy-start
  79.8 6.3 %collective-permute-start.1 = (f32[8,1024]{1,0:T(8,128)S(1)}, f32[8,1024]{1,0:T(8,128)S(1)}, u32[]{:S(2)}, u32[]{:S(2)}) collective-permute-start(f32[8,1024]{1,0:T(8,128)S(1)} %slice_select_fusion), channel_id=1, source_target_pairs={{0,16},{16,0},{32,48},{48,32},{64,80},{80,64},{96,112},{112,96},{1... | collective-permute-start | bytes 98312 | tf_op jit(solution)/shard_map/ppermute | solution.py:179
  86.0 0.7 pad_add_fusion.p_ref
  86.7 0.2 collective-permute-done.1.recv_ref
  86.9 0.0 copy-done
  86.9 0.0 copy-start.2
  86.9 0.6 copy-done.2
  87.5 9.2 %shard_map.39 = f32[8,2048]{1,0:T(8,128)} custom-call(s32[2]{0:T(128)} %pad_add_fusion.p_ref, f32[8,2048]{1,0:T(8,128)} %copy-done, f32[8,1024]{1,0:T(8,128)} %copy-done.2, f32[34,128,128]{2,1,0:T(8,128)} %g_ref.5, f32[13,128,128]{2,1,0:T(8,128)} %c_ref.5), custom_call_target="tpu_custom_call" | custom-call | tf_op jit(solution)/shard_map/pallas_call | solution.py:159
  (2 shorter events, 0.0 us)
Async XLA Ops:
  9.3 22.9 %collective-permute-start = (f32[1024,128]{1,0:T(8,128)}, f32[1024,128]{1,0:T(8,128)S(1)}, u32[]{:S(2)}, u32[]{:S(2)}) collective-permute-start(f32[1024,128]{1,0:T(8,128)} %get-tuple-element.8), channel_id=1, source_target_pairs={{0,256},{16,272},{32,288},{48,304},{64,320},{80,336},{96,352},{112... | collective-permute-start | bytes 1572872 | tf_op jit(solution)/shard_map/ppermute | solution.py:179
  32.2 0.8 copy-start.1
  57.7 22.0 %all-to-all-start.1 = ((f32[4,8,2048]{2,1,0:T(8,128)}), f32[4,8,2048]{2,1,0:T(8,128)S(1)}, u32[]{:S(2)}, u32[]{:S(2)}) async-start(f32[4,8,2048]{2,1,0:T(8,128)} %bitcast.5), calls=%async_computation.1 | async-start | bytes 524288 | tf_op jit(solution)/shard_map/all_to_all | solution.py:253
  79.7 7.1 %copy-start = (f32[8,2048]{1,0:T(8,128)}, f32[8,2048]{1,0:T(8,128)S(1)}, u32[]{:S(2)}) copy-start(f32[8,2048]{1,0:T(8,128)S(1)} %reduce_sum.19.d_ref) | copy-start | bytes 196612
  79.8 7.1 %collective-permute-start.1 = (f32[8,1024]{1,0:T(8,128)S(1)}, f32[8,1024]{1,0:T(8,128)S(1)}, u32[]{:S(2)}, u32[]{:S(2)}) collective-permute-start(f32[8,1024]{1,0:T(8,128)S(1)} %slice_select_fusion), channel_id=1, source_target_pairs={{0,16},{16,0},{32,48},{48,32},{64,80},{80,64},{96,112},{112,96},{1... | collective-permute-start | bytes 98312 | tf_op jit(solution)/shard_map/ppermute | solution.py:179
  86.9 0.6 copy-start.2

commit v11 on v10

--- a/solution.py
+++ b/solution.py
@@ -122,19 +122,24 @@
     )(parity, keep, recv, gate_stack, coupling)
 
 
-def _final_kernel(p_ref, d_ref, recv_ref, g_ref, c_ref, out_ref, o_ref, m_ref, tt_ref, *, gate_base, cpl_base, cycles):
+def _final_kernel(p_ref, cut_ref, d_ref, recv_hbm, g_ref, c_ref, out_ref, o_ref, m_ref, tt_ref, rv_ref, sem, *,
+                  gate_base, cpl_base, cycles):
     width = d_ref.shape[0]
     n_blocks = d_ref.shape[1] // BLOCK
     half = n_blocks // 2
+    half_rows = half * BLOCK
     p = p_ref[0]
-    col_start = pl.multiple_of(p_ref[1] * width, width)
-    for a in range(n_blocks):
-        lane_block = pl.ds(a * BLOCK, BLOCK)
-        other = pl.ds((a % half) * BLOCK, BLOCK)
-        own = d_ref[:, lane_block]
-        got = recv_ref[:, other]
-        keep = (a // half) == p
-        o_ref[lane_block, :] = jnp.where(keep, own, got).T
+    col_start = pl.multiple_of(cut_ref[0] * width, width)
+    fetch = pltpu.make_async_copy(recv_hbm, rv_ref, sem)
+    fetch.start()
+    own_at = pl.multiple_of(p * half_rows, half_rows)
+    got_at = pl.multiple_of((1 - p) * half_rows, half_rows)
+    for a in range(half):
+        lanes = pl.ds(pl.multiple_of(own_at + a * BLOCK, BLOCK), BLOCK)
+        o_ref[pl.ds(pl.multiple_of(own_at + a * BLOCK, BLOCK), BLOCK), :] = d_ref[:, lanes].T
+    fetch.wait()
+    for a in range(half):
+        o_ref[pl.ds(pl.multiple_of(got_at + a * BLOCK, BLOCK), BLOCK), :] = rv_ref[:, pl.ds(a * BLOCK, BLOCK)].T
     for turn in range(cycles):
         for t in range(n_blocks):
             m_ref[pl.ds(t * width, width), :] = o_ref[pl.ds(t, BLOCK, stride=n_blocks), :].T
@@ -153,20 +158,22 @@
                 o_ref[pl.ds(a * BLOCK, BLOCK), :] = m_ref[pl.ds(a * width, width), :].T
 
 
-def final_layers(scalars, cols, recv, gate_stack, coupling, gate_base, cpl_base, cycles):
+def final_layers(parity, cut, cols, recv, gate_stack, coupling, gate_base, cpl_base, cycles):
     width, rows = cols.shape
     kernel = functools.partial(_final_kernel, gate_base=gate_base, cpl_base=cpl_base, cycles=cycles)
     out = pl.pallas_call(
         kernel,
         out_shape=jax.ShapeDtypeStruct((width, rows), cols.dtype),
-        in_specs=[_smem(), _vmem(), _vmem(), _vmem(), _vmem()],
+        in_specs=[_smem(), _smem(), _vmem(), pl.BlockSpec(memory_space=pl.ANY), _vmem(), _vmem()],
         out_specs=_vmem(),
         scratch_shapes=[
             pltpu.VMEM((rows, width), jnp.float32),
             pltpu.VMEM((BLOCK, BLOCK), jnp.float32),
             pltpu.VMEM((BLOCK, BLOCK), jnp.float32),
+            pltpu.VMEM(recv.shape, jnp.float32),
+            pltpu.SemaphoreType.DMA(()),
         ],
-    )(scalars, cols, recv, gate_stack, coupling)
+    )(parity, cut, cols, recv, gate_stack, coupling)
     return out.T
 
 
@@ -277,8 +284,8 @@
     outgoing = jnp.where(low[0] == 0, cols[:, half:], cols[:, :half])
     incoming = partner(outgoing, BITS, 0)
     gate_base, cpl_base = 3 * CYC_A + 3 * CYC_B, CYC_A + CYC_B
-    scalars = jnp.concatenate([low, lax.axis_index(CUTS).astype(jnp.int32).reshape(1)])
-    return final_layers(scalars, cols, incoming, gate_stack, coupling, gate_base, cpl_base, CYC_C)
+    cut = lax.axis_index(CUTS).astype(jnp.int32).reshape(1)
+    return final_layers(low, cut, cols, incoming, gate_stack, coupling, gate_base, cpl_base, CYC_C)
 
 
 def solution(mesh):

time: 97 us -> 97.9 us (level)
  transfers between devices with their start and end apart: 3 -> 3, of which waited for: 3 -> 3; matrix products, arithmetic and copies ran while one was open for 1% -> 0% of each run, Pallas kernels for 0% -> 0%
where the time goes in v11:
time: 97.9 us; the launch traced here: 97.5 us
  starting transfers between devices  31.3 us (32%)
  Pallas kernels  28.6 us (29%)
  waiting for transfers between devices  20.8 us (21%)
  blocking collectives  14.4 us (15%)
  local copies, waits for them, and re-layouts  1.41 us (1%)
    all_to_all x1, starting transfers between devices, reduce_columns(): cols = lax.all_to_all(blocks, axis, 0, 0, tiled=False).sum(0)  16.3 us
    ppermute x2, waiting for transfers between devices, partner(): return lax.ppermute(value, axis, pairs)  15.1 us
    ppermute x2, starting transfers between devices, partner(): return lax.ppermute(value, axis, pairs)  14.9 us
    all_to_all x1, blocking collectives, reduce_columns(): cols = lax.all_to_all(blocks, axis, 0, 0, tiled=False).sum(0)  14.4 us
    pallas_call x1, Pallas kernels, final_layers(): pl.pallas_call(kernel, out_shape=jax.ShapeDtypeStruct((width, rows), cols...  9.79 us
    pallas_call x1, Pallas kernels, group_b(): pl.pallas_call(functools.partial(_group_b_kernel, cycles=cycles), out_sha...  9.53 us
    pallas_call x1, Pallas kernels, group_a(): pl.pallas_call(functools.partial(_group_a_kernel, cycles=cycles), out_sha...  9.31 us
    all_to_all x1, waiting for transfers between devices, reduce_columns(): cols = lax.all_to_all(blocks, axis, 0, 0, tiled=False).sum(0)  5.67 us
  transfers between devices with their start and end apart: 3, of which 3 were waited for; matrix products, arithmetic and copies ran while one was open for 0% of the time, Pallas kernels for 0%

profile of v11, /device:TPU:1, one launch (start us, length us, event | category | flops | bytes accessed | tf_op | source)
XLA Modules:
  0.0 97.5 jit_solution(11032568146531576972)
XLA Ops:
  0.0 9.3 %shard_map.37 = (f32[1024,128]{1,0:T(8,128)}, f32[1024,128]{1,0:T(8,128)}) custom-call(s32[1]{0:T(128)} %bitcast.2.p_ref, f32[2048,128]{1,0:T(8,128)} %bitcast.8, f32[34,128,128]{2,1,0:T(8,128)} %g_ref.5, f32[13,128,128]{2,1,0:T(8,128)} %c_ref.5), custom_call_target="tpu_custom_call" | custom-call | tf_op jit(solution)/shard_map/pallas_call | solution.py:103
  9.3 8.5 %collective-permute-start = (f32[1024,128]{1,0:T(8,128)}, f32[1024,128]{1,0:T(8,128)S(1)}, u32[]{:S(2)}, u32[]{:S(2)}) collective-permute-start(f32[1024,128]{1,0:T(8,128)} %get-tuple-element.8), channel_id=1, source_target_pairs={{0,256},{16,272},{32,288},{48,304},{64,320},{80,336},{96,352},{112... | collective-permute-start | bytes 1572872 | tf_op jit(solution)/shard_map/ppermute | solution.py:186
  17.8 14.5 %collective-permute-done.recv_ref = f32[1024,128]{1,0:T(8,128)S(1)} collective-permute-done((f32[1024,128]{1,0:T(8,128)}, f32[1024,128]{1,0:T(8,128)S(1)}, u32[]{:S(2)}, u32[]{:S(2)}) %collective-permute-start) | collective-permute-done | bytes 524320 | tf_op jit(solution)/shard_map/ppermute | solution.py:186
  32.2 0.0 copy-start.1
  32.2 0.8 copy-done.1
  33.0 9.5 %shard_map.38 = f32[128,2048]{1,0:T(8,128)} custom-call(s32[1]{0:T(128)} %bitcast.2.p_ref, f32[1024,128]{1,0:T(8,128)} %get-tuple-element.7.keep_ref, f32[1024,128]{1,0:T(8,128)} %copy-done.1, f32[34,128,128]{2,1,0:T(8,128)} %g_ref.5, f32[13,128,128]{2,1,0:T(8,128)} %c_ref.5), custom_call_target="tpu_custom_call" | custom-call | tf_op jit(solution)/shard_map/pallas_call | solution.py:115
  42.6 14.4 %all_to_all.10 = f32[4,32,2048]{2,1,0:T(8,128)S(1)} all-to-all(f32[4,32,2048]{2,1,0:T(8,128)} %bitcast.7), channel_id=1, replica_groups=mesh['yh'=2,'z'=8,'core'=2,'x'=4,'yl'=4] {'x'}, dimensions={0} | all-to-all | bytes 2097152 | tf_op jit(solution)/shard_map/all_to_all | solution.py:260
  57.0 0.8 reduce_sum.18
  57.7 16.3 %all-to-all-start.1 = ((f32[4,8,2048]{2,1,0:T(8,128)}), f32[4,8,2048]{2,1,0:T(8,128)S(1)}, u32[]{:S(2)}, u32[]{:S(2)}) async-start(f32[4,8,2048]{2,1,0:T(8,128)} %bitcast.5), calls=%async_computation.1 | async-start | bytes 524288 | tf_op jit(solution)/shard_map/all_to_all | solution.py:260
  74.1 5.7 %all-to-all-done.1 = f32[4,8,2048]{2,1,0:T(8,128)S(1)} async-done(((f32[4,8,2048]{2,1,0:T(8,128)}), f32[4,8,2048]{2,1,0:T(8,128)S(1)}, u32[]{:S(2)}, u32[]{:S(2)}) %all-to-all-start.1) | async-done | bytes 262176 | tf_op jit(solution)/shard_map/all_to_all | solution.py:260
  79.7 0.0 copy-start
  79.8 6.5 %collective-permute-start.1 = (f32[8,1024]{1,0:T(8,128)S(1)}, f32[8,1024]{1,0:T(8,128)S(1)}, u32[]{:S(2)}, u32[]{:S(2)}) collective-permute-start(f32[8,1024]{1,0:T(8,128)S(1)} %slice_select_fusion), channel_id=1, source_target_pairs={{0,16},{16,0},{32,48},{48,32},{64,80},{80,64},{96,112},{112,96},{1... | collective-permute-start | bytes 98312 | tf_op jit(solution)/shard_map/ppermute | solution.py:186
  86.3 0.6 collective-permute-done.1.recv_hbm
  86.9 0.0 copy-start.2
  86.9 0.0 copy-done
  86.9 0.6 copy-done.2
  87.5 9.8 %shard_map.39 = f32[8,2048]{1,0:T(8,128)} custom-call(s32[1]{0:T(128)} %bitcast.p_ref, s32[1]{0:T(128)} %bitcast.1.cut_ref, f32[8,2048]{1,0:T(8,128)} %copy-done, f32[8,1024]{1,0:T(8,128)} %copy-done.2, f32[34,128,128]{2,1,0:T(8,128)} %g_ref.5, f32[13,128,128]{2,1,0:T(8,128)} %c_ref.5), custom_call_target="tpu_custom_call" | custom-call | tf_op jit(solution)/shard_map/pallas_call | solution.py:164
  (2 shorter events, 0.0 us)
Async XLA Ops:
  9.3 22.9 %collective-permute-start = (f32[1024,128]{1,0:T(8,128)}, f32[1024,128]{1,0:T(8,128)S(1)}, u32[]{:S(2)}, u32[]{:S(2)}) collective-permute-start(f32[1024,128]{1,0:T(8,128)} %get-tuple-element.8), channel_id=1, source_target_pairs={{0,256},{16,272},{32,288},{48,304},{64,320},{80,336},{96,352},{112... | collective-permute-start | bytes 1572872 | tf_op jit(solution)/shard_map/ppermute | solution.py:186
  32.2 0.8 copy-start.1
  57.7 22.0 %all-to-all-start.1 = ((f32[4,8,2048]{2,1,0:T(8,128)}), f32[4,8,2048]{2,1,0:T(8,128)S(1)}, u32[]{:S(2)}, u32[]{:S(2)}) async-start(f32[4,8,2048]{2,1,0:T(8,128)} %bitcast.5), calls=%async_computation.1 | async-start | bytes 524288 | tf_op jit(solution)/shard_map/all_to_all | solution.py:260
  79.7 7.1 %copy-start = (f32[8,2048]{1,0:T(8,128)}, f32[8,2048]{1,0:T(8,128)S(1)}, u32[]{:S(2)}) copy-start(f32[8,2048]{1,0:T(8,128)S(1)} %reduce_sum.19.d_ref) | copy-start | bytes 196612
  79.8 7.1 %collective-permute-start.1 = (f32[8,1024]{1,0:T(8,128)S(1)}, f32[8,1024]{1,0:T(8,128)S(1)}, u32[]{:S(2)}, u32[]{:S(2)}) collective-permute-start(f32[8,1024]{1,0:T(8,128)S(1)} %slice_select_fusion), channel_id=1, source_target_pairs={{0,16},{16,0},{32,48},{48,32},{64,80},{80,64},{96,112},{112,96},{1... | collective-permute-start | bytes 98312 | tf_op jit(solution)/shard_map/ppermute | solution.py:186
  86.9 0.6 copy-start.2

commit v12 on v11

--- a/solution.py
+++ b/solution.py
@@ -55,15 +55,15 @@
         for t in range(n_blocks):
             o_ref[pl.ds(t, BLOCK, stride=n_blocks), :] = ys[:, t * BLOCK:(t + 1) * BLOCK]
         y = _apply(o_ref[...], _weights(g_ref[first + 1]))
-        o_ref[...] = (y.reshape(n_blocks, BLOCK, -1) * table[None]).reshape(y.shape)
+        y = (y.reshape(n_blocks, BLOCK, -1) * table[None]).reshape(y.shape)
         if last_to is not None and turn == cycles - 1:
             for a in range(n_blocks):
-                t_ref[pl.ds(a * BLOCK, BLOCK), :] = o_ref[pl.ds(a * BLOCK, BLOCK), :].T
+                t_ref[pl.ds(a * BLOCK, BLOCK), :] = y[a * BLOCK:(a + 1) * BLOCK].T
             t_ref[...] = _apply(t_ref[...], _weights(g_ref[first + 2]))
             for a in range(n_blocks):
                 last_to[:, pl.ds(a * BLOCK, BLOCK)] = t_ref[pl.ds(a * BLOCK, BLOCK), :]
         else:
-            xs = jnp.concatenate([o_ref[pl.ds(a * BLOCK, BLOCK), :] for a in range(n_blocks)], axis=1)
+            xs = jnp.concatenate([y[a * BLOCK:(a + 1) * BLOCK] for a in range(n_blocks)], axis=1)
             ys = _apply_left(_weights_left(g_ref[first + 2]), xs)
             for a in range(n_blocks):
                 o_ref[pl.ds(a * BLOCK, BLOCK), :] = ys[:, a * BLOCK:(a + 1) * BLOCK]

time: 97.9 us -> 98 us (level)
  no operation moved by 1% of the time
where the time goes in v12:
time: 98 us; the launch traced here: 97.6 us
  starting transfers between devices  31.3 us (32%)
  Pallas kernels  28.7 us (29%)
  waiting for transfers between devices  20.7 us (21%)
  blocking collectives  14.4 us (15%)
  local copies, waits for them, and re-layouts  1.41 us (1%)
    all_to_all x1, starting transfers between devices, reduce_columns(): cols = lax.all_to_all(blocks, axis, 0, 0, tiled=False).sum(0)  16.3 us
    ppermute x2, waiting for transfers between devices, partner(): return lax.ppermute(value, axis, pairs)  15.1 us
    ppermute x2, starting transfers between devices, partner(): return lax.ppermute(value, axis, pairs)  14.9 us
    all_to_all x1, blocking collectives, reduce_columns(): cols = lax.all_to_all(blocks, axis, 0, 0, tiled=False).sum(0)  14.4 us
    pallas_call x1, Pallas kernels, final_layers(): pl.pallas_call(kernel, out_shape=jax.ShapeDtypeStruct((width, rows), cols...  9.79 us
    pallas_call x1, Pallas kernels, group_b(): pl.pallas_call(functools.partial(_group_b_kernel, cycles=cycles), out_sha...  9.55 us
    pallas_call x1, Pallas kernels, group_a(): pl.pallas_call(functools.partial(_group_a_kernel, cycles=cycles), out_sha...  9.38 us
    all_to_all x1, waiting for transfers between devices, reduce_columns(): cols = lax.all_to_all(blocks, axis, 0, 0, tiled=False).sum(0)  5.67 us
  transfers between devices with their start and end apart: 3, of which 3 were waited for; matrix products, arithmetic and copies ran while one was open for 0% of the time, Pallas kernels for 0%

profile of v12, /device:TPU:1, one launch (start us, length us, event | category | flops | bytes accessed | tf_op | source)
XLA Modules:
  0.0 97.6 jit_solution(10680611100196890507)
XLA Ops:
  0.0 9.4 %shard_map.37 = (f32[1024,128]{1,0:T(8,128)}, f32[1024,128]{1,0:T(8,128)}) custom-call(s32[1]{0:T(128)} %bitcast.2.p_ref, f32[2048,128]{1,0:T(8,128)} %bitcast.8, f32[34,128,128]{2,1,0:T(8,128)} %g_ref.5, f32[13,128,128]{2,1,0:T(8,128)} %c_ref.5), custom_call_target="tpu_custom_call" | custom-call | tf_op jit(solution)/shard_map/pallas_call | solution.py:103
  9.4 8.5 %collective-permute-start = (f32[1024,128]{1,0:T(8,128)}, f32[1024,128]{1,0:T(8,128)S(1)}, u32[]{:S(2)}, u32[]{:S(2)}) collective-permute-start(f32[1024,128]{1,0:T(8,128)} %get-tuple-element.8), channel_id=1, source_target_pairs={{0,256},{16,272},{32,288},{48,304},{64,320},{80,336},{96,352},{112... | collective-permute-start | bytes 1572872 | tf_op jit(solution)/shard_map/ppermute | solution.py:186
  17.8 14.4 %collective-permute-done.recv_ref = f32[1024,128]{1,0:T(8,128)S(1)} collective-permute-done((f32[1024,128]{1,0:T(8,128)}, f32[1024,128]{1,0:T(8,128)S(1)}, u32[]{:S(2)}, u32[]{:S(2)}) %collective-permute-start) | collective-permute-done | bytes 524320 | tf_op jit(solution)/shard_map/ppermute | solution.py:186
  32.3 0.0 copy-start.1
  32.3 0.8 copy-done.1
  33.1 9.6 %shard_map.38 = f32[128,2048]{1,0:T(8,128)} custom-call(s32[1]{0:T(128)} %bitcast.2.p_ref, f32[1024,128]{1,0:T(8,128)} %get-tuple-element.7.keep_ref, f32[1024,128]{1,0:T(8,128)} %copy-done.1, f32[34,128,128]{2,1,0:T(8,128)} %g_ref.5, f32[13,128,128]{2,1,0:T(8,128)} %c_ref.5), custom_call_target="tpu_custom_call" | custom-call | tf_op jit(solution)/shard_map/pallas_call | solution.py:115
  42.6 14.4 %all_to_all.10 = f32[4,32,2048]{2,1,0:T(8,128)S(1)} all-to-all(f32[4,32,2048]{2,1,0:T(8,128)} %bitcast.7), channel_id=1, replica_groups=mesh['yh'=2,'z'=8,'core'=2,'x'=4,'yl'=4] {'x'}, dimensions={0} | all-to-all | bytes 2097152 | tf_op jit(solution)/shard_map/all_to_all | solution.py:260
  57.1 0.8 reduce_sum.18
  57.8 16.3 %all-to-all-start.1 = ((f32[4,8,2048]{2,1,0:T(8,128)}), f32[4,8,2048]{2,1,0:T(8,128)S(1)}, u32[]{:S(2)}, u32[]{:S(2)}) async-start(f32[4,8,2048]{2,1,0:T(8,128)} %bitcast.5), calls=%async_computation.1 | async-start | bytes 524288 | tf_op jit(solution)/shard_map/all_to_all | solution.py:260
  74.2 5.7 %all-to-all-done.1 = f32[4,8,2048]{2,1,0:T(8,128)S(1)} async-done(((f32[4,8,2048]{2,1,0:T(8,128)}), f32[4,8,2048]{2,1,0:T(8,128)S(1)}, u32[]{:S(2)}, u32[]{:S(2)}) %all-to-all-start.1) | async-done | bytes 262176 | tf_op jit(solution)/shard_map/all_to_all | solution.py:260
  79.8 0.0 copy-start
  79.9 6.5 %collective-permute-start.1 = (f32[8,1024]{1,0:T(8,128)S(1)}, f32[8,1024]{1,0:T(8,128)S(1)}, u32[]{:S(2)}, u32[]{:S(2)}) collective-permute-start(f32[8,1024]{1,0:T(8,128)S(1)} %slice_select_fusion), channel_id=1, source_target_pairs={{0,16},{16,0},{32,48},{48,32},{64,80},{80,64},{96,112},{112,96},{1... | collective-permute-start | bytes 98312 | tf_op jit(solution)/shard_map/ppermute | solution.py:186
  86.4 0.6 collective-permute-done.1.recv_hbm
  87.0 0.0 copy-start.2
  87.0 0.0 copy-done
  87.0 0.6 copy-done.2
  87.6 9.8 %shard_map.39 = f32[8,2048]{1,0:T(8,128)} custom-call(s32[1]{0:T(128)} %bitcast.p_ref, s32[1]{0:T(128)} %bitcast.1.cut_ref, f32[8,2048]{1,0:T(8,128)} %copy-done, f32[8,1024]{1,0:T(8,128)} %copy-done.2, f32[34,128,128]{2,1,0:T(8,128)} %g_ref.5, f32[13,128,128]{2,1,0:T(8,128)} %c_ref.5), custom_call_target="tpu_custom_call" | custom-call | tf_op jit(solution)/shard_map/pallas_call | solution.py:164
  (2 shorter events, 0.0 us)
Async XLA Ops:
  9.4 22.9 %collective-permute-start = (f32[1024,128]{1,0:T(8,128)}, f32[1024,128]{1,0:T(8,128)S(1)}, u32[]{:S(2)}, u32[]{:S(2)}) collective-permute-start(f32[1024,128]{1,0:T(8,128)} %get-tuple-element.8), channel_id=1, source_target_pairs={{0,256},{16,272},{32,288},{48,304},{64,320},{80,336},{96,352},{112... | collective-permute-start | bytes 1572872 | tf_op jit(solution)/shard_map/ppermute | solution.py:186
  32.3 0.8 copy-start.1
  57.8 22.0 %all-to-all-start.1 = ((f32[4,8,2048]{2,1,0:T(8,128)}), f32[4,8,2048]{2,1,0:T(8,128)S(1)}, u32[]{:S(2)}, u32[]{:S(2)}) async-start(f32[4,8,2048]{2,1,0:T(8,128)} %bitcast.5), calls=%async_computation.1 | async-start | bytes 524288 | tf_op jit(solution)/shard_map/all_to_all | solution.py:260
  79.8 7.1 %copy-start = (f32[8,2048]{1,0:T(8,128)}, f32[8,2048]{1,0:T(8,128)S(1)}, u32[]{:S(2)}) copy-start(f32[8,2048]{1,0:T(8,128)S(1)} %reduce_sum.19.d_ref) | copy-start | bytes 196612
  79.9 7.1 %collective-permute-start.1 = (f32[8,1024]{1,0:T(8,128)S(1)}, f32[8,1024]{1,0:T(8,128)S(1)}, u32[]{:S(2)}, u32[]{:S(2)}) collective-permute-start(f32[8,1024]{1,0:T(8,128)S(1)} %slice_select_fusion), channel_id=1, source_target_pairs={{0,16},{16,0},{32,48},{48,32},{64,80},{80,64},{96,112},{112,96},{1... | collective-permute-start | bytes 98312 | tf_op jit(solution)/shard_map/ppermute | solution.py:186
  87.0 0.6 copy-start.2

commit v13 on v7

--- a/solution.py
+++ b/solution.py
@@ -78,11 +78,13 @@
     send_ref[...] = o_ref[pl.ds(pl.multiple_of((1 - p) * half, half), half), :]
 
 
-def _group_b_kernel(p_ref, keep_ref, recv_ref, g_ref, c_ref, out_ref, o_ref, t_ref, *, cycles):
+def _group_b_kernel(p_ref, keep_ref, recv_hbm, g_ref, c_ref, out_ref, o_ref, t_ref, sem, *, cycles):
     half = keep_ref.shape[0]
     p = p_ref[0]
+    fetch = pltpu.make_async_copy(recv_hbm, o_ref.at[pl.ds(pl.multiple_of((1 - p) * half, half), half), :], sem)
+    fetch.start()
     o_ref[pl.ds(pl.multiple_of(p * half, half), half), :] = keep_ref[...]
-    o_ref[pl.ds(pl.multiple_of((1 - p) * half, half), half), :] = recv_ref[...]
+    fetch.wait()
     _layer_turns(o_ref, t_ref, g_ref, c_ref, cycles, last_to=out_ref)
 
 
@@ -116,9 +118,14 @@
         functools.partial(_group_b_kernel, cycles=cycles),
         out_shape=jax.ShapeDtypeStruct((cols, rows), keep.dtype),
         grid=(1,),
-        in_specs=[_smem(), _vmem(), _vmem(), _stack_block(3 * cycles, 1), _stack_block(cycles, 1)],
+        in_specs=[_smem(), _vmem(), pl.BlockSpec(memory_space=pltpu.HBM), _stack_block(3 * cycles, 1),
+                  _stack_block(cycles, 1)],
         out_specs=_vmem(),
-        scratch_shapes=[pltpu.VMEM((rows, cols), jnp.float32), pltpu.VMEM((rows, cols), jnp.float32)],
+        scratch_shapes=[
+            pltpu.VMEM((rows, cols), jnp.float32),
+            pltpu.VMEM((rows, cols), jnp.float32),
+            pltpu.SemaphoreType.DMA(()),
+        ],
     )(parity, keep, recv, gate_stack, coupling)
 
 

time: 97.1 us -> 98 us (level)
  no operation moved by 1% of the time
where the time goes in v13:
time: 98 us; the launch traced here: 97.6 us
  starting transfers between devices  31.3 us (32%)
  Pallas kernels  28.5 us (29%)
  waiting for transfers between devices  20.2 us (21%)
  blocking collectives  14.5 us (15%)
  local copies, waits for them, and re-layouts  1.68 us (2%)
  other arithmetic  1.41 us (1%)
    all_to_all x1, starting transfers between devices, reduce_columns(): cols = lax.all_to_all(blocks, axis, 0, 0, tiled=False).sum(0)  16.3 us
    ppermute x2, starting transfers between devices, partner(): return lax.ppermute(value, axis, pairs)  14.9 us
    all_to_all x1, blocking collectives, reduce_columns(): cols = lax.all_to_all(blocks, axis, 0, 0, tiled=False).sum(0)  14.5 us
    ppermute x2, waiting for transfers between devices, partner(): return lax.ppermute(value, axis, pairs)  14.5 us
    pallas_call x1, Pallas kernels, group_b(): pl.pallas_call(functools.partial(_group_b_kernel, cycles=cycles), out_sha...  10.4 us
    pallas_call x1, Pallas kernels, group_a(): pl.pallas_call(functools.partial(_group_a_kernel, cycles=cycles), out_sha...  9.3 us
    pallas_call x1, Pallas kernels, final_layers(): pl.pallas_call(kernel, out_shape=jax.ShapeDtypeStruct((width, rows), d.dt...  8.82 us
    all_to_all x1, waiting for transfers between devices, reduce_columns(): cols = lax.all_to_all(blocks, axis, 0, 0, tiled=False).sum(0)  5.67 us
  transfers between devices with their start and end apart: 3, of which 2 were waited for; matrix products, arithmetic and copies ran while one was open for 1% of the time, Pallas kernels for 0%

profile of v13, /device:TPU:1, one launch (start us, length us, event | category | flops | bytes accessed | tf_op | source)
XLA Modules:
  0.0 97.6 jit_solution(6242363514471856387)
XLA Ops:
  0.0 9.3 %shard_map.37 = (f32[1024,128]{1,0:T(8,128)}, f32[1024,128]{1,0:T(8,128)}) custom-call(s32[1]{0:T(128)} %bitcast.p_ref, f32[2048,128]{1,0:T(8,128)} %bitcast.7, f32[34,128,128]{2,1,0:T(8,128)} %g_ref.5, f32[13,128,128]{2,1,0:T(8,128)} %c_ref.3), custom_call_target="tpu_custom_call" | custom-call | tf_op jit(solution)/shard_map/pallas_call | solution.py:105
  9.3 8.5 %collective-permute-start = (f32[1024,128]{1,0:T(8,128)}, f32[1024,128]{1,0:T(8,128)S(1)}, u32[]{:S(2)}, u32[]{:S(2)}) collective-permute-start(f32[1024,128]{1,0:T(8,128)} %get-tuple-element.8), channel_id=1, source_target_pairs={{0,256},{16,272},{32,288},{48,304},{64,320},{80,336},{96,352},{112... | collective-permute-start | bytes 1572872 | tf_op jit(solution)/shard_map/ppermute | solution.py:171
  17.8 14.5 %collective-permute-done.recv_hbm = f32[1024,128]{1,0:T(8,128)S(1)} collective-permute-done((f32[1024,128]{1,0:T(8,128)}, f32[1024,128]{1,0:T(8,128)S(1)}, u32[]{:S(2)}, u32[]{:S(2)}) %collective-permute-start) | collective-permute-done | bytes 524320 | tf_op jit(solution)/shard_map/ppermute | solution.py:171
  32.2 0.0 copy-start
  32.2 0.8 copy-done
  33.0 10.4 %shard_map.38 = f32[128,2048]{1,0:T(8,128)} custom-call(s32[1]{0:T(128)} %bitcast.p_ref, f32[1024,128]{1,0:T(8,128)} %get-tuple-element.7.keep_ref, f32[1024,128]{1,0:T(8,128)} %copy-done, f32[34,128,128]{2,1,0:T(8,128)} %g_ref.5, f32[13,128,128]{2,1,0:T(8,128)} %c_ref.3), custom_call_target="tpu_custom_call" | custom-call | tf_op jit(solution)/shard_map/pallas_call | solution.py:117
  43.4 0.0 slice-start
  43.4 14.5 %all_to_all.10 = f32[4,32,2048]{2,1,0:T(8,128)S(1)} all-to-all(f32[4,32,2048]{2,1,0:T(8,128)} %bitcast.6), channel_id=1, replica_groups=mesh['yh'=2,'z'=8,'core'=2,'x'=4,'yl'=4] {'x'}, dimensions={0} | all-to-all | bytes 2097152 | tf_op jit(solution)/shard_map/all_to_all | solution.py:245
  57.9 0.8 reduce_sum.18
  58.7 16.3 %all-to-all-start.1 = ((f32[4,8,2048]{2,1,0:T(8,128)}), f32[4,8,2048]{2,1,0:T(8,128)S(1)}, u32[]{:S(2)}, u32[]{:S(2)}) async-start(f32[4,8,2048]{2,1,0:T(8,128)} %bitcast.3), calls=%async_computation.1 | async-start | bytes 524288 | tf_op jit(solution)/shard_map/all_to_all | solution.py:245
  75.0 5.7 %all-to-all-done.1 = f32[4,8,2048]{2,1,0:T(8,128)S(1)} async-done(((f32[4,8,2048]{2,1,0:T(8,128)}), f32[4,8,2048]{2,1,0:T(8,128)S(1)}, u32[]{:S(2)}, u32[]{:S(2)}) %all-to-all-start.1) | async-done | bytes 262176 | tf_op jit(solution)/shard_map/all_to_all | solution.py:245
  80.7 6.5 %collective-permute-start.1 = (f32[8,1024]{1,0:T(8,128)S(1)}, f32[8,1024]{1,0:T(8,128)S(1)}, u32[]{:S(2)}, u32[]{:S(2)}) collective-permute-start(f32[8,1024]{1,0:T(8,128)S(1)} %get-tuple-element.10), channel_id=1, source_target_pairs={{0,16},{16,0},{32,48},{48,32},{64,80},{80,64},{96,112},{112,96},{1... | collective-permute-start | bytes 98312 | tf_op jit(solution)/shard_map/ppermute | solution.py:171
  87.2 0.0 slice-done
  87.2 0.1 constant_dynamic-slice_fusion
  87.4 0.7 copy.7
  88.1 0.0 collective-permute-done.1
  88.1 0.6 maximum_select_fusion.d_ref
  88.8 8.8 %shard_map.39 = f32[8,2048]{1,0:T(8,128)} custom-call(f32[8,2048]{1,0:T(8,128)} %maximum_select_fusion.d_ref, f32[34,128,128]{2,1,0:T(8,128)} %g_ref.5, f32[5,8,128]{2,1,0:T(8,128)} %bitcast.8), custom_call_target="tpu_custom_call" | custom-call | tf_op jit(solution)/shard_map/pallas_call | solution.py:157
  (2 shorter events, 0.0 us)
Async XLA Ops:
  9.3 22.9 %collective-permute-start = (f32[1024,128]{1,0:T(8,128)}, f32[1024,128]{1,0:T(8,128)S(1)}, u32[]{:S(2)}, u32[]{:S(2)}) collective-permute-start(f32[1024,128]{1,0:T(8,128)} %get-tuple-element.8), channel_id=1, source_target_pairs={{0,256},{16,272},{32,288},{48,304},{64,320},{80,336},{96,352},{112... | collective-permute-start | bytes 1572872 | tf_op jit(solution)/shard_map/ppermute | solution.py:171
  32.2 0.8 copy-start
  43.4 43.8 %slice-start = ((f32[13,128,128]{2,1,0:T(8,128)}), f32[5,128,128]{2,1,0:T(8,128)S(1)}, s32[]{:S(2)}) async-start(f32[13,128,128]{2,1,0:T(8,128)} %c_ref.3), calls=%async_computation.2 | async-start | bytes 655360 | tf_op jit(solution)/shard_map/slice | solution.py:271
  58.7 22.0 %all-to-all-start.1 = ((f32[4,8,2048]{2,1,0:T(8,128)}), f32[4,8,2048]{2,1,0:T(8,128)S(1)}, u32[]{:S(2)}, u32[]{:S(2)}) async-start(f32[4,8,2048]{2,1,0:T(8,128)} %bitcast.3), calls=%async_computation.1 | async-start | bytes 524288 | tf_op jit(solution)/shard_map/all_to_all | solution.py:245
  80.7 7.4 %collective-permute-start.1 = (f32[8,1024]{1,0:T(8,128)S(1)}, f32[8,1024]{1,0:T(8,128)S(1)}, u32[]{:S(2)}, u32[]{:S(2)}) collective-permute-start(f32[8,1024]{1,0:T(8,128)S(1)} %get-tuple-element.10), channel_id=1, source_target_pairs={{0,16},{16,0},{32,48},{48,32},{64,80},{80,64},{96,112},{112,96},{1... | collective-permute-start | bytes 98312 | tf_op jit(solution)/shard_map/ppermute | solution.py:171

commit v14 on v7

--- a/solution.py
+++ b/solution.py
@@ -256,13 +256,14 @@
     parity = (lax.axis_index(BITS) >> top_bit & 1).astype(jnp.int32).reshape(1)
     keep, send = group_a(parity, boundary[0], gate_stack, coupling, CYC_A)
     recv = partner(send, BITS, top_bit)
-    cols = group_b(parity, keep, recv, gate_stack, coupling, CYC_B)
-    cols = swap_lanes(reduce_columns(cols), 0)
-    width = cols.shape[0]
+    width = boundary.shape[2] // lax.axis_size(CUTS)
     col_start = lax.axis_index(CUTS) * width
     cpl_base = CYC_A + CYC_B
     tables = lax.dynamic_slice_in_dim(coupling[cpl_base:cpl_base + CYC_C], col_start, width, axis=2)
-    return final_layers(cols, gate_stack, jnp.swapaxes(tables, 1, 2), 3 * CYC_A + 3 * CYC_B, CYC_C)
+    tables, recv = lax.optimization_barrier((jnp.swapaxes(tables, 1, 2), recv))
+    cols = group_b(parity, keep, recv, gate_stack, coupling, CYC_B)
+    cols = swap_lanes(reduce_columns(cols), 0)
+    return final_layers(cols, gate_stack, tables, 3 * CYC_A + 3 * CYC_B, CYC_C)
 
 
 def solution(mesh):

time: 97.1 us -> 96.7 us (level)
  transfers between devices with their start and end apart: 3 -> 3, of which waited for: 2 -> 3; matrix products, arithmetic and copies ran while one was open for 1% -> 1% of each run, Pallas kernels for 0% -> 0%
where the time goes in v14:
time: 96.7 us; the launch traced here: 96.4 us
  starting transfers between devices  31.3 us (32%)
  Pallas kernels  27.7 us (29%)
  waiting for transfers between devices  19.8 us (20%)
  blocking collectives  14.4 us (15%)
  local copies, waits for them, and re-layouts  1.67 us (2%)
  other arithmetic  1.41 us (1%)
    all_to_all x1, starting transfers between devices, reduce_columns(): cols = lax.all_to_all(blocks, axis, 0, 0, tiled=False).sum(0)  16.4 us
    ppermute x2, starting transfers between devices, partner(): return lax.ppermute(value, axis, pairs)  14.9 us
    all_to_all x1, blocking collectives, reduce_columns(): cols = lax.all_to_all(blocks, axis, 0, 0, tiled=False).sum(0)  14.4 us
    ppermute x2, waiting for transfers between devices, partner(): return lax.ppermute(value, axis, pairs)  14.2 us
    pallas_call x1, Pallas kernels, group_b(): pl.pallas_call(functools.partial(_group_b_kernel, cycles=cycles), out_sha...  9.53 us
    pallas_call x1, Pallas kernels, group_a(): pl.pallas_call(functools.partial(_group_a_kernel, cycles=cycles), out_sha...  9.35 us
    pallas_call x1, Pallas kernels, final_layers(): pl.pallas_call(kernel, out_shape=jax.ShapeDtypeStruct((width, rows), d.dt...  8.82 us
    all_to_all x1, waiting for transfers between devices, reduce_columns(): cols = lax.all_to_all(blocks, axis, 0, 0, tiled=False).sum(0)  5.67 us
  transfers between devices with their start and end apart: 3, of which 3 were waited for; matrix products, arithmetic and copies ran while one was open for 1% of the time, Pallas kernels for 0%

profile of v14, /device:TPU:1, one launch (start us, length us, event | category | flops | bytes accessed | tf_op | source)
XLA Modules:
  0.0 96.4 jit_solution(7767529202504840659)
XLA Ops:
  0.0 0.0 slice-start
  0.0 9.3 %shard_map.37 = (f32[1024,128]{1,0:T(8,128)}, f32[1024,128]{1,0:T(8,128)}) custom-call(s32[1]{0:T(128)} %bitcast.p_ref, f32[2048,128]{1,0:T(8,128)} %bitcast.7, f32[34,128,128]{2,1,0:T(8,128)} %g_ref.5, f32[13,128,128]{2,1,0:T(8,128)} %c_ref.3), custom_call_target="tpu_custom_call" | custom-call | tf_op jit(solution)/shard_map/pallas_call | solution.py:103
  9.4 8.5 %collective-permute-start = (f32[1024,128]{1,0:T(8,128)}, f32[1024,128]{1,0:T(8,128)S(1)}, u32[]{:S(2)}, u32[]{:S(2)}) collective-permute-start(f32[1024,128]{1,0:T(8,128)} %get-tuple-element.10), channel_id=1, source_target_pairs={{0,256},{16,272},{32,288},{48,304},{64,320},{80,336},{96,352},{112... | collective-permute-start | bytes 1572872 | tf_op jit(solution)/shard_map/ppermute | solution.py:164
  17.8 0.0 slice-done
  17.8 0.1 constant_dynamic-slice_fusion
  18.0 0.7 copy.7
  18.7 13.6 %collective-permute-done.recv_ref = f32[1024,128]{1,0:T(8,128)S(1)} collective-permute-done((f32[1024,128]{1,0:T(8,128)}, f32[1024,128]{1,0:T(8,128)S(1)}, u32[]{:S(2)}, u32[]{:S(2)}) %collective-permute-start) | collective-permute-done | bytes 524320 | tf_op jit(solution)/shard_map/ppermute | solution.py:164
  32.3 0.0 copy-start
  32.3 0.8 copy-done
  33.1 9.5 %shard_map.38 = f32[128,2048]{1,0:T(8,128)} custom-call(s32[1]{0:T(128)} %bitcast.p_ref, f32[1024,128]{1,0:T(8,128)} %get-tuple-element.9.keep_ref, f32[1024,128]{1,0:T(8,128)} %copy-done, f32[34,128,128]{2,1,0:T(8,128)} %g_ref.5, f32[13,128,128]{2,1,0:T(8,128)} %c_ref.3), custom_call_target="tpu_custom_call" | custom-call | tf_op jit(solution)/shard_map/pallas_call | solution.py:115
  42.6 14.4 %all_to_all.10 = f32[4,32,2048]{2,1,0:T(8,128)S(1)} all-to-all(f32[4,32,2048]{2,1,0:T(8,128)} %bitcast.6), channel_id=1, replica_groups=mesh['yh'=2,'z'=8,'core'=2,'x'=4,'yl'=4] {'x'}, dimensions={0} | all-to-all | bytes 2097152 | tf_op jit(solution)/shard_map/all_to_all | solution.py:238
  57.0 0.8 reduce_sum.18
  57.7 16.4 %all-to-all-start.1 = ((f32[4,8,2048]{2,1,0:T(8,128)}), f32[4,8,2048]{2,1,0:T(8,128)S(1)}, u32[]{:S(2)}, u32[]{:S(2)}) async-start(f32[4,8,2048]{2,1,0:T(8,128)} %bitcast.4), calls=%async_computation.1 | async-start | bytes 524288 | tf_op jit(solution)/shard_map/all_to_all | solution.py:238
  74.1 5.7 %all-to-all-done.1 = f32[4,8,2048]{2,1,0:T(8,128)S(1)} async-done(((f32[4,8,2048]{2,1,0:T(8,128)}), f32[4,8,2048]{2,1,0:T(8,128)S(1)}, u32[]{:S(2)}, u32[]{:S(2)}) %all-to-all-start.1) | async-done | bytes 262176 | tf_op jit(solution)/shard_map/all_to_all | solution.py:238
  79.8 6.5 %collective-permute-start.1 = (f32[8,1024]{1,0:T(8,128)S(1)}, f32[8,1024]{1,0:T(8,128)S(1)}, u32[]{:S(2)}, u32[]{:S(2)}) collective-permute-start(f32[8,1024]{1,0:T(8,128)S(1)} %get-tuple-element.14), channel_id=1, source_target_pairs={{0,16},{16,0},{32,48},{48,32},{64,80},{80,64},{96,112},{112,96},{1... | collective-permute-start | bytes 98312 | tf_op jit(solution)/shard_map/ppermute | solution.py:164
  86.3 0.6 collective-permute-done.1
  86.9 0.6 maximum_select_fusion.d_ref
  87.5 8.8 %shard_map.39 = f32[8,2048]{1,0:T(8,128)} custom-call(f32[8,2048]{1,0:T(8,128)} %maximum_select_fusion.d_ref, f32[34,128,128]{2,1,0:T(8,128)} %g_ref.5, f32[5,8,128]{2,1,0:T(8,128)} %bitcast.8), custom_call_target="tpu_custom_call" | custom-call | tf_op jit(solution)/shard_map/pallas_call | solution.py:150
  (2 shorter events, 0.0 us)
Async XLA Ops:
  0.0 17.8 %slice-start = ((f32[13,128,128]{2,1,0:T(8,128)}), f32[5,128,128]{2,1,0:T(8,128)S(1)}, s32[]{:S(2)}) async-start(f32[13,128,128]{2,1,0:T(8,128)} %c_ref.3), calls=%async_computation.2 | async-start | bytes 655360 | tf_op jit(solution)/shard_map/slice | solution.py:262
  9.4 22.9 %collective-permute-start = (f32[1024,128]{1,0:T(8,128)}, f32[1024,128]{1,0:T(8,128)S(1)}, u32[]{:S(2)}, u32[]{:S(2)}) collective-permute-start(f32[1024,128]{1,0:T(8,128)} %get-tuple-element.10), channel_id=1, source_target_pairs={{0,256},{16,272},{32,288},{48,304},{64,320},{80,336},{96,352},{112... | collective-permute-start | bytes 1572872 | tf_op jit(solution)/shard_map/ppermute | solution.py:164
  32.3 0.8 copy-start
  57.7 22.0 %all-to-all-start.1 = ((f32[4,8,2048]{2,1,0:T(8,128)}), f32[4,8,2048]{2,1,0:T(8,128)S(1)}, u32[]{:S(2)}, u32[]{:S(2)}) async-start(f32[4,8,2048]{2,1,0:T(8,128)} %bitcast.4), calls=%async_computation.1 | async-start | bytes 524288 | tf_op jit(solution)/shard_map/all_to_all | solution.py:238
  79.8 7.1 %collective-permute-start.1 = (f32[8,1024]{1,0:T(8,128)S(1)}, f32[8,1024]{1,0:T(8,128)S(1)}, u32[]{:S(2)}, u32[]{:S(2)}) collective-permute-start(f32[8,1024]{1,0:T(8,128)S(1)} %get-tuple-element.14), channel_id=1, source_target_pairs={{0,16},{16,0},{32,48},{48,32},{64,80},{80,64},{96,112},{112,96},{1... | collective-permute-start | bytes 98312 | tf_op jit(solution)/shard_map/ppermute | solution.py:164
